TPU v7x, 512 devices: a whole 4x4x16 slice. The times are simulated.
512 devices in a mesh: blk: 64 (over y_lo, z, core), exp: 8 (over y_hi, x).
Axes of the slice: x: 4, y: 4 (y_hi: 2, y_lo: 2; y = y_hi * 2 + y_lo), z: 16, core: 2. Of those that a mesh axis runs over, the one named last changes fastest.
Arguments:
- hidden_in: bfloat16 [32, 4, 2048], P('exp'), may hold values from -3 to 3
- q_lat: bfloat16 [32, 4, 16, 512], P('exp'), may hold values from -28 to 28
- q_rope: bfloat16 [32, 4, 16, 64], P('exp'), may hold values from -4 to 4
- new_lat: bfloat16 [32, 4, 512], P('exp'), may hold values from -4 to 4
- new_rope: bfloat16 [32, 4, 64], P('exp'), may hold values from -4 to 4
- cache_lat: bfloat16 [32, 16384, 512], P('exp', 'blk'), may hold values from -4 to 4
- cache_rope: bfloat16 [32, 16384, 64], P('exp', 'blk'), may hold values from -4 to 4
- lengths: int32 [32], P('exp'), may hold values from 2 to 16384, as said below
- w_uv: bfloat16 [512, 2048], P(None, 'blk'), may hold values from -3 to 3
- w_out: bfloat16 [2048, 2048], P('blk'), may hold values from -0.125 to 0.125
- norm_gain: float32 [2048], replicated, may hold values from 0.1 to 1.9
- w_router: bfloat16 [2048, 64], replicated, may hold values from -0.125 to 0.125
- routes: int32 [32, 4, 6], P('exp'), may hold values from 0 to 63, all different within a row; in each aligned block of 16 rows (0 to 15, 16 to 31, ..., all dimensions but the last counted through in order) at most 3 rows name the same one
- w_gate: bfloat16 [64, 2048, 1408], P('blk', None, 'exp'), may hold values from -0.125 to 0.125
- w_up: bfloat16 [64, 2048, 1408], P('blk', None, 'exp'), may hold values from -0.125 to 0.125
- w_down: bfloat16 [64, 1408, 2048], P('blk', 'exp'), may hold values from -0.15625 to 0.15625
Outputs:
- hidden_out: bfloat16 [32, 4, 2048], P('exp')
Inputs may be any that keep to these rules, and one draw needn't show every extreme that they name: `lengths`: in each aligned group of 4 requests exactly 1 have length 16384; the others have 2 to 512. `routes`: each row names 6 different experts; in the 16 rows of one index of exp no expert is named more than 3 times.
All inputs are finite; a program needn't handle non-finite values.
Results may differ from a plain program's by a relative error of at most 0.0062.
Values may be sent and summed in bfloat16 or wider, within the bound.
No kernel may reach another device: no remote copies, remote signals or barrier semaphores. Data moves between devices by JAX's collectives and lax.ppermute only.
A program may use at most 128 MiB of HBM per device.

v0:
```python
import jax
import jax.numpy as jnp
from jax import lax
from jax.sharding import PartitionSpec as P

V = 128
QK = 192
CAP = 3


NEG_FILL = -1e30
ROUTE_SCALE = 2.446
NORM_EPS = 1e-06


def merged_2(x, axis, combine):
    everything = jax.tree.map(lambda part: lax.all_gather(part, axis), x)
    leading = jax.tree.map(lambda part: part[0], everything)

    def step(k, so_far):
        return combine(so_far, jax.tree.map(lambda part: part[k], everything))

    return lax.fori_loop(1, lax.axis_size(axis), step, leading)


def block_partial(query, query_rope, keys_lat, keys_rope, valid):
    scale = QK ** (-0.5)
    scores = (
        jnp.einsum("rmc,rkc->rmk", query, keys_lat, preferred_element_type=jnp.float32)
        + jnp.einsum("rmc,rkc->rmk", query_rope, keys_rope, preferred_element_type=jnp.float32)
    ) * scale
    masked = jnp.where(valid, scores, NEG_FILL)
    peak_val = jnp.max(masked, axis=2)
    weights = jnp.where(valid, jnp.exp(masked - peak_val[:, :, None]), 0.0)
    weight_sum = jnp.sum(weights, axis=2)
    summed = jnp.einsum(
        "rmk,rkc->rmc", weights.astype(jnp.bfloat16), keys_lat, preferred_element_type=jnp.float32
    )
    return (peak_val, weight_sum, summed)


def merge_pair(left_part, right_part):
    peak_left, total_left, sum_left = left_part
    peak_right, total_right, sum_right = right_part
    peak_val = jnp.maximum(peak_left, peak_right)
    factor_left = jnp.exp(peak_left - peak_val)
    factor_right = jnp.exp(peak_right - peak_val)
    weight_sum = factor_left * total_left + factor_right * total_right
    summed = factor_left[..., None] * sum_left + factor_right[..., None] * sum_right
    return (peak_val, weight_sum, summed)


def local(
    hidden_in,
    q_lat,
    q_rope,
    new_lat,
    new_rope,
    cache_lat,
    cache_rope,
    lengths,
    w_uv,
    w_out,
    norm_gain,
    w_router,
    routes,
    w_gate,
    w_up,
    w_down,
):
    requests, new_steps, head_count, latent_dim = q_lat.shape
    query_rows = new_steps * head_count
    query = q_lat.reshape(requests, query_rows, latent_dim)
    query_rope = q_rope.reshape(requests, query_rows, q_rope.shape[3])
    cache_span = cache_lat.shape[1]
    position = lax.axis_index("blk") * cache_span + lax.iota(jnp.int32, cache_span)
    cache_valid = jnp.broadcast_to(
        position[None, None, :] < lengths[:, None, None], (requests, query_rows, cache_span)
    )
    cache_part = block_partial(query, query_rope, cache_lat, cache_rope, cache_valid)
    token_of_row = lax.iota(jnp.int32, query_rows) // head_count
    fresh_valid = lax.iota(jnp.int32, new_steps)[None, :] <= token_of_row[:, None]
    fresh_valid = jnp.broadcast_to(fresh_valid[None, :, :], (requests, query_rows, new_steps))
    fresh_part = block_partial(query, query_rope, new_lat, new_rope, fresh_valid)
    merged = merged_2(cache_part, "blk", merge_pair)
    peak_val, weight_sum, summed = merge_pair(merged, fresh_part)
    lat_out = (summed / weight_sum[:, :, None]).astype(jnp.bfloat16)
    token_rows = requests * new_steps
    head_cols = w_uv.shape[1]
    head_pick = lax.axis_index("blk") * head_cols // V
    lat_heads = lat_out.reshape(requests, new_steps, head_count, latent_dim)
    lat_head = lax.dynamic_index_in_dim(lat_heads, head_pick, axis=2, keepdims=False).reshape(
        token_rows, latent_dim
    )
    heads_out = jnp.dot(lat_head, w_uv, preferred_element_type=jnp.float32).astype(jnp.bfloat16)
    proj_part = jnp.dot(heads_out, w_out, preferred_element_type=jnp.float32)
    projected = lax.psum(proj_part, "blk")
    width = hidden_in.shape[2]
    mixed = hidden_in.reshape(token_rows, width).astype(jnp.float32) + projected
    meansq = jnp.mean(mixed * mixed, axis=1, keepdims=True)
    normed = (mixed * lax.rsqrt(meansq + NORM_EPS) * norm_gain[None, :]).astype(jnp.bfloat16)
    affinity = jax.nn.sigmoid(jnp.dot(normed, w_router, preferred_element_type=jnp.float32))
    expert_total = w_router.shape[1]
    top_count = routes.shape[2]
    flat_routes = routes.reshape(token_rows, top_count)
    route_hits = flat_routes[:, :, None] == lax.iota(jnp.int32, expert_total)[None, None, :]
    chosen = jnp.sum(jnp.where(route_hits, affinity[:, None, :], 0.0), axis=2)
    route_weight = ROUTE_SCALE * chosen / jnp.sum(chosen, axis=1, keepdims=True)
    local_count = w_gate.shape[0]
    local_ids = lax.axis_index("blk") * local_count + lax.iota(jnp.int32, local_count)
    pair_routes = flat_routes.reshape(token_rows * top_count)
    local_hits = (pair_routes[:, None] == local_ids[None, :]).astype(jnp.int32)
    ranks = jnp.cumsum(local_hits, axis=0) - 1
    slot_ids = lax.iota(jnp.int32, CAP)
    slot_match = local_hits.T[:, None, :] * (ranks.T[:, None, :] == slot_ids[None, :, None]).astype(
        jnp.int32
    )
    select = slot_match.reshape(local_count, CAP, token_rows, top_count).astype(jnp.float32)
    dispatch_map = jnp.sum(select, axis=3)
    combine_map = jnp.sum(select * route_weight[None, None, :, :], axis=3)
    dispatched = jnp.einsum(
        "esr,rd->esd", dispatch_map.astype(jnp.bfloat16), normed, preferred_element_type=jnp.float32
    ).astype(jnp.bfloat16)
    piece = lax.all_gather(dispatched, "exp", axis=1, tiled=True)
    gate = jnp.einsum("erd,edf->erf", piece, w_gate, preferred_element_type=jnp.float32)
    upper = jnp.einsum("erd,edf->erf", piece, w_up, preferred_element_type=jnp.float32)
    hidden_all = (jax.nn.silu(gate) * upper).astype(jnp.bfloat16)
    partial_out = jnp.einsum("erf,efd->erd", hidden_all, w_down, preferred_element_type=jnp.float32)
    expert_out = lax.psum_scatter(partial_out, "exp", scatter_dimension=1, tiled=True)
    moe_part = jnp.einsum("esr,esd->rd", combine_map, expert_out, precision=lax.Precision.HIGHEST)
    moe_all = lax.psum(moe_part, "blk")
    result = (mixed + moe_all).astype(jnp.bfloat16)
    return result.reshape(requests, new_steps, width)


def solution(mesh):
    in_specs = (
        P("exp", None, None),
        P("exp", None, None, None),
        P("exp", None, None, None),
        P("exp", None, None),
        P("exp", None, None),
        P("exp", "blk", None),
        P("exp", "blk", None),
        P("exp"),
        P(None, "blk"),
        P("blk", None),
        P(),
        P(),
        P("exp", None, None),
        P("blk", None, "exp"),
        P("blk", None, "exp"),
        P("blk", "exp", None),
    )
    out_specs = P("exp", None, None)
    return jax.shard_map(local, mesh=mesh, in_specs=in_specs, out_specs=out_specs, check_vma=False)
```

profile of v0, /device:TPU:1, one launch (start us, length us, event | category | flops | bytes accessed | tf_op | source)
XLA Modules:
  0.0 1199.2 jit_solution(7835807839142678732)
XLA Ops:
  7.8 1.4 fusion.56
  11.8 72.7 %all-gather.5 = f32[64,4,64]{2,1,0:T(4,128)S(1)} all-gather(f32[1,4,64]{2,1,0:T(4,128)S(1)} %bitcast.74), channel_id=3, replica_groups=mesh['blk'=64,'exp'=8] {'blk'}, dimensions={0}, use_global_device_ids=true | all-gather | bytes 66560 | tf_op jit(solution)/shard_map/all_gather | solution.py:17
  84.5 61.4 %all-gather.4 = f32[64,4,64]{2,1,0:T(4,128)S(1)} all-gather(f32[1,4,64]{2,1,0:T(4,128)S(1)} %bitcast.73), channel_id=2, replica_groups=mesh['blk'=64,'exp'=8] {'blk'}, dimensions={0}, use_global_device_ids=true | all-gather | bytes 66560 | tf_op jit(solution)/shard_map/all_gather | solution.py:17
  148.8 64.6 %all-gather.9.cloned.1.call-done = f32[256,64,512]{2,1,0:T(8,128)} async-done(((f32[4,64,512]{2,1,0:T(8,128)}), f32[256,64,512]{2,1,0:T(8,128)}) %all-gather.9.cloned.1.call-update) | async-done | bytes 33554448 | tf_op jit(solution)/shard_map/all_gather | solution.py:17
  214.5 79.7 %while.19 = (s32[]{:T(128)}, f32[4,64]{1,0:T(4,128)S(1)}, f32[4,64]{1,0:T(4,128)S(1)}, f32[4,64,512]{2,1,0:T(8,128)S(1)}, f32[64,4,64]{2,1,0:T(4,128)S(1)}, /*in...) while((s32[]{:T(128)}, f32[4,64]{1,0:T(4,128)S(1)}, ...), condition=%wide.region_3.4_spmd, body=%wide.region_2.3_spmd.sunk | while | flops 394757 | bytes 1583255 | solution.py:23
  214.5 1.2 fusion.79
  215.8 1.2 fusion.79
  217.1 1.2 fusion.79
  218.3 1.2 fusion.79
  219.6 1.2 fusion.79
  220.9 1.2 fusion.79
  222.1 1.2 fusion.79
  223.4 1.2 fusion.79
  224.6 1.2 fusion.79
  225.9 1.2 fusion.79
  227.2 1.2 fusion.79
  228.4 1.2 fusion.79
  229.7 1.2 fusion.79
  231.0 1.2 fusion.79
  232.2 1.2 fusion.79
  233.5 1.2 fusion.79
  234.8 1.2 fusion.79
  236.0 1.2 fusion.79
  237.3 1.2 fusion.79
  238.6 1.2 fusion.79
  239.8 1.2 fusion.79
  241.1 1.2 fusion.79
  242.4 1.2 fusion.79
  243.6 1.2 fusion.79
  244.9 1.2 fusion.79
  246.2 1.2 fusion.79
  247.4 1.2 fusion.79
  248.7 1.2 fusion.79
  250.0 1.2 fusion.79
  251.2 1.2 fusion.79
  252.5 1.2 fusion.79
  255.0 1.2 fusion.79
  256.3 1.2 fusion.79
  257.5 1.2 fusion.79
  258.8 1.2 fusion.79
  263.9 1.2 fusion.79
  265.1 1.2 fusion.79
  266.4 1.2 fusion.79
  267.7 1.2 fusion.79
  271.5 1.2 fusion.79
  272.7 1.2 fusion.79
  274.0 1.2 fusion.79
  275.3 1.2 fusion.79
  279.1 1.2 fusion.79
  280.3 1.2 fusion.79
  281.6 1.2 fusion.79
  282.9 1.2 fusion.79
  287.9 1.2 fusion.79
  289.2 1.2 fusion.79
  290.4 1.2 fusion.79
  291.7 1.2 fusion.79
  295.4 1.9 fusion.15
  300.3 373.4 %all-reduce.5.cloned.1.call-done = f32[16,2048]{1,0:T(8,128)} async-done(((f32[16,2048]{1,0:T(8,128)}), f32[16,2048]{1,0:T(8,128)}) %all-reduce.5.cloned.1.call-update) | async-done | bytes 131088 | tf_op jit(solution)/shard_map/psum | solution.py:97
  677.1 27.9 %all-gather.6 = bf16[8,3,2048]{2,1,0:T(4,128)(2,1)S(1)} all-gather(bf16[1,3,2048]{2,1,0:T(4,128)(2,1)S(1)} %fusion.3), channel_id=5, replica_groups=mesh['blk'=64,'exp'=8] {'exp'}, dimensions={0}, use_global_device_ids=true | all-gather | bytes 110592 | tf_op jit(solution)/shard_map/all_gather | solution.py:124
  705.1 1.4 fusion.19
  706.5 2.0 convolution_bitcast_fusion
  709.5 1.3 dynamic-slice
  711.4 97.7 %all-reduce.9.cloned.1.call-done = f32[1,24,2048]{2,0,1:T(1,128)} async-done(((f32[1,24,2048]{2,0,1:T(1,128)}), f32[1,24,2048]{2,0,1:T(1,128)}) %all-reduce.9.cloned.1.call-update) | async-done | bytes 196624
  810.9 380.2 %all-reduce.7.cloned.1.call-done = f32[16,2048]{1,0:T(8,128)} async-done(((f32[16,2048]{1,0:T(8,128)}), f32[16,2048]{1,0:T(8,128)}) %all-reduce.7.cloned.1.call-update) | async-done | bytes 131088 | tf_op jit(solution)/shard_map/psum | solution.py:131
  (125 shorter events, 35.9 us)
Async XLA Ops:
  6.5 1.2 copy-start
  6.5 206.9 %all-gather.9.cloned.1.call-start = ((), (), s32[]{:S(2)}) async-start(), calls=%async_computation.2 | async-start | bytes 34078720 | tf_op jit(solution)/shard_map/all_gather | solution.py:17
  11.5 662.2 %all-reduce.5.cloned.1.call-start = ((), (), s32[]{:S(2)}) async-start(), calls=%async_computation | async-start | bytes 262144 | tf_op jit(solution)/shard_map/psum | solution.py:97
  297.3 511.9 %all-reduce.9.cloned.1.call-start = ((), (), s32[]{:S(2)}) async-start(), calls=%async_computation.3 | async-start | bytes 393216
  709.5 481.7 %all-reduce.7.cloned.1.call-start = ((), (), s32[]{:S(2)}) async-start(), calls=%async_computation.1 | async-start | bytes 262144 | tf_op jit(solution)/shard_map/psum | solution.py:131
Sparse Core Ops, SparseCore 0:
  11.6 201.7 all-gather.8
  297.4 376.2 all-reduce.4
  709.6 99.5 all-reduce.8
  811.9 379.1 all-reduce.6
where the time goes:
time: 1200 us
  waiting for transfers between devices  916 us (76%)
  blocking collectives  162 us (14%)
  other arithmetic  82.9 us (7%)
  matrix products  15.3 us (1%)
  between operations  13.9 us (1%)
    psum x1, waiting for transfers between devices, local(): moe_all = lax.psum(moe_part, 'blk')  380 us
    psum x1, waiting for transfers between devices, local(): projected = lax.psum(proj_part, 'blk')  373 us
    all_gather x2, blocking collectives, merged_2(): everything = jax.tree.map(lambda part: lax.all_gather(part, axis), x)  134 us
    unnamed x5, waiting for transfers between devices  97.8 us
    add x63, other arithmetic, merge_pair(): factor_left[..., None] * sum_left + factor_right[..., None] * sum_right  76.3 us
    all_gather x1, waiting for transfers between devices, merged_2(): everything = jax.tree.map(lambda part: lax.all_gather(part, axis), x)  64.6 us
    all_gather x1, blocking collectives, local(): piece = lax.all_gather(dispatched, 'exp', axis=1, tiled=True)  27.9 us
  transfers between devices with their start and end apart: 4, of which 4 were waited for; matrix products, arithmetic and copies ran while one was open for 1% of the time, Pallas kernels for 0%

commit v1 on v0

--- a/solution.py
+++ b/solution.py
@@ -13,14 +13,49 @@
 NORM_EPS = 1e-06
 
 
-def merged_2(x, axis, combine):
-    everything = jax.tree.map(lambda part: lax.all_gather(part, axis), x)
-    leading = jax.tree.map(lambda part: part[0], everything)
-
-    def step(k, so_far):
-        return combine(so_far, jax.tree.map(lambda part: part[k], everything))
-
-    return lax.fori_loop(1, lax.axis_size(axis), step, leading)
+def xor_pairs(count, mask):
+    return [(i, i ^ mask) for i in range(count)]
+
+
+def exchange(x, axis, mask):
+    count = lax.axis_size(axis)
+    return jax.tree.map(lambda part: lax.ppermute(part, axis, xor_pairs(count, mask)), x)
+
+
+def exchange_state(state, axis, mask):
+    peak_val, weight_sum, summed = state
+    packed = jnp.concatenate([summed, peak_val[..., None], weight_sum[..., None]], axis=-1)
+    got = exchange(packed, axis, mask)
+    width = summed.shape[-1]
+    return (got[..., width], got[..., width + 1], got[..., :width])
+
+
+def butterfly_sum(x, axis, bits):
+    for bit in bits:
+        x = x + exchange(x, axis, 1 << bit)
+    return x
+
+
+def butterfly_gather(x, axis, bits):
+    me = lax.axis_index(axis)
+    x = x[None]
+    for bit in bits:
+        other = exchange(x, axis, 1 << bit)
+        high = ((me >> bit) & 1) == 1
+        low_part = jnp.where(high, other, x)
+        high_part = jnp.where(high, x, other)
+        x = jnp.concatenate([low_part, high_part], axis=0)
+    return x
+
+
+def butterfly_scatter_sum(x, axis, bits):
+    me = lax.axis_index(axis)
+    for bit in bits:
+        side = (me >> bit) & 1
+        keep = lax.dynamic_index_in_dim(x, side, 0, keepdims=False)
+        send = lax.dynamic_index_in_dim(x, 1 - side, 0, keepdims=False)
+        x = keep + exchange(send, axis, 1 << bit)
+    return x
 
 
 def block_partial(query, query_rope, keys_lat, keys_rope, valid):
@@ -69,32 +104,53 @@
     w_down,
 ):
     requests, new_steps, head_count, latent_dim = q_lat.shape
+    me = lax.axis_index("blk")
+    blk_bits = lax.axis_size("blk").bit_length() - 1
+    exp_bits = lax.axis_size("exp").bit_length() - 1
     query_rows = new_steps * head_count
     query = q_lat.reshape(requests, query_rows, latent_dim)
     query_rope = q_rope.reshape(requests, query_rows, q_rope.shape[3])
     cache_span = cache_lat.shape[1]
-    position = lax.axis_index("blk") * cache_span + lax.iota(jnp.int32, cache_span)
+    position = me * cache_span + lax.iota(jnp.int32, cache_span)
     cache_valid = jnp.broadcast_to(
         position[None, None, :] < lengths[:, None, None], (requests, query_rows, cache_span)
     )
-    cache_part = block_partial(query, query_rope, cache_lat, cache_rope, cache_valid)
-    token_of_row = lax.iota(jnp.int32, query_rows) // head_count
-    fresh_valid = lax.iota(jnp.int32, new_steps)[None, :] <= token_of_row[:, None]
-    fresh_valid = jnp.broadcast_to(fresh_valid[None, :, :], (requests, query_rows, new_steps))
-    fresh_part = block_partial(query, query_rope, new_lat, new_rope, fresh_valid)
-    merged = merged_2(cache_part, "blk", merge_pair)
-    peak_val, weight_sum, summed = merge_pair(merged, fresh_part)
+    peak_val, weight_sum, summed = block_partial(query, query_rope, cache_lat, cache_rope, cache_valid)
+    head_bits = head_count.bit_length() - 1
+    split = (2,) * head_bits
+    state = (
+        peak_val.reshape(requests, new_steps, head_count).transpose(2, 0, 1).reshape(split + (requests, new_steps)),
+        weight_sum.reshape(requests, new_steps, head_count).transpose(2, 0, 1).reshape(split + (requests, new_steps)),
+        summed.reshape(requests, new_steps, head_count, latent_dim)
+        .transpose(2, 0, 1, 3)
+        .reshape(split + (requests, new_steps, latent_dim)),
+    )
+    low_bits = blk_bits - head_bits
+    order = [head_bits - 1] + list(range(head_bits - 1))
+    remaining = list(range(head_bits - 1, -1, -1))
+    for head_bit in order:
+        axis_pos = remaining.index(head_bit)
+        remaining.pop(axis_pos)
+        bit = head_bit + low_bits
+        side = (me >> bit) & 1
+        keep = jax.tree.map(lambda part: lax.dynamic_index_in_dim(part, side, axis_pos, keepdims=False), state)
+        send = jax.tree.map(lambda part: lax.dynamic_index_in_dim(part, 1 - side, axis_pos, keepdims=False), state)
+        state = merge_pair(keep, exchange_state(send, "blk", 1 << bit))
+    for bit in range(low_bits - 1, -1, -1):
+        state = merge_pair(state, exchange_state(state, "blk", 1 << bit))
+    head_pick = me >> low_bits
+    own_query = lax.dynamic_index_in_dim(q_lat, head_pick, axis=2, keepdims=False)
+    own_rope = lax.dynamic_index_in_dim(q_rope, head_pick, axis=2, keepdims=False)
+    fresh_valid = lax.iota(jnp.int32, new_steps)[None, :] <= lax.iota(jnp.int32, new_steps)[:, None]
+    fresh_valid = jnp.broadcast_to(fresh_valid[None, :, :], (requests, new_steps, new_steps))
+    fresh_part = block_partial(own_query, own_rope, new_lat, new_rope, fresh_valid)
+    peak_val, weight_sum, summed = merge_pair(state, fresh_part)
     lat_out = (summed / weight_sum[:, :, None]).astype(jnp.bfloat16)
     token_rows = requests * new_steps
-    head_cols = w_uv.shape[1]
-    head_pick = lax.axis_index("blk") * head_cols // V
-    lat_heads = lat_out.reshape(requests, new_steps, head_count, latent_dim)
-    lat_head = lax.dynamic_index_in_dim(lat_heads, head_pick, axis=2, keepdims=False).reshape(
-        token_rows, latent_dim
-    )
+    lat_head = lat_out.reshape(token_rows, latent_dim)
     heads_out = jnp.dot(lat_head, w_uv, preferred_element_type=jnp.float32).astype(jnp.bfloat16)
     proj_part = jnp.dot(heads_out, w_out, preferred_element_type=jnp.float32)
-    projected = lax.psum(proj_part, "blk")
+    projected = butterfly_sum(proj_part, "blk", range(blk_bits))
     width = hidden_in.shape[2]
     mixed = hidden_in.reshape(token_rows, width).astype(jnp.float32) + projected
     meansq = jnp.mean(mixed * mixed, axis=1, keepdims=True)
@@ -107,7 +163,7 @@
     chosen = jnp.sum(jnp.where(route_hits, affinity[:, None, :], 0.0), axis=2)
     route_weight = ROUTE_SCALE * chosen / jnp.sum(chosen, axis=1, keepdims=True)
     local_count = w_gate.shape[0]
-    local_ids = lax.axis_index("blk") * local_count + lax.iota(jnp.int32, local_count)
+    local_ids = me * local_count + lax.iota(jnp.int32, local_count)
     pair_routes = flat_routes.reshape(token_rows * top_count)
     local_hits = (pair_routes[:, None] == local_ids[None, :]).astype(jnp.int32)
     ranks = jnp.cumsum(local_hits, axis=0) - 1
@@ -121,14 +177,18 @@
     dispatched = jnp.einsum(
         "esr,rd->esd", dispatch_map.astype(jnp.bfloat16), normed, preferred_element_type=jnp.float32
     ).astype(jnp.bfloat16)
-    piece = lax.all_gather(dispatched, "exp", axis=1, tiled=True)
+    gathered = butterfly_gather(dispatched, "exp", range(exp_bits))
+    groups = gathered.shape[0]
+    piece = gathered.transpose(1, 0, 2, 3).reshape(local_count, groups * CAP, width)
     gate = jnp.einsum("erd,edf->erf", piece, w_gate, preferred_element_type=jnp.float32)
     upper = jnp.einsum("erd,edf->erf", piece, w_up, preferred_element_type=jnp.float32)
     hidden_all = (jax.nn.silu(gate) * upper).astype(jnp.bfloat16)
     partial_out = jnp.einsum("erf,efd->erd", hidden_all, w_down, preferred_element_type=jnp.float32)
-    expert_out = lax.psum_scatter(partial_out, "exp", scatter_dimension=1, tiled=True)
+    split_out = partial_out.reshape((local_count,) + (2,) * exp_bits + (CAP, width))
+    split_out = jnp.moveaxis(split_out, 0, exp_bits)
+    expert_out = butterfly_scatter_sum(split_out, "exp", range(exp_bits - 1, -1, -1))
     moe_part = jnp.einsum("esr,esd->rd", combine_map, expert_out, precision=lax.Precision.HIGHEST)
-    moe_all = lax.psum(moe_part, "blk")
+    moe_all = butterfly_sum(moe_part, "blk", range(blk_bits))
     result = (mixed + moe_all).astype(jnp.bfloat16)
     return result.reshape(requests, new_steps, width)
 

time: 1200 us -> 257 us (0.21)
  waiting for transfers between devices: 916 us -> 108 us
  blocking collectives: 162 us -> 0 us
  starting transfers between devices: 0.13 us -> 131 us
  other arithmetic: 82.9 us -> 3.25 us
  between operations: 13.9 us -> 0.72 us
    psum x2 -> x0, waiting for transfers between devices: 754 us -> none  [the longest x1 380 us: local(): moe_all = lax.psum(moe_part, 'blk')]
    all_gather x3 -> x0, blocking collectives: 162 us -> none  [the longest x2 134 us: merged_2(): everything = jax.tree.map(lambda part: lax.all_gather(part, axis), x)]
    ppermute x0 -> x24, starting transfers between devices: none -> 131 us  [exchange(): lax.ppermute(part, axis, xor_pairs(count, mask))]
    ppermute x0 -> x24, waiting for transfers between devices: none -> 108 us  [exchange(): lax.ppermute(part, axis, xor_pairs(count, mask))]
    unnamed x5 -> x0, waiting for transfers between devices: 97.8 us -> none
    add x63 -> x5, other arithmetic: 76.3 us -> 0.49 us  [merge_pair(): factor_left[..., None] * sum_left + factor_right[..., None] * sum_right]
    all_gather x1 -> x0, waiting for transfers between devices: 64.6 us -> none  [merged_2(): everything = jax.tree.map(lambda part: lax.all_gather(part, axis), x)]
  transfers between devices with their start and end apart: 4 -> 24, of which waited for: 4 -> 24; matrix products, arithmetic and copies ran while one was open for 1% -> 1% of each run, Pallas kernels for 0% -> 0%
where the time goes in v1:
time: 257 us; the launch traced here: 256 us
  starting transfers between devices  131 us (51%)
  waiting for transfers between devices  108 us (42%)
  local copies, waits for them, and re-layouts  9.34 us (4%)
  matrix products  4.35 us (2%)
  other arithmetic  3.25 us (1%)
    ppermute x24, starting transfers between devices, exchange(): lax.ppermute(part, axis, xor_pairs(count, mask))  131 us
    ppermute x24, waiting for transfers between devices, exchange(): lax.ppermute(part, axis, xor_pairs(count, mask))  108 us
  transfers between devices with their start and end apart: 24, of which 24 were waited for; matrix products, arithmetic and copies ran while one was open for 1% of the time, Pallas kernels for 0%

profile of v1, /device:TPU:1, one launch (start us, length us, event | category | flops | bytes accessed | tf_op | source)
XLA Modules:
  0.0 256.0 jit_solution(5418944868669916474)
XLA Ops:
  0.0 0.7 copy-done.12
  0.8 0.4 copy-done
  1.2 1.4 fusion.107
  3.1 0.3 fusion.18
  3.8 0.3 copy.117
  4.1 0.3 copy.143
  4.6 0.3 copy.116
  5.0 4.0 %collective-permute-start = (f32[2,2,2,4,4,514]{5,4,3,2,1,0:T(4,128)S(1)}, f32[2,2,2,4,4,514]{5,4,3,2,1,0:T(4,128)S(1)}, u32[]{:S(2)}, u32[]{:S(2)}) collective-permute-start(f32[2,2,2,4,4,514]{5,4,3,2,1,0:T(4,128)S(1)} %pad_maximum_fusion), channel_id=1, source_target_pairs={{0,256},{8,264},{16,272},{24,280},{32,288},{40,296},{48,304},{56,3... | collective-permute-start | bytes 789512 | tf_op jit(solution)/shard_map/ppermute | solution.py:22
  9.1 0.9 constant_dynamic-slice_fusion.1
  10.0 3.5 %collective-permute-done = f32[2,2,2,4,4,514]{5,4,3,2,1,0:T(4,128)S(1)} collective-permute-done((f32[2,2,2,4,4,514]{5,4,3,2,1,0:T(4,128)S(1)}, f32[2,2,2,4,4,514]{5,4,3,2,1,0:T(4,128)S(1)}, u32[]{:S(2)}, u32[]{:S(2)}) %collective-permute-start) | collective-permute-done | bytes 263200 | tf_op jit(solution)/shard_map/ppermute | solution.py:22
  13.7 0.3 copy.146
  14.8 7.7 %collective-permute-start.1 = (f32[2,2,4,4,514]{4,3,2,1,0:T(4,128)S(1)}, f32[2,2,4,4,514]{4,3,2,1,0:T(4,128)S(1)}, u32[]{:S(2)}, u32[]{:S(2)}) collective-permute-start(f32[2,2,4,4,514]{4,3,2,1,0:T(4,128)S(1)} %pad_maximum_fusion.1), channel_id=1, source_target_pairs={{0,32},{8,40},{16,48},{24,56},{32,0},{40,8},{48,16},{56,24},{64,96... | collective-permute-start | bytes 394760 | tf_op jit(solution)/shard_map/ppermute | solution.py:22
  22.7 6.7 %collective-permute-done.1 = f32[2,2,4,4,514]{4,3,2,1,0:T(4,128)S(1)} collective-permute-done((f32[2,2,4,4,514]{4,3,2,1,0:T(4,128)S(1)}, f32[2,2,4,4,514]{4,3,2,1,0:T(4,128)S(1)}, u32[]{:S(2)}, u32[]{:S(2)}) %collective-permute-start.1) | collective-permute-done | bytes 131616 | tf_op jit(solution)/shard_map/ppermute | solution.py:22
  30.3 8.8 %collective-permute-start.2 = (f32[2,4,4,514]{3,2,1,0:T(4,128)S(1)}, f32[2,4,4,514]{3,2,1,0:T(4,128)S(1)}, u32[]{:S(2)}, u32[]{:S(2)}) collective-permute-start(f32[2,4,4,514]{3,2,1,0:T(4,128)S(1)} %pad_maximum_fusion.3), channel_id=1, source_target_pairs={{0,64},{8,72},{16,80},{24,88},{32,96},{40,104},{48,112},{56,120},{... | collective-permute-start | bytes 197384 | tf_op jit(solution)/shard_map/ppermute | solution.py:22
  39.1 1.8 collective-permute-done.2
  41.7 19.1 %collective-permute-start.3 = (f32[4,4,514]{2,1,0:T(4,128)S(1)}, f32[4,4,514]{2,1,0:T(4,128)S(1)}, u32[]{:S(2)}, u32[]{:S(2)}) collective-permute-start(f32[4,4,514]{2,1,0:T(4,128)S(1)} %pad_maximum_fusion.5), channel_id=1, source_target_pairs={{0,128},{8,136},{16,144},{24,152},{32,160},{40,168},{48,176},{56,1... | collective-permute-start | bytes 98696 | tf_op jit(solution)/shard_map/ppermute | solution.py:22
  61.0 1.1 collective-permute-done.3
  62.5 1.9 collective-permute-start.4
  64.5 2.7 %collective-permute-done.4 = f32[4,4,514]{2,1,0:T(4,128)S(1)} collective-permute-done((f32[4,4,514]{2,1,0:T(4,128)S(1)}, f32[4,4,514]{2,1,0:T(4,128)S(1)}, u32[]{:S(2)}, u32[]{:S(2)}) %collective-permute-start.4) | collective-permute-done | bytes 32928 | tf_op jit(solution)/shard_map/ppermute | solution.py:22
  67.5 4.4 %collective-permute-start.5 = (f32[4,4,514]{2,1,0:T(4,128)S(1)}, f32[4,4,514]{2,1,0:T(4,128)S(1)}, u32[]{:S(2)}, u32[]{:S(2)}) collective-permute-start(f32[4,4,514]{2,1,0:T(4,128)S(1)} %pad_maximum_fusion.7), channel_id=1, source_target_pairs={{0,8},{8,0},{16,24},{24,16},{32,40},{40,32},{48,56},{56,48},{64,72... | collective-permute-start | bytes 98696 | tf_op jit(solution)/shard_map/ppermute | solution.py:22
  72.2 0.6 collective-permute-done.5
  73.2 0.7 copy-done.5
  74.2 2.3 collective-permute-start.6
  76.5 1.0 collective-permute-done.6
  77.5 1.9 collective-permute-start.7
  79.4 4.7 %collective-permute-done.7 = f32[16,2048]{1,0:T(8,128)S(1)} collective-permute-done((f32[16,2048]{1,0:T(8,128)S(1)}, f32[16,2048]{1,0:T(8,128)S(1)}, u32[]{:S(2)}, u32[]{:S(2)}) %collective-permute-start.7) | collective-permute-done | bytes 131104 | tf_op jit(solution)/shard_map/ppermute | solution.py:22
  84.1 1.9 collective-permute-start.8
  86.0 9.1 %collective-permute-done.8 = f32[16,2048]{1,0:T(8,128)S(1)} collective-permute-done((f32[16,2048]{1,0:T(8,128)S(1)}, f32[16,2048]{1,0:T(8,128)S(1)}, u32[]{:S(2)}, u32[]{:S(2)}) %collective-permute-start.8) | collective-permute-done | bytes 131104 | tf_op jit(solution)/shard_map/ppermute | solution.py:22
  95.1 5.2 %collective-permute-start.9 = (f32[16,2048]{1,0:T(8,128)S(1)}, f32[16,2048]{1,0:T(8,128)S(1)}, u32[]{:S(2)}, u32[]{:S(2)}) collective-permute-start(f32[16,2048]{1,0:T(8,128)S(1)} %add.251), channel_id=1, source_target_pairs={{0,64},{8,72},{16,80},{24,88},{32,96},{40,104},{48,112},{56,120},{... | collective-permute-start | bytes 393224 | tf_op jit(solution)/shard_map/ppermute | solution.py:22
  100.4 13.4 %collective-permute-done.9 = f32[16,2048]{1,0:T(8,128)S(1)} collective-permute-done((f32[16,2048]{1,0:T(8,128)S(1)}, f32[16,2048]{1,0:T(8,128)S(1)}, u32[]{:S(2)}, u32[]{:S(2)}) %collective-permute-start.9) | collective-permute-done | bytes 131104 | tf_op jit(solution)/shard_map/ppermute | solution.py:22
  113.8 10.2 %collective-permute-start.10 = (f32[16,2048]{1,0:T(8,128)S(1)}, f32[16,2048]{1,0:T(8,128)S(1)}, u32[]{:S(2)}, u32[]{:S(2)}) collective-permute-start(f32[16,2048]{1,0:T(8,128)S(1)} %add.252), channel_id=1, source_target_pairs={{0,128},{8,136},{16,144},{24,152},{32,160},{40,168},{48,176},{56,1... | collective-permute-start | bytes 393224 | tf_op jit(solution)/shard_map/ppermute | solution.py:22
  124.1 4.9 %collective-permute-done.10 = f32[16,2048]{1,0:T(8,128)S(1)} collective-permute-done((f32[16,2048]{1,0:T(8,128)S(1)}, f32[16,2048]{1,0:T(8,128)S(1)}, u32[]{:S(2)}, u32[]{:S(2)}) %collective-permute-start.10) | collective-permute-done | bytes 131104 | tf_op jit(solution)/shard_map/ppermute | solution.py:22
  129.0 3.2 %collective-permute-start.11 = (f32[16,2048]{1,0:T(8,128)S(1)}, f32[16,2048]{1,0:T(8,128)S(1)}, u32[]{:S(2)}, u32[]{:S(2)}) collective-permute-start(f32[16,2048]{1,0:T(8,128)S(1)} %add.253), channel_id=1, source_target_pairs={{0,256},{8,264},{16,272},{24,280},{32,288},{40,296},{48,304},{56,3... | collective-permute-start | bytes 393224 | tf_op jit(solution)/shard_map/ppermute | solution.py:22
  133.0 2.0 collective-permute-done.11
  135.2 0.5 copy-done.11
  136.4 3.1 %collective-permute-start.12 = (bf16[1,1,3,2048]{3,2,1,0:T(4,128)(2,1)S(1)}, bf16[1,1,3,2048]{3,2,1,0:T(4,128)(2,1)S(1)}, u32[]{:S(2)}, u32[]{:S(2)}) collective-permute-start(bf16[1,1,3,2048]{3,2,1,0:T(4,128)(2,1)S(1)} %fusion), channel_id=1, source_target_pairs={{0,1},{1,0},{2,3},{3,2},{4,5},{5,4},{6,7},{7,6},{8,9},{9,8},{10,11... | collective-permute-start | bytes 36872 | tf_op jit(solution)/shard_map/ppermute | solution.py:22
  139.5 1.4 collective-permute-done.12
  141.0 4.6 %collective-permute-start.13 = (bf16[2,1,3,2048]{3,2,1,0:T(4,128)(2,1)S(1)}, bf16[2,1,3,2048]{3,2,1,0:T(4,128)(2,1)S(1)}, u32[]{:S(2)}, u32[]{:S(2)}) collective-permute-start(bf16[2,1,3,2048]{3,2,1,0:T(4,128)(2,1)S(1)} %pad_maximum_fusion.8), channel_id=1, source_target_pairs={{0,2},{1,3},{2,0},{3,1},{4,6},{5,7},{6,4},{7,5},{8,10},{9,11},{10,... | collective-permute-start | bytes 73736 | tf_op jit(solution)/shard_map/ppermute | solution.py:22
  145.6 1.5 collective-permute-done.13
  147.2 4.8 %collective-permute-start.14 = (bf16[4,1,3,2048]{3,2,1,0:T(4,128)(2,1)S(1)}, bf16[4,1,3,2048]{3,2,1,0:T(4,128)(2,1)S(1)}, u32[]{:S(2)}, u32[]{:S(2)}) collective-permute-start(bf16[4,1,3,2048]{3,2,1,0:T(4,128)(2,1)S(1)} %pad_maximum_fusion.4), channel_id=1, source_target_pairs={{0,4},{1,5},{2,6},{3,7},{4,0},{5,1},{6,2},{7,3},{8,12},{9,13},{10,... | collective-permute-start | bytes 147464 | tf_op jit(solution)/shard_map/ppermute | solution.py:22
  152.1 1.7 collective-permute-done.14
  154.1 0.3 fusion.13
  154.4 0.6 copy-done.2
  155.0 0.3 fusion.3
  155.6 4.8 %collective-permute-start.15 = (f32[2,2,1,3,2048]{4,3,1,0,2:T(4,128)S(1)}, f32[2,2,1,3,2048]{4,3,1,0,2:T(4,128)S(1)}, u32[]{:S(2)}, u32[]{:S(2)}) collective-permute-start(f32[2,2,1,3,2048]{4,3,1,0,2:T(4,128)S(1)} %dynamic-slice_bitcast_fusion.1), channel_id=1, source_target_pairs={{0,4},{1,5},{2,6},{3,7},{4,0},{5,1},{6,2},{7,3},{8,12},{9,13},{10,... | collective-permute-start | bytes 294920 | tf_op jit(solution)/shard_map/ppermute | solution.py:22
  160.4 2.4 collective-permute-done.15
  162.9 4.6 %collective-permute-start.16 = (f32[2,1,3,2048]{3,2,0,1:T(4,128)S(1)}, f32[2,1,3,2048]{3,2,0,1:T(4,128)S(1)}, u32[]{:S(2)}, u32[]{:S(2)}) collective-permute-start(f32[2,1,3,2048]{3,2,0,1:T(4,128)S(1)} %dynamic-slice_bitcast_fusion.3), channel_id=1, source_target_pairs={{0,2},{1,3},{2,0},{3,1},{4,6},{5,7},{6,4},{7,5},{8,10},{9,11},{10,... | collective-permute-start | bytes 147464 | tf_op jit(solution)/shard_map/ppermute | solution.py:22
  167.5 1.9 collective-permute-done.16
  169.4 3.1 %collective-permute-start.17 = (f32[1,3,2048]{2,1,0:T(4,128)S(1)}, f32[1,3,2048]{2,1,0:T(4,128)S(1)}, u32[]{:S(2)}, u32[]{:S(2)}) collective-permute-start(f32[1,3,2048]{2,1,0:T(4,128)S(1)} %dynamic-slice_bitcast_fusion.5), channel_id=1, source_target_pairs={{0,1},{1,0},{2,3},{3,2},{4,5},{5,4},{6,7},{7,6},{8,9},{9,8},{10,11... | collective-permute-start | bytes 73736 | tf_op jit(solution)/shard_map/ppermute | solution.py:22
  172.5 1.6 collective-permute-done.17
  174.1 0.4 fusion.31
  174.4 17.9 %collective-permute-start.18 = (f32[16,2048]{1,0:T(8,128)S(1)}, f32[16,2048]{1,0:T(8,128)S(1)}, u32[]{:S(2)}, u32[]{:S(2)}) collective-permute-start(f32[16,2048]{1,0:T(8,128)S(1)} %fusion.31), channel_id=1, source_target_pairs={{0,8},{8,0},{16,24},{24,16},{32,40},{40,32},{48,56},{56,48},{64,72... | collective-permute-start | bytes 393224 | tf_op jit(solution)/shard_map/ppermute | solution.py:22
  192.3 1.0 collective-permute-done.18
  193.3 1.9 collective-permute-start.19
  195.2 4.7 %collective-permute-done.19 = f32[16,2048]{1,0:T(8,128)S(1)} collective-permute-done((f32[16,2048]{1,0:T(8,128)S(1)}, f32[16,2048]{1,0:T(8,128)S(1)}, u32[]{:S(2)}, u32[]{:S(2)}) %collective-permute-start.19) | collective-permute-done | bytes 131104 | tf_op jit(solution)/shard_map/ppermute | solution.py:22
  199.9 1.9 collective-permute-start.20
  201.8 9.1 %collective-permute-done.20 = f32[16,2048]{1,0:T(8,128)S(1)} collective-permute-done((f32[16,2048]{1,0:T(8,128)S(1)}, f32[16,2048]{1,0:T(8,128)S(1)}, u32[]{:S(2)}, u32[]{:S(2)}) %collective-permute-start.20) | collective-permute-done | bytes 131104 | tf_op jit(solution)/shard_map/ppermute | solution.py:22
  210.9 3.8 %collective-permute-start.21 = (f32[16,2048]{1,0:T(8,128)S(1)}, f32[16,2048]{1,0:T(8,128)S(1)}, u32[]{:S(2)}, u32[]{:S(2)}) collective-permute-start(f32[16,2048]{1,0:T(8,128)S(1)} %add.270), channel_id=1, source_target_pairs={{0,64},{8,72},{16,80},{24,88},{32,96},{40,104},{48,112},{56,120},{... | collective-permute-start | bytes 393224 | tf_op jit(solution)/shard_map/ppermute | solution.py:22
  214.7 13.4 %collective-permute-done.21 = f32[16,2048]{1,0:T(8,128)S(1)} collective-permute-done((f32[16,2048]{1,0:T(8,128)S(1)}, f32[16,2048]{1,0:T(8,128)S(1)}, u32[]{:S(2)}, u32[]{:S(2)}) %collective-permute-start.21) | collective-permute-done | bytes 131104 | tf_op jit(solution)/shard_map/ppermute | solution.py:22
  228.1 6.2 %collective-permute-start.22 = (f32[16,2048]{1,0:T(8,128)S(1)}, f32[16,2048]{1,0:T(8,128)S(1)}, u32[]{:S(2)}, u32[]{:S(2)}) collective-permute-start(f32[16,2048]{1,0:T(8,128)S(1)} %add.271), channel_id=1, source_target_pairs={{0,128},{8,136},{16,144},{24,152},{32,160},{40,168},{48,176},{56,1... | collective-permute-start | bytes 393224 | tf_op jit(solution)/shard_map/ppermute | solution.py:22
  234.4 14.5 %collective-permute-done.22 = f32[16,2048]{1,0:T(8,128)S(1)} collective-permute-done((f32[16,2048]{1,0:T(8,128)S(1)}, f32[16,2048]{1,0:T(8,128)S(1)}, u32[]{:S(2)}, u32[]{:S(2)}) %collective-permute-start.22) | collective-permute-done | bytes 131104 | tf_op jit(solution)/shard_map/ppermute | solution.py:22
  248.9 3.4 %collective-permute-start.23 = (f32[16,2048]{1,0:T(8,128)S(1)}, f32[16,2048]{1,0:T(8,128)S(1)}, u32[]{:S(2)}, u32[]{:S(2)}) collective-permute-start(f32[16,2048]{1,0:T(8,128)S(1)} %add.272), channel_id=1, source_target_pairs={{0,256},{8,264},{16,272},{24,280},{32,288},{40,296},{48,304},{56,3... | collective-permute-start | bytes 393224 | tf_op jit(solution)/shard_map/ppermute | solution.py:22
  252.2 3.1 %collective-permute-done.23 = f32[16,2048]{1,0:T(8,128)S(1)} collective-permute-done((f32[16,2048]{1,0:T(8,128)S(1)}, f32[16,2048]{1,0:T(8,128)S(1)}, u32[]{:S(2)}, u32[]{:S(2)}) %collective-permute-start.23) | collective-permute-done | bytes 131104 | tf_op jit(solution)/shard_map/ppermute | solution.py:22
  255.3 0.7 reshape.323
  (131 shorter events, 8.4 us)
Async XLA Ops:
  0.0 1.2 copy-start
  0.0 0.7 copy-start.12
  1.2 1.4 copy-start.6
  1.2 1.4 copy-start.7
  5.0 8.5 %collective-permute-start = (f32[2,2,2,4,4,514]{5,4,3,2,1,0:T(4,128)S(1)}, f32[2,2,2,4,4,514]{5,4,3,2,1,0:T(4,128)S(1)}, u32[]{:S(2)}, u32[]{:S(2)}) collective-permute-start(f32[2,2,2,4,4,514]{5,4,3,2,1,0:T(4,128)S(1)} %pad_maximum_fusion), channel_id=1, source_target_pairs={{0,256},{8,264},{16,272},{24,280},{32,288},{40,296},{48,304},{56,3... | collective-permute-start | bytes 789512 | tf_op jit(solution)/shard_map/ppermute | solution.py:22
  14.7 7.8 %copy-start.13 = (bf16[4,4,512]{2,1,0:T(4,128)(2,1)S(1)}, bf16[4,4,512]{2,1,0:T(4,128)(2,1)}, u32[]{:S(2)}) copy-start(bf16[4,4,512]{2,1,0:T(4,128)(2,1)} %param.19) | copy-start | bytes 49156
  14.8 14.5 %collective-permute-start.1 = (f32[2,2,4,4,514]{4,3,2,1,0:T(4,128)S(1)}, f32[2,2,4,4,514]{4,3,2,1,0:T(4,128)S(1)}, u32[]{:S(2)}, u32[]{:S(2)}) collective-permute-start(f32[2,2,4,4,514]{4,3,2,1,0:T(4,128)S(1)} %pad_maximum_fusion.1), channel_id=1, source_target_pairs={{0,32},{8,40},{16,48},{24,56},{32,0},{40,8},{48,16},{56,24},{64,96... | collective-permute-start | bytes 394760 | tf_op jit(solution)/shard_map/ppermute | solution.py:22
  30.3 10.6 %collective-permute-start.2 = (f32[2,4,4,514]{3,2,1,0:T(4,128)S(1)}, f32[2,4,4,514]{3,2,1,0:T(4,128)S(1)}, u32[]{:S(2)}, u32[]{:S(2)}) collective-permute-start(f32[2,4,4,514]{3,2,1,0:T(4,128)S(1)} %pad_maximum_fusion.3), channel_id=1, source_target_pairs={{0,64},{8,72},{16,80},{24,88},{32,96},{40,104},{48,112},{56,120},{... | collective-permute-start | bytes 197384 | tf_op jit(solution)/shard_map/ppermute | solution.py:22
  41.7 20.4 %collective-permute-start.3 = (f32[4,4,514]{2,1,0:T(4,128)S(1)}, f32[4,4,514]{2,1,0:T(4,128)S(1)}, u32[]{:S(2)}, u32[]{:S(2)}) collective-permute-start(f32[4,4,514]{2,1,0:T(4,128)S(1)} %pad_maximum_fusion.5), channel_id=1, source_target_pairs={{0,128},{8,136},{16,144},{24,152},{32,160},{40,168},{48,176},{56,1... | collective-permute-start | bytes 98696 | tf_op jit(solution)/shard_map/ppermute | solution.py:22
  62.4 2.0 copy-start.14
  62.5 4.7 %collective-permute-start.4 = (f32[4,4,514]{2,1,0:T(4,128)S(1)}, f32[4,4,514]{2,1,0:T(4,128)S(1)}, u32[]{:S(2)}, u32[]{:S(2)}) collective-permute-start(f32[4,4,514]{2,1,0:T(4,128)S(1)} %pad_maximum_fusion.6), channel_id=1, source_target_pairs={{0,16},{8,24},{16,0},{24,8},{32,48},{40,56},{48,32},{56,40},{64,80... | collective-permute-start | bytes 98696 | tf_op jit(solution)/shard_map/ppermute | solution.py:22
  67.5 5.3 %collective-permute-start.5 = (f32[4,4,514]{2,1,0:T(4,128)S(1)}, f32[4,4,514]{2,1,0:T(4,128)S(1)}, u32[]{:S(2)}, u32[]{:S(2)}) collective-permute-start(f32[4,4,514]{2,1,0:T(4,128)S(1)} %pad_maximum_fusion.7), channel_id=1, source_target_pairs={{0,8},{8,0},{16,24},{24,16},{32,40},{40,32},{48,56},{56,48},{64,72... | collective-permute-start | bytes 98696 | tf_op jit(solution)/shard_map/ppermute | solution.py:22
  73.0 0.9 copy-start.5
  73.2 0.8 copy-start.10
  74.2 3.2 %collective-permute-start.6 = (f32[16,2048]{1,0:T(8,128)S(1)}, f32[16,2048]{1,0:T(8,128)S(1)}, u32[]{:S(2)}, u32[]{:S(2)}) collective-permute-start(f32[16,2048]{1,0:T(8,128)S(1)} %fusion.9), channel_id=1, source_target_pairs={{0,8},{8,0},{16,24},{24,16},{32,40},{40,32},{48,56},{56,48},{64,72... | collective-permute-start | bytes 393224 | tf_op jit(solution)/shard_map/ppermute | solution.py:22
  77.5 6.6 %collective-permute-start.7 = (f32[16,2048]{1,0:T(8,128)S(1)}, f32[16,2048]{1,0:T(8,128)S(1)}, u32[]{:S(2)}, u32[]{:S(2)}) collective-permute-start(f32[16,2048]{1,0:T(8,128)S(1)} %add.249), channel_id=1, source_target_pairs={{0,16},{8,24},{16,0},{24,8},{32,48},{40,56},{48,32},{56,40},{64,80... | collective-permute-start | bytes 393224 | tf_op jit(solution)/shard_map/ppermute | solution.py:22
  84.1 11.0 %collective-permute-start.8 = (f32[16,2048]{1,0:T(8,128)S(1)}, f32[16,2048]{1,0:T(8,128)S(1)}, u32[]{:S(2)}, u32[]{:S(2)}) collective-permute-start(f32[16,2048]{1,0:T(8,128)S(1)} %add.250), channel_id=1, source_target_pairs={{0,32},{8,40},{16,48},{24,56},{32,0},{40,8},{48,16},{56,24},{64,96... | collective-permute-start | bytes 393224 | tf_op jit(solution)/shard_map/ppermute | solution.py:22
  95.1 28.9 %copy-start.8 = (s32[4,4,6]{2,1,0:T(4,128)S(1)}, s32[4,4,6]{2,1,0:T(4,128)}, u32[]{:S(2)}) copy-start(s32[4,4,6]{2,1,0:T(4,128)} %param.28) | copy-start | bytes 1156
  95.1 18.6 %collective-permute-start.9 = (f32[16,2048]{1,0:T(8,128)S(1)}, f32[16,2048]{1,0:T(8,128)S(1)}, u32[]{:S(2)}, u32[]{:S(2)}) collective-permute-start(f32[16,2048]{1,0:T(8,128)S(1)} %add.251), channel_id=1, source_target_pairs={{0,64},{8,72},{16,80},{24,88},{32,96},{40,104},{48,112},{56,120},{... | collective-permute-start | bytes 393224 | tf_op jit(solution)/shard_map/ppermute | solution.py:22
  113.8 15.2 %collective-permute-start.10 = (f32[16,2048]{1,0:T(8,128)S(1)}, f32[16,2048]{1,0:T(8,128)S(1)}, u32[]{:S(2)}, u32[]{:S(2)}) collective-permute-start(f32[16,2048]{1,0:T(8,128)S(1)} %add.252), channel_id=1, source_target_pairs={{0,128},{8,136},{16,144},{24,152},{32,160},{40,168},{48,176},{56,1... | collective-permute-start | bytes 393224 | tf_op jit(solution)/shard_map/ppermute | solution.py:22
  129.0 3.3 %copy-start.9 = (bf16[4,4,2048]{2,1,0:T(4,128)(2,1)S(1)}, bf16[4,4,2048]{2,1,0:T(4,128)(2,1)}, u32[]{:S(2)}) copy-start(bf16[4,4,2048]{2,1,0:T(4,128)(2,1)} %param.16) | copy-start | bytes 196612
  129.0 6.0 %collective-permute-start.11 = (f32[16,2048]{1,0:T(8,128)S(1)}, f32[16,2048]{1,0:T(8,128)S(1)}, u32[]{:S(2)}, u32[]{:S(2)}) collective-permute-start(f32[16,2048]{1,0:T(8,128)S(1)} %add.253), channel_id=1, source_target_pairs={{0,256},{8,264},{16,272},{24,280},{32,288},{40,296},{48,304},{56,3... | collective-permute-start | bytes 393224 | tf_op jit(solution)/shard_map/ppermute | solution.py:22
  133.0 2.2 copy-start.4
  135.0 0.7 copy-start.11
  135.9 18.1 %copy-start.1 = (bf16[1,2048,176]{1,2,0:T(8,128)(2,1)S(1)}, bf16[1,2048,176]{1,2,0:T(8,128)(2,1)}, u32[]{:S(2)}) copy-start(bf16[1,2048,176]{1,2,0:T(8,128)(2,1)} %param.29) | copy-start | bytes 2162692
  136.4 4.5 %collective-permute-start.12 = (bf16[1,1,3,2048]{3,2,1,0:T(4,128)(2,1)S(1)}, bf16[1,1,3,2048]{3,2,1,0:T(4,128)(2,1)S(1)}, u32[]{:S(2)}, u32[]{:S(2)}) collective-permute-start(bf16[1,1,3,2048]{3,2,1,0:T(4,128)(2,1)S(1)} %fusion), channel_id=1, source_target_pairs={{0,1},{1,0},{2,3},{3,2},{4,5},{5,4},{6,7},{7,6},{8,9},{9,8},{10,11... | collective-permute-start | bytes 36872 | tf_op jit(solution)/shard_map/ppermute | solution.py:22
  141.0 6.2 %collective-permute-start.13 = (bf16[2,1,3,2048]{3,2,1,0:T(4,128)(2,1)S(1)}, bf16[2,1,3,2048]{3,2,1,0:T(4,128)(2,1)S(1)}, u32[]{:S(2)}, u32[]{:S(2)}) collective-permute-start(bf16[2,1,3,2048]{3,2,1,0:T(4,128)(2,1)S(1)} %pad_maximum_fusion.8), channel_id=1, source_target_pairs={{0,2},{1,3},{2,0},{3,1},{4,6},{5,7},{6,4},{7,5},{8,10},{9,11},{10,... | collective-permute-start | bytes 73736 | tf_op jit(solution)/shard_map/ppermute | solution.py:22
  147.2 6.5 %collective-permute-start.14 = (bf16[4,1,3,2048]{3,2,1,0:T(4,128)(2,1)S(1)}, bf16[4,1,3,2048]{3,2,1,0:T(4,128)(2,1)S(1)}, u32[]{:S(2)}, u32[]{:S(2)}) collective-permute-start(bf16[4,1,3,2048]{3,2,1,0:T(4,128)(2,1)S(1)} %pad_maximum_fusion.4), channel_id=1, source_target_pairs={{0,4},{1,5},{2,6},{3,7},{4,0},{5,1},{6,2},{7,3},{8,12},{9,13},{10,... | collective-permute-start | bytes 147464 | tf_op jit(solution)/shard_map/ppermute | solution.py:22
  153.8 1.1 copy-start.2
  154.0 1.2 copy-start.3
  155.6 7.2 %collective-permute-start.15 = (f32[2,2,1,3,2048]{4,3,1,0,2:T(4,128)S(1)}, f32[2,2,1,3,2048]{4,3,1,0,2:T(4,128)S(1)}, u32[]{:S(2)}, u32[]{:S(2)}) collective-permute-start(f32[2,2,1,3,2048]{4,3,1,0,2:T(4,128)S(1)} %dynamic-slice_bitcast_fusion.1), channel_id=1, source_target_pairs={{0,4},{1,5},{2,6},{3,7},{4,0},{5,1},{6,2},{7,3},{8,12},{9,13},{10,... | collective-permute-start | bytes 294920 | tf_op jit(solution)/shard_map/ppermute | solution.py:22
  162.9 6.5 %collective-permute-start.16 = (f32[2,1,3,2048]{3,2,0,1:T(4,128)S(1)}, f32[2,1,3,2048]{3,2,0,1:T(4,128)S(1)}, u32[]{:S(2)}, u32[]{:S(2)}) collective-permute-start(f32[2,1,3,2048]{3,2,0,1:T(4,128)S(1)} %dynamic-slice_bitcast_fusion.3), channel_id=1, source_target_pairs={{0,2},{1,3},{2,0},{3,1},{4,6},{5,7},{6,4},{7,5},{8,10},{9,11},{10,... | collective-permute-start | bytes 147464 | tf_op jit(solution)/shard_map/ppermute | solution.py:22
  169.4 4.7 %collective-permute-start.17 = (f32[1,3,2048]{2,1,0:T(4,128)S(1)}, f32[1,3,2048]{2,1,0:T(4,128)S(1)}, u32[]{:S(2)}, u32[]{:S(2)}) collective-permute-start(f32[1,3,2048]{2,1,0:T(4,128)S(1)} %dynamic-slice_bitcast_fusion.5), channel_id=1, source_target_pairs={{0,1},{1,0},{2,3},{3,2},{4,5},{5,4},{6,7},{7,6},{8,9},{9,8},{10,11... | collective-permute-start | bytes 73736 | tf_op jit(solution)/shard_map/ppermute | solution.py:22
  174.4 18.8 %collective-permute-start.18 = (f32[16,2048]{1,0:T(8,128)S(1)}, f32[16,2048]{1,0:T(8,128)S(1)}, u32[]{:S(2)}, u32[]{:S(2)}) collective-permute-start(f32[16,2048]{1,0:T(8,128)S(1)} %fusion.31), channel_id=1, source_target_pairs={{0,8},{8,0},{16,24},{24,16},{32,40},{40,32},{48,56},{56,48},{64,72... | collective-permute-start | bytes 393224 | tf_op jit(solution)/shard_map/ppermute | solution.py:22
  193.3 6.6 %collective-permute-start.19 = (f32[16,2048]{1,0:T(8,128)S(1)}, f32[16,2048]{1,0:T(8,128)S(1)}, u32[]{:S(2)}, u32[]{:S(2)}) collective-permute-start(f32[16,2048]{1,0:T(8,128)S(1)} %add.268), channel_id=1, source_target_pairs={{0,16},{8,24},{16,0},{24,8},{32,48},{40,56},{48,32},{56,40},{64,80... | collective-permute-start | bytes 393224 | tf_op jit(solution)/shard_map/ppermute | solution.py:22
  199.9 11.0 %collective-permute-start.20 = (f32[16,2048]{1,0:T(8,128)S(1)}, f32[16,2048]{1,0:T(8,128)S(1)}, u32[]{:S(2)}, u32[]{:S(2)}) collective-permute-start(f32[16,2048]{1,0:T(8,128)S(1)} %add.269), channel_id=1, source_target_pairs={{0,32},{8,40},{16,48},{24,56},{32,0},{40,8},{48,16},{56,24},{64,96... | collective-permute-start | bytes 393224 | tf_op jit(solution)/shard_map/ppermute | solution.py:22
  210.9 17.2 %collective-permute-start.21 = (f32[16,2048]{1,0:T(8,128)S(1)}, f32[16,2048]{1,0:T(8,128)S(1)}, u32[]{:S(2)}, u32[]{:S(2)}) collective-permute-start(f32[16,2048]{1,0:T(8,128)S(1)} %add.270), channel_id=1, source_target_pairs={{0,64},{8,72},{16,80},{24,88},{32,96},{40,104},{48,112},{56,120},{... | collective-permute-start | bytes 393224 | tf_op jit(solution)/shard_map/ppermute | solution.py:22
  228.1 20.7 %collective-permute-start.22 = (f32[16,2048]{1,0:T(8,128)S(1)}, f32[16,2048]{1,0:T(8,128)S(1)}, u32[]{:S(2)}, u32[]{:S(2)}) collective-permute-start(f32[16,2048]{1,0:T(8,128)S(1)} %add.271), channel_id=1, source_target_pairs={{0,128},{8,136},{16,144},{24,152},{32,160},{40,168},{48,176},{56,1... | collective-permute-start | bytes 393224 | tf_op jit(solution)/shard_map/ppermute | solution.py:22
  248.9 6.5 %collective-permute-start.23 = (f32[16,2048]{1,0:T(8,128)S(1)}, f32[16,2048]{1,0:T(8,128)S(1)}, u32[]{:S(2)}, u32[]{:S(2)}) collective-permute-start(f32[16,2048]{1,0:T(8,128)S(1)} %add.272), channel_id=1, source_target_pairs={{0,256},{8,264},{16,272},{24,280},{32,288},{40,296},{48,304},{56,3... | collective-permute-start | bytes 393224 | tf_op jit(solution)/shard_map/ppermute | solution.py:22

commit v2 on v1

--- a/solution.py
+++ b/solution.py
@@ -177,16 +177,13 @@
     dispatched = jnp.einsum(
         "esr,rd->esd", dispatch_map.astype(jnp.bfloat16), normed, preferred_element_type=jnp.float32
     ).astype(jnp.bfloat16)
-    gathered = butterfly_gather(dispatched, "exp", range(exp_bits))
-    groups = gathered.shape[0]
-    piece = gathered.transpose(1, 0, 2, 3).reshape(local_count, groups * CAP, width)
-    gate = jnp.einsum("erd,edf->erf", piece, w_gate, preferred_element_type=jnp.float32)
-    upper = jnp.einsum("erd,edf->erf", piece, w_up, preferred_element_type=jnp.float32)
+    gate_w = lax.all_gather(w_gate, "exp", axis=2, tiled=True)
+    up_w = lax.all_gather(w_up, "exp", axis=2, tiled=True)
+    down_w = lax.all_gather(w_down, "exp", axis=1, tiled=True)
+    gate = jnp.einsum("erd,edf->erf", dispatched, gate_w, preferred_element_type=jnp.float32)
+    upper = jnp.einsum("erd,edf->erf", dispatched, up_w, preferred_element_type=jnp.float32)
     hidden_all = (jax.nn.silu(gate) * upper).astype(jnp.bfloat16)
-    partial_out = jnp.einsum("erf,efd->erd", hidden_all, w_down, preferred_element_type=jnp.float32)
-    split_out = partial_out.reshape((local_count,) + (2,) * exp_bits + (CAP, width))
-    split_out = jnp.moveaxis(split_out, 0, exp_bits)
-    expert_out = butterfly_scatter_sum(split_out, "exp", range(exp_bits - 1, -1, -1))
+    expert_out = jnp.einsum("erf,efd->erd", hidden_all, down_w, preferred_element_type=jnp.float32)
     moe_part = jnp.einsum("esr,esd->rd", combine_map, expert_out, precision=lax.Precision.HIGHEST)
     moe_all = butterfly_sum(moe_part, "blk", range(blk_bits))
     result = (mixed + moe_all).astype(jnp.bfloat16)

time: 257 us -> 403 us (1.57)
  waiting for transfers between devices: 108 us -> 260 us
  starting transfers between devices: 131 us -> 103 us
  between operations: 0.72 us -> 13.7 us
  matrix products: 4.35 us -> 15.8 us
    all_gather x0 -> x3, waiting for transfers between devices: none -> 168 us  [the longest x1 101 us: local(): down_w = lax.all_gather(w_down, 'exp', axis=1, tiled=True)]
    ppermute x24 -> x18, starting transfers between devices: 131 us -> 103 us  [exchange(): lax.ppermute(part, axis, xor_pairs(count, mask))]
    ppermute x24 -> x18, waiting for transfers between devices: 108 us -> 90 us  [exchange(): lax.ppermute(part, axis, xor_pairs(count, mask))]
    dot_general x3 -> x2, matrix products: 0.82 us -> 11.3 us  [the longest x1 7.01 us: local(): jnp.einsum('erf,efd->erd', hidden_all, down_w, preferred_element_type=jnp...]
  transfers between devices with their start and end apart: 24 -> 21, of which waited for: 24 -> 20; matrix products, arithmetic and copies ran while one was open for 1% -> 4% of each run, Pallas kernels for 0% -> 0%
where the time goes in v2:
time: 403 us; the launch traced here: 402 us
  waiting for transfers between devices  260 us (65%)
  starting transfers between devices  103 us (26%)
  matrix products  15.8 us (4%)
  between operations  13.7 us (3%)
  local copies, waits for them, and re-layouts  6.86 us (2%)
    ppermute x18, starting transfers between devices, exchange(): lax.ppermute(part, axis, xor_pairs(count, mask))  103 us
    all_gather x1, waiting for transfers between devices, local(): down_w = lax.all_gather(w_down, 'exp', axis=1, tiled=True)  101 us
    ppermute x18, waiting for transfers between devices, exchange(): lax.ppermute(part, axis, xor_pairs(count, mask))  90 us
    all_gather x1, waiting for transfers between devices, local(): up_w = lax.all_gather(w_up, 'exp', axis=2, tiled=True)  66.7 us
  transfers between devices with their start and end apart: 21, of which 20 were waited for; matrix products, arithmetic and copies ran while one was open for 4% of the time, Pallas kernels for 0%

profile of v2, /device:TPU:1, one launch (start us, length us, event | category | flops | bytes accessed | tf_op | source)
XLA Modules:
  0.0 402.4 jit_solution(3735238704035035130)
XLA Ops:
  6.5 0.7 all-gather.4.cloned.1.call-update
  7.3 0.7 all-gather.6.cloned.1.call-update
  8.1 0.7 all-gather.8.cloned.1.call-update
  8.8 0.7 broadcast_compare_fusion
  9.5 1.4 fusion.115
  10.9 1.2 fusion.113
  12.1 0.2 fusion.23
  12.4 0.3 fusion.25
  13.0 0.3 copy.117
  13.3 0.3 copy.142
  13.8 0.3 copy.116
  14.3 4.0 collective-permute-start
  18.3 0.9 constant_dynamic-slice_fusion.1
  19.3 3.5 collective-permute-done
  22.7 0.2 fusion.110
  23.0 0.3 copy.145
  23.3 0.2 copy.121
  23.5 0.2 copy.122
  24.0 7.7 %collective-permute-start.1 = (f32[2,2,4,4,514]{4,3,2,1,0:T(4,128)S(1)}, f32[2,2,4,4,514]{4,3,2,1,0:T(4,128)S(1)}, u32[]{:S(2)}, u32[]{:S(2)}) collective-permute-start(f32[2,2,4,4,514]{4,3,2,1,0:T(4,128)S(1)} %pad_maximum_fusion.1), channel_id=1, source_target_pairs={{0,32},{8,40},{16,48},{24,56},{32,0},{40,8},{48,16},{56,24},{64,96... | collective-permute-start | bytes 394760 | tf_op jit(solution)/shard_map/ppermute | solution.py:22
  31.9 6.8 %collective-permute-done.1 = f32[2,2,4,4,514]{4,3,2,1,0:T(4,128)S(1)} collective-permute-done((f32[2,2,4,4,514]{4,3,2,1,0:T(4,128)S(1)}, f32[2,2,4,4,514]{4,3,2,1,0:T(4,128)S(1)}, u32[]{:S(2)}, u32[]{:S(2)}) %collective-permute-start.1) | collective-permute-done | bytes 131616 | tf_op jit(solution)/shard_map/ppermute | solution.py:22
  39.6 8.8 %collective-permute-start.2 = (f32[2,4,4,514]{3,2,1,0:T(4,128)S(1)}, f32[2,4,4,514]{3,2,1,0:T(4,128)S(1)}, u32[]{:S(2)}, u32[]{:S(2)}) collective-permute-start(f32[2,4,4,514]{3,2,1,0:T(4,128)S(1)} %pad_maximum_fusion.2), channel_id=1, source_target_pairs={{0,64},{8,72},{16,80},{24,88},{32,96},{40,104},{48,112},{56,120},{... | collective-permute-start | bytes 197384 | tf_op jit(solution)/shard_map/ppermute | solution.py:22
  48.4 0.8 constant_dynamic-slice_fusion
  49.2 1.0 collective-permute-done.2
  51.0 18.9 %collective-permute-start.3 = (f32[4,4,514]{2,1,0:T(4,128)S(1)}, f32[4,4,514]{2,1,0:T(4,128)S(1)}, u32[]{:S(2)}, u32[]{:S(2)}) collective-permute-start(f32[4,4,514]{2,1,0:T(4,128)S(1)} %pad_maximum_fusion.3), channel_id=1, source_target_pairs={{0,128},{8,136},{16,144},{24,152},{32,160},{40,168},{48,176},{56,1... | collective-permute-start | bytes 98696 | tf_op jit(solution)/shard_map/ppermute | solution.py:22
  70.2 1.1 collective-permute-done.3
  71.6 1.9 collective-permute-start.4
  73.7 3.1 collective-permute-done.4
  77.1 4.0 collective-permute-start.5
  81.4 0.6 collective-permute-done.5
  82.1 0.2 fusion.38
  82.4 0.3 fusion.19
  82.7 2.3 collective-permute-start.6
  84.9 1.0 collective-permute-done.6
  85.9 1.9 collective-permute-start.7
  87.9 4.8 %collective-permute-done.7 = f32[16,2048]{1,0:T(8,128)S(1)} collective-permute-done((f32[16,2048]{1,0:T(8,128)S(1)}, f32[16,2048]{1,0:T(8,128)S(1)}, u32[]{:S(2)}, u32[]{:S(2)}) %collective-permute-start.7) | collective-permute-done | bytes 131104 | tf_op jit(solution)/shard_map/ppermute | solution.py:22
  92.7 1.9 collective-permute-start.8
  94.6 9.1 %collective-permute-done.8 = f32[16,2048]{1,0:T(8,128)S(1)} collective-permute-done((f32[16,2048]{1,0:T(8,128)S(1)}, f32[16,2048]{1,0:T(8,128)S(1)}, u32[]{:S(2)}, u32[]{:S(2)}) %collective-permute-start.8) | collective-permute-done | bytes 131104 | tf_op jit(solution)/shard_map/ppermute | solution.py:22
  103.7 5.4 %collective-permute-start.9 = (f32[16,2048]{1,0:T(8,128)S(1)}, f32[16,2048]{1,0:T(8,128)S(1)}, u32[]{:S(2)}, u32[]{:S(2)}) collective-permute-start(f32[16,2048]{1,0:T(8,128)S(1)} %add.218), channel_id=1, source_target_pairs={{0,64},{8,72},{16,80},{24,88},{32,96},{40,104},{48,112},{56,120},{... | collective-permute-start | bytes 393224 | tf_op jit(solution)/shard_map/ppermute | solution.py:22
  109.1 13.3 %collective-permute-done.9 = f32[16,2048]{1,0:T(8,128)S(1)} collective-permute-done((f32[16,2048]{1,0:T(8,128)S(1)}, f32[16,2048]{1,0:T(8,128)S(1)}, u32[]{:S(2)}, u32[]{:S(2)}) %collective-permute-start.9) | collective-permute-done | bytes 131104 | tf_op jit(solution)/shard_map/ppermute | solution.py:22
  122.3 10.2 %collective-permute-start.10 = (f32[16,2048]{1,0:T(8,128)S(1)}, f32[16,2048]{1,0:T(8,128)S(1)}, u32[]{:S(2)}, u32[]{:S(2)}) collective-permute-start(f32[16,2048]{1,0:T(8,128)S(1)} %add.219), channel_id=1, source_target_pairs={{0,128},{8,136},{16,144},{24,152},{32,160},{40,168},{48,176},{56,1... | collective-permute-start | bytes 393224 | tf_op jit(solution)/shard_map/ppermute | solution.py:22
  132.6 4.9 %collective-permute-done.10 = f32[16,2048]{1,0:T(8,128)S(1)} collective-permute-done((f32[16,2048]{1,0:T(8,128)S(1)}, f32[16,2048]{1,0:T(8,128)S(1)}, u32[]{:S(2)}, u32[]{:S(2)}) %collective-permute-start.10) | collective-permute-done | bytes 131104 | tf_op jit(solution)/shard_map/ppermute | solution.py:22
  137.5 3.2 collective-permute-start.11
  141.0 0.3 reduce_window_sum.11
  141.5 5.1 %collective-permute-done.11 = f32[16,2048]{1,0:T(8,128)S(1)} collective-permute-done((f32[16,2048]{1,0:T(8,128)S(1)}, f32[16,2048]{1,0:T(8,128)S(1)}, u32[]{:S(2)}, u32[]{:S(2)}) %collective-permute-start.11) | collective-permute-done | bytes 131104 | tf_op jit(solution)/shard_map/ppermute | solution.py:22
  146.7 0.2 fusion.16
  147.0 0.2 select_reduce_fusion
  147.5 4.3 %fusion.4 = f32[3,1408]{1,0:T(4,128)S(1)} fusion(bf16[3,2048]{1,0:T(4,128)(2,1)S(1)} %convolution_convert_fusion, bf16[1,2048,1408]{1,2,0:T(8,128)(2,1)} %all-gather.4.cloned.1.call-done), kind=kOutput, calls=%fused_computation.4 | convolution fusion | flops 17301504 | bytes 5796352 | tf_op jit(solution)/shard_map/erd,edf->erf/dot_general | solution.py:183
  151.8 66.7 %all-gather.6.cloned.1.call-done = bf16[1,2048,1408]{1,2,0:T(8,128)(2,1)} async-done(((bf16[1,2048,176]{1,2,0:T(8,128)(2,1)}), bf16[1,2048,1408]{1,2,0:T(8,128)(2,1)}) %all-gather.6.cloned.1.call-update) | async-done | bytes 5767184 | tf_op jit(solution)/shard_map/all_gather | solution.py:181
  218.5 100.9 %all-gather.8.cloned.1.call-done = bf16[1,1408,2048]{2,1,0:T(8,128)(2,1)} async-done(((bf16[1,176,2048]{2,1,0:T(8,128)(2,1)}), bf16[1,1408,2048]{2,1,0:T(8,128)(2,1)}) %all-gather.8.cloned.1.call-update) | async-done | bytes 5767184 | tf_op jit(solution)/shard_map/all_gather | solution.py:182
  319.4 7.0 %fusion = f32[3,2048]{1,0:T(4,128)S(1)} fusion(bf16[1,1408,2048]{2,1,0:T(8,128)(2,1)} %all-gather.8.cloned.1.call-done, bf16[3,2048]{1,0:T(4,128)(2,1)S(1)} %convolution_convert_fusion, bf16[1,2048,1408]{1,2,0:T(8,128)(2,1)} %all-gather.6.cloned.1.call-done, f32[3,1408]{1,0:T(4,128)S(1)} %fusion.4), kind=kOutput, calls=%fused_computation | convolution fusion | flops 34628352 | bytes 11588096 | tf_op jit(solution)/shard_map/erf,efd->erd/dot_general | solution.py:186
  326.4 0.4 fusion.116
  326.8 3.3 collective-permute-start.12
  330.1 1.0 collective-permute-done.12
  331.1 3.2 collective-permute-start.13
  334.3 3.4 collective-permute-done.13
  337.7 4.2 %collective-permute-start.14 = (f32[16,2048]{1,0:T(8,128)S(1)}, f32[16,2048]{1,0:T(8,128)S(1)}, u32[]{:S(2)}, u32[]{:S(2)}) collective-permute-start(f32[16,2048]{1,0:T(8,128)S(1)} %add.227), channel_id=1, source_target_pairs={{0,32},{8,40},{16,48},{24,56},{32,0},{40,8},{48,16},{56,24},{64,96... | collective-permute-start | bytes 393224 | tf_op jit(solution)/shard_map/ppermute | solution.py:22
  341.9 5.8 %collective-permute-done.14 = f32[16,2048]{1,0:T(8,128)S(1)} collective-permute-done((f32[16,2048]{1,0:T(8,128)S(1)}, f32[16,2048]{1,0:T(8,128)S(1)}, u32[]{:S(2)}, u32[]{:S(2)}) %collective-permute-start.14) | collective-permute-done | bytes 131104 | tf_op jit(solution)/shard_map/ppermute | solution.py:22
  347.8 7.4 %collective-permute-start.15 = (f32[16,2048]{1,0:T(8,128)S(1)}, f32[16,2048]{1,0:T(8,128)S(1)}, u32[]{:S(2)}, u32[]{:S(2)}) collective-permute-start(f32[16,2048]{1,0:T(8,128)S(1)} %add.228), channel_id=1, source_target_pairs={{0,64},{8,72},{16,80},{24,88},{32,96},{40,104},{48,112},{56,120},{... | collective-permute-start | bytes 393224 | tf_op jit(solution)/shard_map/ppermute | solution.py:22
  355.1 10.7 %collective-permute-done.15 = f32[16,2048]{1,0:T(8,128)S(1)} collective-permute-done((f32[16,2048]{1,0:T(8,128)S(1)}, f32[16,2048]{1,0:T(8,128)S(1)}, u32[]{:S(2)}, u32[]{:S(2)}) %collective-permute-start.15) | collective-permute-done | bytes 131104 | tf_op jit(solution)/shard_map/ppermute | solution.py:22
  365.8 12.2 %collective-permute-start.16 = (f32[16,2048]{1,0:T(8,128)S(1)}, f32[16,2048]{1,0:T(8,128)S(1)}, u32[]{:S(2)}, u32[]{:S(2)}) collective-permute-start(f32[16,2048]{1,0:T(8,128)S(1)} %add.229), channel_id=1, source_target_pairs={{0,128},{8,136},{16,144},{24,152},{32,160},{40,168},{48,176},{56,1... | collective-permute-start | bytes 393224 | tf_op jit(solution)/shard_map/ppermute | solution.py:22
  378.1 11.4 %collective-permute-done.16 = f32[16,2048]{1,0:T(8,128)S(1)} collective-permute-done((f32[16,2048]{1,0:T(8,128)S(1)}, f32[16,2048]{1,0:T(8,128)S(1)}, u32[]{:S(2)}, u32[]{:S(2)}) %collective-permute-start.16) | collective-permute-done | bytes 131104 | tf_op jit(solution)/shard_map/ppermute | solution.py:22
  389.5 2.2 collective-permute-start.17
  391.7 3.5 collective-permute-done.17
  395.2 0.7 reshape.304
  (102 shorter events, 5.3 us)
Async XLA Ops:
  6.5 3.0 copy-start
  6.5 25.2 %copy-start.7 = (bf16[4,4,512]{2,1,0:T(4,128)(2,1)S(1)}, bf16[4,4,512]{2,1,0:T(4,128)(2,1)}, u32[]{:S(2)}) copy-start(bf16[4,4,512]{2,1,0:T(4,128)(2,1)} %param.19) | copy-start | bytes 49156
  6.5 141.0 %all-gather.4.cloned.1.call-start = ((), (), s32[]{:S(2)}) async-start(), calls=%async_computation | async-start | bytes 6488064 | tf_op jit(solution)/shard_map/all_gather | solution.py:180
  7.3 211.2 %all-gather.6.cloned.1.call-start = ((), (), s32[]{:S(2)}) async-start(), calls=%async_computation.1 | async-start | bytes 6488064 | tf_op jit(solution)/shard_map/all_gather | solution.py:181
  8.0 311.4 %all-gather.8.cloned.1.call-start = ((), (), s32[]{:S(2)}) async-start(), calls=%async_computation.2 | async-start | bytes 6488064 | tf_op jit(solution)/shard_map/all_gather | solution.py:182
  8.7 64.8 %copy-start.8 = (bf16[4,4,64]{2,1,0:T(4,128)(2,1)S(1)}, bf16[4,4,64]{2,1,0:T(4,128)(2,1)}, u32[]{:S(2)}) copy-start(bf16[4,4,64]{2,1,0:T(4,128)(2,1)} %param.20) | copy-start | bytes 6148
  9.5 72.9 %copy-start.2 = (bf16[32,2048]{1,0:T(8,128)(2,1)S(1)}, bf16[32,2048]{1,0:T(8,128)(2,1)}, u32[]{:S(2)}) copy-start(bf16[32,2048]{1,0:T(8,128)(2,1)} %param.25) | copy-start | bytes 393220
  9.5 72.9 %copy-start.5 = (bf16[512,32]{0,1:T(8,128)(2,1)S(1)}, bf16[512,32]{0,1:T(8,128)(2,1)}, u32[]{:S(2)}) copy-start(bf16[512,32]{0,1:T(8,128)(2,1)} %param.24) | copy-start | bytes 98308
  12.3 120.2 %copy-start.3 = (s32[4,4,6]{2,1,0:T(4,128)S(1)}, s32[4,4,6]{2,1,0:T(4,128)}, u32[]{:S(2)}) copy-start(s32[4,4,6]{2,1,0:T(4,128)} %param.28) | copy-start | bytes 1156
  12.3 128.5 %copy-start.4 = (bf16[4,4,2048]{2,1,0:T(4,128)(2,1)S(1)}, bf16[4,4,2048]{2,1,0:T(4,128)(2,1)}, u32[]{:S(2)}) copy-start(bf16[4,4,2048]{2,1,0:T(4,128)(2,1)} %param.16) | copy-start | bytes 196612
  12.7 134.0 %copy-start.1 = (bf16[2048,64]{0,1:T(8,128)(2,1)S(1)}, bf16[2048,64]{0,1:T(8,128)(2,1)}, u32[]{:S(2)}) copy-start(bf16[2048,64]{0,1:T(8,128)(2,1)} %param.27) | copy-start | bytes 786436
  12.7 134.0 %copy-start.6 = (f32[2048]{0:T(1024)S(1)}, f32[2048]{0:T(1024)}, u32[]{:S(2)}) copy-start(f32[2048]{0:T(1024)} %param.26) | copy-start | bytes 24580
  14.3 8.5 %collective-permute-start = (f32[2,2,2,4,4,514]{5,4,3,2,1,0:T(4,128)S(1)}, f32[2,2,2,4,4,514]{5,4,3,2,1,0:T(4,128)S(1)}, u32[]{:S(2)}, u32[]{:S(2)}) collective-permute-start(f32[2,2,2,4,4,514]{5,4,3,2,1,0:T(4,128)S(1)} %pad_maximum_fusion), channel_id=1, source_target_pairs={{0,256},{8,264},{16,272},{24,280},{32,288},{40,296},{48,304},{56,3... | collective-permute-start | bytes 789512 | tf_op jit(solution)/shard_map/ppermute | solution.py:22
  24.0 14.6 %collective-permute-start.1 = (f32[2,2,4,4,514]{4,3,2,1,0:T(4,128)S(1)}, f32[2,2,4,4,514]{4,3,2,1,0:T(4,128)S(1)}, u32[]{:S(2)}, u32[]{:S(2)}) collective-permute-start(f32[2,2,4,4,514]{4,3,2,1,0:T(4,128)S(1)} %pad_maximum_fusion.1), channel_id=1, source_target_pairs={{0,32},{8,40},{16,48},{24,56},{32,0},{40,8},{48,16},{56,24},{64,96... | collective-permute-start | bytes 394760 | tf_op jit(solution)/shard_map/ppermute | solution.py:22
  39.6 10.7 %collective-permute-start.2 = (f32[2,4,4,514]{3,2,1,0:T(4,128)S(1)}, f32[2,4,4,514]{3,2,1,0:T(4,128)S(1)}, u32[]{:S(2)}, u32[]{:S(2)}) collective-permute-start(f32[2,4,4,514]{3,2,1,0:T(4,128)S(1)} %pad_maximum_fusion.2), channel_id=1, source_target_pairs={{0,64},{8,72},{16,80},{24,88},{32,96},{40,104},{48,112},{56,120},{... | collective-permute-start | bytes 197384 | tf_op jit(solution)/shard_map/ppermute | solution.py:22
  51.0 20.3 %collective-permute-start.3 = (f32[4,4,514]{2,1,0:T(4,128)S(1)}, f32[4,4,514]{2,1,0:T(4,128)S(1)}, u32[]{:S(2)}, u32[]{:S(2)}) collective-permute-start(f32[4,4,514]{2,1,0:T(4,128)S(1)} %pad_maximum_fusion.3), channel_id=1, source_target_pairs={{0,128},{8,136},{16,144},{24,152},{32,160},{40,168},{48,176},{56,1... | collective-permute-start | bytes 98696 | tf_op jit(solution)/shard_map/ppermute | solution.py:22
  71.6 5.1 %collective-permute-start.4 = (f32[4,4,514]{2,1,0:T(4,128)S(1)}, f32[4,4,514]{2,1,0:T(4,128)S(1)}, u32[]{:S(2)}, u32[]{:S(2)}) collective-permute-start(f32[4,4,514]{2,1,0:T(4,128)S(1)} %pad_maximum_fusion.4), channel_id=1, source_target_pairs={{0,16},{8,24},{16,0},{24,8},{32,48},{40,56},{48,32},{56,40},{64,80... | collective-permute-start | bytes 98696 | tf_op jit(solution)/shard_map/ppermute | solution.py:22
  77.1 4.9 %collective-permute-start.5 = (f32[4,4,514]{2,1,0:T(4,128)S(1)}, f32[4,4,514]{2,1,0:T(4,128)S(1)}, u32[]{:S(2)}, u32[]{:S(2)}) collective-permute-start(f32[4,4,514]{2,1,0:T(4,128)S(1)} %pad_maximum_fusion.5), channel_id=1, source_target_pairs={{0,8},{8,0},{16,24},{24,16},{32,40},{40,32},{48,56},{56,48},{64,72... | collective-permute-start | bytes 98696 | tf_op jit(solution)/shard_map/ppermute | solution.py:22
  82.7 3.2 collective-permute-start.6
  85.9 6.7 %collective-permute-start.7 = (f32[16,2048]{1,0:T(8,128)S(1)}, f32[16,2048]{1,0:T(8,128)S(1)}, u32[]{:S(2)}, u32[]{:S(2)}) collective-permute-start(f32[16,2048]{1,0:T(8,128)S(1)} %add.216), channel_id=1, source_target_pairs={{0,16},{8,24},{16,0},{24,8},{32,48},{40,56},{48,32},{56,40},{64,80... | collective-permute-start | bytes 393224 | tf_op jit(solution)/shard_map/ppermute | solution.py:22
  92.7 11.0 %collective-permute-start.8 = (f32[16,2048]{1,0:T(8,128)S(1)}, f32[16,2048]{1,0:T(8,128)S(1)}, u32[]{:S(2)}, u32[]{:S(2)}) collective-permute-start(f32[16,2048]{1,0:T(8,128)S(1)} %add.217), channel_id=1, source_target_pairs={{0,32},{8,40},{16,48},{24,56},{32,0},{40,8},{48,16},{56,24},{64,96... | collective-permute-start | bytes 393224 | tf_op jit(solution)/shard_map/ppermute | solution.py:22
  103.7 18.6 %collective-permute-start.9 = (f32[16,2048]{1,0:T(8,128)S(1)}, f32[16,2048]{1,0:T(8,128)S(1)}, u32[]{:S(2)}, u32[]{:S(2)}) collective-permute-start(f32[16,2048]{1,0:T(8,128)S(1)} %add.218), channel_id=1, source_target_pairs={{0,64},{8,72},{16,80},{24,88},{32,96},{40,104},{48,112},{56,120},{... | collective-permute-start | bytes 393224 | tf_op jit(solution)/shard_map/ppermute | solution.py:22
  122.3 15.2 %collective-permute-start.10 = (f32[16,2048]{1,0:T(8,128)S(1)}, f32[16,2048]{1,0:T(8,128)S(1)}, u32[]{:S(2)}, u32[]{:S(2)}) collective-permute-start(f32[16,2048]{1,0:T(8,128)S(1)} %add.219), channel_id=1, source_target_pairs={{0,128},{8,136},{16,144},{24,152},{32,160},{40,168},{48,176},{56,1... | collective-permute-start | bytes 393224 | tf_op jit(solution)/shard_map/ppermute | solution.py:22
  137.5 9.0 %collective-permute-start.11 = (f32[16,2048]{1,0:T(8,128)S(1)}, f32[16,2048]{1,0:T(8,128)S(1)}, u32[]{:S(2)}, u32[]{:S(2)}) collective-permute-start(f32[16,2048]{1,0:T(8,128)S(1)} %add.220), channel_id=1, source_target_pairs={{0,256},{8,264},{16,272},{24,280},{32,288},{40,296},{48,304},{56,3... | collective-permute-start | bytes 393224 | tf_op jit(solution)/shard_map/ppermute | solution.py:22
  326.8 4.3 %collective-permute-start.12 = (f32[16,2048]{1,0:T(8,128)S(1)}, f32[16,2048]{1,0:T(8,128)S(1)}, u32[]{:S(2)}, u32[]{:S(2)}) collective-permute-start(f32[16,2048]{1,0:T(8,128)S(1)} %fusion.116), channel_id=1, source_target_pairs={{0,8},{8,0},{16,24},{24,16},{32,40},{40,32},{48,56},{56,48},{64,72... | collective-permute-start | bytes 393224 | tf_op jit(solution)/shard_map/ppermute | solution.py:22
  331.1 6.6 %collective-permute-start.13 = (f32[16,2048]{1,0:T(8,128)S(1)}, f32[16,2048]{1,0:T(8,128)S(1)}, u32[]{:S(2)}, u32[]{:S(2)}) collective-permute-start(f32[16,2048]{1,0:T(8,128)S(1)} %add.226), channel_id=1, source_target_pairs={{0,16},{8,24},{16,0},{24,8},{32,48},{40,56},{48,32},{56,40},{64,80... | collective-permute-start | bytes 393224 | tf_op jit(solution)/shard_map/ppermute | solution.py:22
  337.7 10.0 %collective-permute-start.14 = (f32[16,2048]{1,0:T(8,128)S(1)}, f32[16,2048]{1,0:T(8,128)S(1)}, u32[]{:S(2)}, u32[]{:S(2)}) collective-permute-start(f32[16,2048]{1,0:T(8,128)S(1)} %add.227), channel_id=1, source_target_pairs={{0,32},{8,40},{16,48},{24,56},{32,0},{40,8},{48,16},{56,24},{64,96... | collective-permute-start | bytes 393224 | tf_op jit(solution)/shard_map/ppermute | solution.py:22
  347.8 18.0 %collective-permute-start.15 = (f32[16,2048]{1,0:T(8,128)S(1)}, f32[16,2048]{1,0:T(8,128)S(1)}, u32[]{:S(2)}, u32[]{:S(2)}) collective-permute-start(f32[16,2048]{1,0:T(8,128)S(1)} %add.228), channel_id=1, source_target_pairs={{0,64},{8,72},{16,80},{24,88},{32,96},{40,104},{48,112},{56,120},{... | collective-permute-start | bytes 393224 | tf_op jit(solution)/shard_map/ppermute | solution.py:22
  365.8 23.6 %collective-permute-start.16 = (f32[16,2048]{1,0:T(8,128)S(1)}, f32[16,2048]{1,0:T(8,128)S(1)}, u32[]{:S(2)}, u32[]{:S(2)}) collective-permute-start(f32[16,2048]{1,0:T(8,128)S(1)} %add.229), channel_id=1, source_target_pairs={{0,128},{8,136},{16,144},{24,152},{32,160},{40,168},{48,176},{56,1... | collective-permute-start | bytes 393224 | tf_op jit(solution)/shard_map/ppermute | solution.py:22
  389.5 5.7 %collective-permute-start.17 = (f32[16,2048]{1,0:T(8,128)S(1)}, f32[16,2048]{1,0:T(8,128)S(1)}, u32[]{:S(2)}, u32[]{:S(2)}) collective-permute-start(f32[16,2048]{1,0:T(8,128)S(1)} %add.230), channel_id=1, source_target_pairs={{0,256},{8,264},{16,272},{24,280},{32,288},{40,296},{48,304},{56,3... | collective-permute-start | bytes 393224 | tf_op jit(solution)/shard_map/ppermute | solution.py:22
Sparse Core Ops, SparseCore 0:
  10.5 104.4 all-gather.3
  118.2 100.2 all-gather.5
  221.7 97.7 all-gather.7

commit v3 on v1

--- a/solution.py
+++ b/solution.py
@@ -56,6 +56,26 @@
         send = lax.dynamic_index_in_dim(x, 1 - side, 0, keepdims=False)
         x = keep + exchange(send, axis, 1 << bit)
     return x
+
+
+def a2a_sum(x, axis):
+    count = lax.axis_size(axis)
+    rows, cols = x.shape
+    parts = x.reshape(rows, count, cols // count).transpose(1, 0, 2)
+    mine = lax.all_to_all(parts, axis, 0, 0, tiled=True).sum(axis=0)
+    spread = jnp.broadcast_to(mine[None], (count,) + mine.shape)
+    back = lax.all_to_all(spread, axis, 0, 0, tiled=True)
+    return back.transpose(1, 0, 2).reshape(rows, cols)
+
+
+def a2a_gather(x, axis):
+    count = lax.axis_size(axis)
+    spread = jnp.broadcast_to(x[None], (count,) + x.shape)
+    return lax.all_to_all(spread, axis, 0, 0, tiled=True)
+
+
+def a2a_scatter_sum(x, axis):
+    return lax.all_to_all(x, axis, 0, 0, tiled=True).sum(axis=0)
 
 
 def block_partial(query, query_rope, keys_lat, keys_rope, valid):
@@ -150,7 +170,7 @@
     lat_head = lat_out.reshape(token_rows, latent_dim)
     heads_out = jnp.dot(lat_head, w_uv, preferred_element_type=jnp.float32).astype(jnp.bfloat16)
     proj_part = jnp.dot(heads_out, w_out, preferred_element_type=jnp.float32)
-    projected = butterfly_sum(proj_part, "blk", range(blk_bits))
+    projected = a2a_sum(proj_part, "blk")
     width = hidden_in.shape[2]
     mixed = hidden_in.reshape(token_rows, width).astype(jnp.float32) + projected
     meansq = jnp.mean(mixed * mixed, axis=1, keepdims=True)
@@ -177,18 +197,17 @@
     dispatched = jnp.einsum(
         "esr,rd->esd", dispatch_map.astype(jnp.bfloat16), normed, preferred_element_type=jnp.float32
     ).astype(jnp.bfloat16)
-    gathered = butterfly_gather(dispatched, "exp", range(exp_bits))
+    gathered = a2a_gather(dispatched, "exp")
     groups = gathered.shape[0]
     piece = gathered.transpose(1, 0, 2, 3).reshape(local_count, groups * CAP, width)
     gate = jnp.einsum("erd,edf->erf", piece, w_gate, preferred_element_type=jnp.float32)
     upper = jnp.einsum("erd,edf->erf", piece, w_up, preferred_element_type=jnp.float32)
     hidden_all = (jax.nn.silu(gate) * upper).astype(jnp.bfloat16)
     partial_out = jnp.einsum("erf,efd->erd", hidden_all, w_down, preferred_element_type=jnp.float32)
-    split_out = partial_out.reshape((local_count,) + (2,) * exp_bits + (CAP, width))
-    split_out = jnp.moveaxis(split_out, 0, exp_bits)
-    expert_out = butterfly_scatter_sum(split_out, "exp", range(exp_bits - 1, -1, -1))
+    groups_out = partial_out.reshape(local_count, groups, CAP, width).transpose(1, 0, 2, 3)
+    expert_out = a2a_scatter_sum(groups_out, "exp")
     moe_part = jnp.einsum("esr,esd->rd", combine_map, expert_out, precision=lax.Precision.HIGHEST)
-    moe_all = butterfly_sum(moe_part, "blk", range(blk_bits))
+    moe_all = a2a_sum(moe_part, "blk")
     result = (mixed + moe_all).astype(jnp.bfloat16)
     return result.reshape(requests, new_steps, width)
 

time: 257 us -> 212 us (0.82)
  starting transfers between devices: 131 us -> 68.8 us
  blocking collectives: 0 us -> 46.5 us
  waiting for transfers between devices: 108 us -> 65.4 us
  local copies, waits for them, and re-layouts: 9.34 us -> 16.3 us
  other arithmetic: 3.25 us -> 7.91 us
    ppermute x24 -> x6, waiting for transfers between devices: 108 us -> 16.3 us  [exchange(): lax.ppermute(part, axis, xor_pairs(count, mask))]
    ppermute x24 -> x6, starting transfers between devices: 131 us -> 45.9 us  [exchange(): lax.ppermute(part, axis, xor_pairs(count, mask))]
    all_to_all x0 -> x3, waiting for transfers between devices: none -> 49 us  [the longest x2 32.8 us: a2a_sum(): back = lax.all_to_all(spread, axis, 0, 0, tiled=True)]
    all_to_all x0 -> x3, blocking collectives: none -> 46.5 us  [the longest x1 23.7 us: a2a_sum(): mine = lax.all_to_all(parts, axis, 0, 0, tiled=True).sum(axis=0)]
    all_to_all x0 -> x3, starting transfers between devices: none -> 22.9 us  [the longest x1 14 us: a2a_sum(): mine = lax.all_to_all(parts, axis, 0, 0, tiled=True).sum(axis=0)]
    unnamed x33 -> x39, local copies, waits for them, and re-layouts: 3.74 us -> 8.06 us
    all_to_all x0 -> x4, other arithmetic: none -> 3.8 us  [the longest x2 1.9 us: a2a_sum(): back = lax.all_to_all(spread, axis, 0, 0, tiled=True)]
  transfers between devices with their start and end apart: 24 -> 9, of which waited for: 24 -> 9; matrix products, arithmetic and copies ran while one was open for 1% -> 1% of each run, Pallas kernels for 0% -> 0%
where the time goes in v3:
time: 212 us; the launch traced here: 211 us
  starting transfers between devices  68.8 us (32%)
  waiting for transfers between devices  65.4 us (31%)
  blocking collectives  46.5 us (22%)
  local copies, waits for them, and re-layouts  16.3 us (8%)
  other arithmetic  7.91 us (4%)
  matrix products  5.5 us (3%)
    ppermute x6, starting transfers between devices, exchange(): lax.ppermute(part, axis, xor_pairs(count, mask))  45.9 us
    all_to_all x2, waiting for transfers between devices, a2a_sum(): back = lax.all_to_all(spread, axis, 0, 0, tiled=True)  32.8 us
    all_to_all x1, blocking collectives, a2a_sum(): mine = lax.all_to_all(parts, axis, 0, 0, tiled=True).sum(axis=0)  23.7 us
    ppermute x6, waiting for transfers between devices, exchange(): lax.ppermute(part, axis, xor_pairs(count, mask))  16.3 us
    all_to_all x1, waiting for transfers between devices, a2a_sum(): mine = lax.all_to_all(parts, axis, 0, 0, tiled=True).sum(axis=0)  16.3 us
    all_to_all x1, starting transfers between devices, a2a_sum(): mine = lax.all_to_all(parts, axis, 0, 0, tiled=True).sum(axis=0)  14 us
    all_to_all x1, blocking collectives, a2a_gather(): return lax.all_to_all(spread, axis, 0, 0, tiled=True)  13.1 us
    all_to_all x1, blocking collectives, a2a_scatter_sum(): return lax.all_to_all(x, axis, 0, 0, tiled=True).sum(axis=0)  9.69 us
  transfers between devices with their start and end apart: 9, of which 9 were waited for; matrix products, arithmetic and copies ran while one was open for 1% of the time, Pallas kernels for 0%

profile of v3, /device:TPU:1, one launch (start us, length us, event | category | flops | bytes accessed | tf_op | source)
XLA Modules:
  0.0 211.1 jit_solution(9546651763993478217)
XLA Ops:
  0.0 0.7 copy-done.11
  0.8 0.4 copy-done
  1.2 1.4 fusion.106
  2.7 0.3 fusion.104
  3.2 0.3 fusion.16
  3.9 0.3 copy.172
  4.2 0.3 copy.173
  4.5 0.3 copy.207
  5.0 4.0 %collective-permute-start = (f32[2,2,2,4,4,514]{5,4,3,2,1,0:T(4,128)S(1)}, f32[2,2,2,4,4,514]{5,4,3,2,1,0:T(4,128)S(1)}, u32[]{:S(2)}, u32[]{:S(2)}) collective-permute-start(f32[2,2,2,4,4,514]{5,4,3,2,1,0:T(4,128)S(1)} %pad_maximum_fusion), channel_id=1, source_target_pairs={{0,256},{8,264},{16,272},{24,280},{32,288},{40,296},{48,304},{56,3... | collective-permute-start | bytes 789512 | tf_op jit(solution)/shard_map/ppermute | solution.py:22
  9.1 0.9 constant_dynamic-slice_fusion.1
  10.0 3.5 %collective-permute-done = f32[2,2,2,4,4,514]{5,4,3,2,1,0:T(4,128)S(1)} collective-permute-done((f32[2,2,2,4,4,514]{5,4,3,2,1,0:T(4,128)S(1)}, f32[2,2,2,4,4,514]{5,4,3,2,1,0:T(4,128)S(1)}, u32[]{:S(2)}, u32[]{:S(2)}) %collective-permute-start) | collective-permute-done | bytes 263200 | tf_op jit(solution)/shard_map/ppermute | solution.py:22
  13.5 0.2 fusion.101
  13.7 0.3 copy.211
  14.1 0.2 copy.178
  14.3 0.2 copy.177
  14.8 7.7 %collective-permute-start.1 = (f32[2,2,4,4,514]{4,3,2,1,0:T(4,128)S(1)}, f32[2,2,4,4,514]{4,3,2,1,0:T(4,128)S(1)}, u32[]{:S(2)}, u32[]{:S(2)}) collective-permute-start(f32[2,2,4,4,514]{4,3,2,1,0:T(4,128)S(1)} %pad_maximum_fusion.1), channel_id=1, source_target_pairs={{0,32},{8,40},{16,48},{24,56},{32,0},{40,8},{48,16},{56,24},{64,96... | collective-permute-start | bytes 394760 | tf_op jit(solution)/shard_map/ppermute | solution.py:22
  22.7 6.7 %collective-permute-done.1 = f32[2,2,4,4,514]{4,3,2,1,0:T(4,128)S(1)} collective-permute-done((f32[2,2,4,4,514]{4,3,2,1,0:T(4,128)S(1)}, f32[2,2,4,4,514]{4,3,2,1,0:T(4,128)S(1)}, u32[]{:S(2)}, u32[]{:S(2)}) %collective-permute-start.1) | collective-permute-done | bytes 131616 | tf_op jit(solution)/shard_map/ppermute | solution.py:22
  30.3 8.8 %collective-permute-start.2 = (f32[2,4,4,514]{3,2,1,0:T(4,128)S(1)}, f32[2,4,4,514]{3,2,1,0:T(4,128)S(1)}, u32[]{:S(2)}, u32[]{:S(2)}) collective-permute-start(f32[2,4,4,514]{3,2,1,0:T(4,128)S(1)} %pad_maximum_fusion.2), channel_id=1, source_target_pairs={{0,64},{8,72},{16,80},{24,88},{32,96},{40,104},{48,112},{56,120},{... | collective-permute-start | bytes 197384 | tf_op jit(solution)/shard_map/ppermute | solution.py:22
  39.1 1.8 collective-permute-done.2
  41.7 19.0 %collective-permute-start.3 = (f32[4,4,514]{2,1,0:T(4,128)S(1)}, f32[4,4,514]{2,1,0:T(4,128)S(1)}, u32[]{:S(2)}, u32[]{:S(2)}) collective-permute-start(f32[4,4,514]{2,1,0:T(4,128)S(1)} %pad_maximum_fusion.3), channel_id=1, source_target_pairs={{0,128},{8,136},{16,144},{24,152},{32,160},{40,168},{48,176},{56,1... | collective-permute-start | bytes 98696 | tf_op jit(solution)/shard_map/ppermute | solution.py:22
  61.0 1.1 collective-permute-done.3
  62.5 1.9 collective-permute-start.4
  64.5 2.7 %collective-permute-done.4 = f32[4,4,514]{2,1,0:T(4,128)S(1)} collective-permute-done((f32[4,4,514]{2,1,0:T(4,128)S(1)}, f32[4,4,514]{2,1,0:T(4,128)S(1)}, u32[]{:S(2)}, u32[]{:S(2)}) %collective-permute-start.4) | collective-permute-done | bytes 32928 | tf_op jit(solution)/shard_map/ppermute | solution.py:22
  67.6 4.4 %collective-permute-start.5 = (f32[4,4,514]{2,1,0:T(4,128)S(1)}, f32[4,4,514]{2,1,0:T(4,128)S(1)}, u32[]{:S(2)}, u32[]{:S(2)}) collective-permute-start(f32[4,4,514]{2,1,0:T(4,128)S(1)} %pad_maximum_fusion.5), channel_id=1, source_target_pairs={{0,8},{8,0},{16,24},{24,16},{32,40},{40,32},{48,56},{56,48},{64,72... | collective-permute-start | bytes 98696 | tf_op jit(solution)/shard_map/ppermute | solution.py:22
  72.2 0.6 collective-permute-done.5
  73.2 0.7 copy-done.5
  74.0 0.3 fusion.8
  74.4 0.3 copy.192
  74.7 0.9 reshape.380
  75.6 14.0 %all-to-all-start = ((f32[64,1,512]{2,1,0:T(1,128)}), f32[64,1,512]{2,1,0:T(1,128)S(1)}, u32[]{:S(2)}, u32[]{:S(2)}) async-start(f32[64,1,512]{2,1,0:T(1,128)} %reshape.380), calls=%async_computation | async-start | bytes 262144 | tf_op jit(solution)/shard_map/all_to_all | solution.py:65
  89.8 0.6 copy-done.8
  90.5 16.3 %all-to-all-done = f32[64,1,512]{2,1,0:T(1,128)S(1)} async-done(((f32[64,1,512]{2,1,0:T(1,128)}), f32[64,1,512]{2,1,0:T(1,128)S(1)}, u32[]{:S(2)}, u32[]{:S(2)}) %all-to-all-start) | async-done | bytes 131104 | tf_op jit(solution)/shard_map/all_to_all | solution.py:65
  106.8 0.5 broadcast.209
  107.3 0.9 reduce.33
  108.5 0.9 reshape.382
  109.4 4.4 %all-to-all-start.1 = ((f32[64,1,512]{2,1,0:T(1,128)}), f32[64,1,512]{2,1,0:T(1,128)S(1)}, u32[]{:S(2)}, u32[]{:S(2)}) async-start(f32[64,1,512]{2,1,0:T(1,128)} %reshape.382), calls=%async_computation.1 | async-start | bytes 262144 | tf_op jit(solution)/shard_map/all_to_all | solution.py:67
  114.1 0.3 reduce_window_sum.11
  114.5 0.6 copy-done.9
  115.2 15.8 %all-to-all-done.1 = f32[64,1,512]{2,1,0:T(1,128)S(1)} async-done(((f32[64,1,512]{2,1,0:T(1,128)}), f32[64,1,512]{2,1,0:T(1,128)S(1)}, u32[]{:S(2)}, u32[]{:S(2)}) %all-to-all-start.1) | async-done | bytes 131104 | tf_op jit(solution)/shard_map/all_to_all | solution.py:67
  131.1 1.0 reduce.34
  132.4 0.3 multiply_reduce_fusion
  132.7 0.2 multiply_convert_fusion
  132.9 0.3 convert_element_type.111
  133.2 0.2 reshape.349
  133.5 0.7 copy-done.4
  134.2 0.2 fusion.5
  134.4 0.2 select_reduce_fusion
  134.9 13.1 %all_to_all.30 = bf16[8,1,3,2048]{3,2,1,0:T(4,128)(2,1)S(1)} all-to-all(bf16[8,1,3,2048]{3,2,1,0:T(4,128)(2,1)S(1)} %broadcast_in_dim.130), channel_id=1, replica_groups=mesh['blk'=64,'exp'=8] {'exp'}, dimensions={0} | all-to-all | bytes 196608 | tf_op jit(solution)/shard_map/all_to_all | solution.py:74
  148.1 0.3 fusion.11
  148.4 1.4 fusion.2
  149.8 0.2 convolution_bitcast_fusion
  150.3 9.7 %all_to_all.31 = f32[8,1,3,2048]{3,1,2,0:T(1,128)S(1)} all-to-all(f32[8,1,3,2048]{3,1,2,0:T(1,128)S(1)} %copy.198), channel_id=1, replica_groups=mesh['blk'=64,'exp'=8] {'exp'}, dimensions={0} | all-to-all | bytes 393216 | tf_op jit(solution)/shard_map/all_to_all | solution.py:78
  160.3 0.5 convolution_bitcast_fusion.1
  160.8 0.3 copy.200
  161.1 0.3 reshape.384
  161.4 23.7 %all_to_all.32 = f32[64,1,512]{2,1,0:T(1,128)S(1)} all-to-all(f32[64,1,512]{2,1,0:T(1,128)S(1)} %reshape.384), channel_id=1, replica_groups=mesh['blk'=64,'exp'=8] {'blk'}, dimensions={0} | all-to-all | bytes 262144 | tf_op jit(solution)/shard_map/all_to_all | solution.py:65
  185.1 1.0 reduce.35
  186.3 0.9 reshape.386
  187.2 4.4 %all-to-all-start.5 = ((f32[64,1,512]{2,1,0:T(1,128)}), f32[64,1,512]{2,1,0:T(1,128)S(1)}, u32[]{:S(2)}, u32[]{:S(2)}) async-start(f32[64,1,512]{2,1,0:T(1,128)} %reshape.386), calls=%async_computation.5 | async-start | bytes 262144 | tf_op jit(solution)/shard_map/all_to_all | solution.py:67
  191.7 0.3 reshape.348
  191.9 16.9 %all-to-all-done.5 = f32[64,1,512]{2,1,0:T(1,128)S(1)} async-done(((f32[64,1,512]{2,1,0:T(1,128)}), f32[64,1,512]{2,1,0:T(1,128)S(1)}, u32[]{:S(2)}, u32[]{:S(2)}) %all-to-all-start.5) | async-done | bytes 131104 | tf_op jit(solution)/shard_map/all_to_all | solution.py:67
  208.9 1.0 reduce.36
  210.2 0.3 reshape.355
  210.4 0.7 add_convert_fusion
  (114 shorter events, 7.7 us)
Async XLA Ops:
  0.0 1.2 copy-start
  0.0 0.7 copy-start.11
  1.2 1.4 copy-start.6
  1.2 1.4 copy-start.7
  5.0 8.5 %collective-permute-start = (f32[2,2,2,4,4,514]{5,4,3,2,1,0:T(4,128)S(1)}, f32[2,2,2,4,4,514]{5,4,3,2,1,0:T(4,128)S(1)}, u32[]{:S(2)}, u32[]{:S(2)}) collective-permute-start(f32[2,2,2,4,4,514]{5,4,3,2,1,0:T(4,128)S(1)} %pad_maximum_fusion), channel_id=1, source_target_pairs={{0,256},{8,264},{16,272},{24,280},{32,288},{40,296},{48,304},{56,3... | collective-permute-start | bytes 789512 | tf_op jit(solution)/shard_map/ppermute | solution.py:22
  14.7 7.8 %copy-start.12 = (bf16[4,4,512]{2,1,0:T(4,128)(2,1)S(1)}, bf16[4,4,512]{2,1,0:T(4,128)(2,1)}, u32[]{:S(2)}) copy-start(bf16[4,4,512]{2,1,0:T(4,128)(2,1)} %param.19) | copy-start | bytes 49156
  14.8 14.5 %collective-permute-start.1 = (f32[2,2,4,4,514]{4,3,2,1,0:T(4,128)S(1)}, f32[2,2,4,4,514]{4,3,2,1,0:T(4,128)S(1)}, u32[]{:S(2)}, u32[]{:S(2)}) collective-permute-start(f32[2,2,4,4,514]{4,3,2,1,0:T(4,128)S(1)} %pad_maximum_fusion.1), channel_id=1, source_target_pairs={{0,32},{8,40},{16,48},{24,56},{32,0},{40,8},{48,16},{56,24},{64,96... | collective-permute-start | bytes 394760 | tf_op jit(solution)/shard_map/ppermute | solution.py:22
  30.3 10.6 %collective-permute-start.2 = (f32[2,4,4,514]{3,2,1,0:T(4,128)S(1)}, f32[2,4,4,514]{3,2,1,0:T(4,128)S(1)}, u32[]{:S(2)}, u32[]{:S(2)}) collective-permute-start(f32[2,4,4,514]{3,2,1,0:T(4,128)S(1)} %pad_maximum_fusion.2), channel_id=1, source_target_pairs={{0,64},{8,72},{16,80},{24,88},{32,96},{40,104},{48,112},{56,120},{... | collective-permute-start | bytes 197384 | tf_op jit(solution)/shard_map/ppermute | solution.py:22
  41.7 20.4 %collective-permute-start.3 = (f32[4,4,514]{2,1,0:T(4,128)S(1)}, f32[4,4,514]{2,1,0:T(4,128)S(1)}, u32[]{:S(2)}, u32[]{:S(2)}) collective-permute-start(f32[4,4,514]{2,1,0:T(4,128)S(1)} %pad_maximum_fusion.3), channel_id=1, source_target_pairs={{0,128},{8,136},{16,144},{24,152},{32,160},{40,168},{48,176},{56,1... | collective-permute-start | bytes 98696 | tf_op jit(solution)/shard_map/ppermute | solution.py:22
  62.4 2.0 copy-start.13
  62.5 4.7 %collective-permute-start.4 = (f32[4,4,514]{2,1,0:T(4,128)S(1)}, f32[4,4,514]{2,1,0:T(4,128)S(1)}, u32[]{:S(2)}, u32[]{:S(2)}) collective-permute-start(f32[4,4,514]{2,1,0:T(4,128)S(1)} %pad_maximum_fusion.4), channel_id=1, source_target_pairs={{0,16},{8,24},{16,0},{24,8},{32,48},{40,56},{48,32},{56,40},{64,80... | collective-permute-start | bytes 98696 | tf_op jit(solution)/shard_map/ppermute | solution.py:22
  67.6 5.3 %collective-permute-start.5 = (f32[4,4,514]{2,1,0:T(4,128)S(1)}, f32[4,4,514]{2,1,0:T(4,128)S(1)}, u32[]{:S(2)}, u32[]{:S(2)}) collective-permute-start(f32[4,4,514]{2,1,0:T(4,128)S(1)} %pad_maximum_fusion.5), channel_id=1, source_target_pairs={{0,8},{8,0},{16,24},{24,16},{32,40},{40,32},{48,56},{56,48},{64,72... | collective-permute-start | bytes 98696 | tf_op jit(solution)/shard_map/ppermute | solution.py:22
  73.0 0.9 copy-start.5
  73.2 0.8 copy-start.10
  75.6 14.0 %copy-start.3 = (bf16[4,4,2048]{2,1,0:T(4,128)(2,1)S(1)}, bf16[4,4,2048]{2,1,0:T(4,128)(2,1)}, u32[]{:S(2)}) copy-start(bf16[4,4,2048]{2,1,0:T(4,128)(2,1)} %param.16) | copy-start | bytes 196612
  75.6 31.1 %all-to-all-start = ((f32[64,1,512]{2,1,0:T(1,128)}), f32[64,1,512]{2,1,0:T(1,128)S(1)}, u32[]{:S(2)}, u32[]{:S(2)}) async-start(f32[64,1,512]{2,1,0:T(1,128)} %reshape.380), calls=%async_computation | async-start | bytes 262144 | tf_op jit(solution)/shard_map/all_to_all | solution.py:65
  89.7 0.7 copy-start.8
  109.4 21.6 %all-to-all-start.1 = ((f32[64,1,512]{2,1,0:T(1,128)}), f32[64,1,512]{2,1,0:T(1,128)S(1)}, u32[]{:S(2)}, u32[]{:S(2)}) async-start(f32[64,1,512]{2,1,0:T(1,128)} %reshape.382), calls=%async_computation.1 | async-start | bytes 262144 | tf_op jit(solution)/shard_map/all_to_all | solution.py:67
  114.4 0.7 copy-start.9
  133.2 1.0 copy-start.4
  134.2 13.9 %copy-start.1 = (bf16[1,2048,176]{1,2,0:T(8,128)(2,1)S(1)}, bf16[1,2048,176]{1,2,0:T(8,128)(2,1)}, u32[]{:S(2)}) copy-start(bf16[1,2048,176]{1,2,0:T(8,128)(2,1)} %param.29) | copy-start | bytes 2162692
  148.1 1.8 copy-start.2
  187.2 21.6 %all-to-all-start.5 = ((f32[64,1,512]{2,1,0:T(1,128)}), f32[64,1,512]{2,1,0:T(1,128)S(1)}, u32[]{:S(2)}, u32[]{:S(2)}) async-start(f32[64,1,512]{2,1,0:T(1,128)} %reshape.386), calls=%async_computation.5 | async-start | bytes 262144 | tf_op jit(solution)/shard_map/all_to_all | solution.py:67

commit v4 on v3

--- a/solution.py
+++ b/solution.py
@@ -137,35 +137,34 @@
     )
     peak_val, weight_sum, summed = block_partial(query, query_rope, cache_lat, cache_rope, cache_valid)
     head_bits = head_count.bit_length() - 1
-    split = (2,) * head_bits
+    low_bits = blk_bits - head_bits
+    packed = jnp.concatenate([summed, peak_val[..., None], weight_sum[..., None]], axis=-1)
+    packed = packed.reshape(requests, new_steps, head_count, latent_dim + 2).transpose(2, 0, 1, 3)
+    packed = packed.reshape(head_count * requests, new_steps, latent_dim + 2)
+    got = lax.all_to_all(packed, "blk", 0, 0, tiled=True)
+    peaks = got[..., latent_dim]
+    totals = got[..., latent_dim + 1]
+    peak_all = jnp.max(peaks, axis=0)
+    factors = jnp.exp(peaks - peak_all[None])
     state = (
-        peak_val.reshape(requests, new_steps, head_count).transpose(2, 0, 1).reshape(split + (requests, new_steps)),
-        weight_sum.reshape(requests, new_steps, head_count).transpose(2, 0, 1).reshape(split + (requests, new_steps)),
-        summed.reshape(requests, new_steps, head_count, latent_dim)
-        .transpose(2, 0, 1, 3)
-        .reshape(split + (requests, new_steps, latent_dim)),
-    )
-    low_bits = blk_bits - head_bits
-    order = [head_bits - 1] + list(range(head_bits - 1))
-    remaining = list(range(head_bits - 1, -1, -1))
-    for head_bit in order:
-        axis_pos = remaining.index(head_bit)
-        remaining.pop(axis_pos)
-        bit = head_bit + low_bits
-        side = (me >> bit) & 1
-        keep = jax.tree.map(lambda part: lax.dynamic_index_in_dim(part, side, axis_pos, keepdims=False), state)
-        send = jax.tree.map(lambda part: lax.dynamic_index_in_dim(part, 1 - side, axis_pos, keepdims=False), state)
-        state = merge_pair(keep, exchange_state(send, "blk", 1 << bit))
-    for bit in range(low_bits - 1, -1, -1):
-        state = merge_pair(state, exchange_state(state, "blk", 1 << bit))
+        peak_all[None],
+        jnp.sum(factors * totals, axis=0)[None],
+        jnp.sum(factors[..., None] * got[..., :latent_dim], axis=0)[None],
+    )
     head_pick = me >> low_bits
-    own_query = lax.dynamic_index_in_dim(q_lat, head_pick, axis=2, keepdims=False)
-    own_rope = lax.dynamic_index_in_dim(q_rope, head_pick, axis=2, keepdims=False)
+    request_pick = me & ((1 << low_bits) - 1)
+    own_query = lax.dynamic_index_in_dim(q_lat, request_pick, axis=0, keepdims=True)
+    own_query = lax.dynamic_index_in_dim(own_query, head_pick, axis=2, keepdims=False)
+    own_rope = lax.dynamic_index_in_dim(q_rope, request_pick, axis=0, keepdims=True)
+    own_rope = lax.dynamic_index_in_dim(own_rope, head_pick, axis=2, keepdims=False)
+    own_lat = lax.dynamic_index_in_dim(new_lat, request_pick, axis=0, keepdims=True)
+    own_new_rope = lax.dynamic_index_in_dim(new_rope, request_pick, axis=0, keepdims=True)
     fresh_valid = lax.iota(jnp.int32, new_steps)[None, :] <= lax.iota(jnp.int32, new_steps)[:, None]
-    fresh_valid = jnp.broadcast_to(fresh_valid[None, :, :], (requests, new_steps, new_steps))
-    fresh_part = block_partial(own_query, own_rope, new_lat, new_rope, fresh_valid)
+    fresh_valid = fresh_valid[None, :, :]
+    fresh_part = block_partial(own_query, own_rope, own_lat, own_new_rope, fresh_valid)
     peak_val, weight_sum, summed = merge_pair(state, fresh_part)
-    lat_out = (summed / weight_sum[:, :, None]).astype(jnp.bfloat16)
+    own_out = (summed / weight_sum[:, :, None]).astype(jnp.bfloat16)
+    lat_out = butterfly_gather(own_out[0], "blk", range(low_bits))
     token_rows = requests * new_steps
     lat_head = lat_out.reshape(token_rows, latent_dim)
     heads_out = jnp.dot(lat_head, w_uv, preferred_element_type=jnp.float32).astype(jnp.bfloat16)

time: 212 us -> 201 us (0.948)
  starting transfers between devices: 68.8 us -> 40.7 us
  waiting for transfers between devices: 65.4 us -> 85.5 us
  local copies, waits for them, and re-layouts: 16.3 us -> 13.3 us
    ppermute x6 -> x2, starting transfers between devices: 45.9 us -> 6.91 us  [exchange(): lax.ppermute(part, axis, xor_pairs(count, mask))]
    all_to_all x0 -> x1, waiting for transfers between devices: none -> 34.3 us  [local(): got = lax.all_to_all(packed, 'blk', 0, 0, tiled=True)]
    all_to_all x0 -> x1, starting transfers between devices: none -> 18.1 us  [local(): got = lax.all_to_all(packed, 'blk', 0, 0, tiled=True)]
    ppermute x6 -> x2, waiting for transfers between devices: 16.3 us -> 2.15 us  [exchange(): lax.ppermute(part, axis, xor_pairs(count, mask))]
    all_to_all x1, starting transfers between devices: 14 us -> 6.71 us  [a2a_sum(): mine = lax.all_to_all(parts, axis, 0, 0, tiled=True).sum(axis=0)]
    unnamed x39 -> x35, local copies, waits for them, and re-layouts: 8.06 us -> 7.48 us
  transfers between devices with their start and end apart: 9 -> 6, of which waited for: 9 -> 6; matrix products, arithmetic and copies ran while one was open for 1% -> 1% of each run, Pallas kernels for 0% -> 0%
where the time goes in v4:
time: 201 us
  waiting for transfers between devices  85.5 us (43%)
  blocking collectives  46.5 us (23%)
  starting transfers between devices  40.7 us (20%)
  local copies, waits for them, and re-layouts  13.3 us (7%)
  other arithmetic  8.01 us (4%)
  matrix products  6.14 us (3%)
    all_to_all x1, waiting for transfers between devices, local(): got = lax.all_to_all(packed, 'blk', 0, 0, tiled=True)  34.3 us
    all_to_all x2, waiting for transfers between devices, a2a_sum(): back = lax.all_to_all(spread, axis, 0, 0, tiled=True)  32.8 us
    all_to_all x1, blocking collectives, a2a_sum(): mine = lax.all_to_all(parts, axis, 0, 0, tiled=True).sum(axis=0)  23.7 us
    all_to_all x1, starting transfers between devices, local(): got = lax.all_to_all(packed, 'blk', 0, 0, tiled=True)  18.1 us
    all_to_all x1, waiting for transfers between devices, a2a_sum(): mine = lax.all_to_all(parts, axis, 0, 0, tiled=True).sum(axis=0)  16.3 us
    all_to_all x1, blocking collectives, a2a_gather(): return lax.all_to_all(spread, axis, 0, 0, tiled=True)  13.1 us
    all_to_all x1, blocking collectives, a2a_scatter_sum(): return lax.all_to_all(x, axis, 0, 0, tiled=True).sum(axis=0)  9.69 us
    all_to_all x2, starting transfers between devices, a2a_sum(): back = lax.all_to_all(spread, axis, 0, 0, tiled=True)  8.89 us
  transfers between devices with their start and end apart: 6, of which 6 were waited for; matrix products, arithmetic and copies ran while one was open for 1% of the time, Pallas kernels for 0%

profile of v4, /device:TPU:1, one launch (start us, length us, event | category | flops | bytes accessed | tf_op | source)
XLA Modules:
  0.0 200.5 jit_solution(13257297015653758)
XLA Ops:
  0.0 0.7 copy-done.11
  0.8 0.4 copy-done
  1.2 1.4 fusion.63
  2.7 0.3 fusion.61
  3.0 0.2 fusion.18
  3.2 0.3 fusion.20
  3.7 0.2 copy.103
  3.8 0.2 copy.104
  4.0 0.3 copy.102
  4.4 1.0 pad_maximum_fusion
  5.4 18.1 %all-to-all-start = ((f32[64,4,514]{2,1,0:T(4,128)}), f32[64,4,514]{2,1,0:T(4,128)S(1)}, u32[]{:S(2)}, u32[]{:S(2)}) async-start(f32[64,4,514]{2,1,0:T(4,128)} %bitcast.4), calls=%async_computation | async-start | bytes 1310720 | tf_op jit(solution)/shard_map/all_to_all | solution.py:144
  23.6 0.8 constant_dynamic-slice_fusion.1
  24.5 0.8 fusion.62
  25.4 34.3 %all-to-all-done = f32[64,4,514]{2,1,0:T(4,128)S(1)} async-done(((f32[64,4,514]{2,1,0:T(4,128)}), f32[64,4,514]{2,1,0:T(4,128)S(1)}, u32[]{:S(2)}, u32[]{:S(2)}) %all-to-all-start) | async-done | bytes 526368 | tf_op jit(solution)/shard_map/all_to_all | solution.py:144
  59.6 0.2 fusion.60
  60.1 0.2 fusion.38
  60.5 0.2 fusion.17
  60.6 0.2 fusion.9
  60.8 1.9 collective-permute-start
  62.8 1.1 collective-permute-done
  63.9 5.0 %collective-permute-start.1 = (bf16[2,4,512]{2,1,0:T(4,128)(2,1)S(1)}, bf16[2,4,512]{2,1,0:T(4,128)(2,1)S(1)}, u32[]{:S(2)}, u32[]{:S(2)}) collective-permute-start(bf16[2,4,512]{2,1,0:T(4,128)(2,1)S(1)} %pad_maximum_fusion.2), channel_id=1, source_target_pairs={{0,16},{8,24},{16,0},{24,8},{32,48},{40,56},{48,32},{56,40},{64,80... | collective-permute-start | bytes 24584 | tf_op jit(solution)/shard_map/ppermute | solution.py:22
  68.9 1.0 collective-permute-done.1
  70.0 0.7 copy-done.10
  70.7 0.3 fusion.10
  71.0 0.2 reshape.383
  71.2 0.3 copy.110
  71.5 0.9 reshape.404
  72.4 6.7 %all-to-all-start.1 = ((f32[64,1,512]{2,1,0:T(1,128)}), f32[64,1,512]{2,1,0:T(1,128)S(1)}, u32[]{:S(2)}, u32[]{:S(2)}) async-start(f32[64,1,512]{2,1,0:T(1,128)} %reshape.404), calls=%async_computation.1 | async-start | bytes 262144 | tf_op jit(solution)/shard_map/all_to_all | solution.py:65
  79.3 0.6 copy-done.7
  79.9 16.3 %all-to-all-done.1 = f32[64,1,512]{2,1,0:T(1,128)S(1)} async-done(((f32[64,1,512]{2,1,0:T(1,128)}), f32[64,1,512]{2,1,0:T(1,128)S(1)}, u32[]{:S(2)}, u32[]{:S(2)}) %all-to-all-start.1) | async-done | bytes 131104 | tf_op jit(solution)/shard_map/all_to_all | solution.py:65
  96.2 0.5 broadcast.211
  96.7 0.9 reduce.14
  98.0 0.9 reshape.406
  98.8 4.4 %all-to-all-start.2 = ((f32[64,1,512]{2,1,0:T(1,128)}), f32[64,1,512]{2,1,0:T(1,128)S(1)}, u32[]{:S(2)}, u32[]{:S(2)}) async-start(f32[64,1,512]{2,1,0:T(1,128)} %reshape.406), calls=%async_computation.2 | async-start | bytes 262144 | tf_op jit(solution)/shard_map/all_to_all | solution.py:67
  103.5 0.3 reduce_window_sum.11
  104.0 0.6 copy-done.9
  104.7 15.8 %all-to-all-done.2 = f32[64,1,512]{2,1,0:T(1,128)S(1)} async-done(((f32[64,1,512]{2,1,0:T(1,128)}), f32[64,1,512]{2,1,0:T(1,128)S(1)}, u32[]{:S(2)}, u32[]{:S(2)}) %all-to-all-start.2) | async-done | bytes 131104 | tf_op jit(solution)/shard_map/all_to_all | solution.py:67
  120.5 1.0 reduce.15
  121.6 0.2 copy.147
  121.8 0.3 multiply_reduce_fusion
  122.1 0.2 multiply_convert_fusion
  122.3 0.3 convert_element_type.116
  122.6 0.2 reshape.385
  122.9 0.7 copy-done.4
  123.6 0.2 fusion.7
  123.8 0.2 select_reduce_fusion
  124.3 13.1 %all_to_all.35 = bf16[8,1,3,2048]{3,2,1,0:T(4,128)(2,1)S(1)} all-to-all(bf16[8,1,3,2048]{3,2,1,0:T(4,128)(2,1)S(1)} %broadcast_in_dim.42), channel_id=1, replica_groups=mesh['blk'=64,'exp'=8] {'exp'}, dimensions={0} | all-to-all | bytes 196608 | tf_op jit(solution)/shard_map/all_to_all | solution.py:74
  137.5 0.3 fusion.15
  137.8 1.4 fusion.2
  139.2 0.2 convolution_bitcast_fusion
  139.5 0.2 copy.116
  139.7 9.7 %all_to_all.36 = f32[8,1,3,2048]{3,1,2,0:T(1,128)S(1)} all-to-all(f32[8,1,3,2048]{3,1,2,0:T(1,128)S(1)} %copy.116), channel_id=1, replica_groups=mesh['blk'=64,'exp'=8] {'exp'}, dimensions={0} | all-to-all | bytes 393216 | tf_op jit(solution)/shard_map/all_to_all | solution.py:78
  149.7 0.5 convolution_bitcast_fusion.1
  150.2 0.3 copy.118
  150.5 0.3 reshape.408
  150.8 23.7 %all_to_all.37 = f32[64,1,512]{2,1,0:T(1,128)S(1)} all-to-all(f32[64,1,512]{2,1,0:T(1,128)S(1)} %reshape.408), channel_id=1, replica_groups=mesh['blk'=64,'exp'=8] {'blk'}, dimensions={0} | all-to-all | bytes 262144 | tf_op jit(solution)/shard_map/all_to_all | solution.py:65
  174.5 1.0 reduce.16
  175.7 0.9 reshape.410
  176.6 4.4 %all-to-all-start.6 = ((f32[64,1,512]{2,1,0:T(1,128)}), f32[64,1,512]{2,1,0:T(1,128)S(1)}, u32[]{:S(2)}, u32[]{:S(2)}) async-start(f32[64,1,512]{2,1,0:T(1,128)} %reshape.410), calls=%async_computation.6 | async-start | bytes 262144 | tf_op jit(solution)/shard_map/all_to_all | solution.py:67
  181.1 0.3 reshape.384
  181.3 16.9 %all-to-all-done.6 = f32[64,1,512]{2,1,0:T(1,128)S(1)} async-done(((f32[64,1,512]{2,1,0:T(1,128)}), f32[64,1,512]{2,1,0:T(1,128)S(1)}, u32[]{:S(2)}, u32[]{:S(2)}) %all-to-all-start.6) | async-done | bytes 131104 | tf_op jit(solution)/shard_map/all_to_all | solution.py:67
  198.3 1.0 reduce.17
  199.6 0.3 reshape.391
  199.9 0.7 add_convert_fusion
  (67 shorter events, 3.3 us)
Async XLA Ops:
  0.0 1.2 copy-start
  0.0 0.7 copy-start.11
  1.2 1.4 copy-start.6
  1.2 1.4 copy-start.8
  5.4 54.2 %all-to-all-start = ((f32[64,4,514]{2,1,0:T(4,128)}), f32[64,4,514]{2,1,0:T(4,128)S(1)}, u32[]{:S(2)}, u32[]{:S(2)}) async-start(f32[64,4,514]{2,1,0:T(4,128)} %bitcast.4), calls=%async_computation | async-start | bytes 1310720 | tf_op jit(solution)/shard_map/all_to_all | solution.py:144
  23.6 0.8 copy-start.12
  60.6 9.4 %copy-start.5 = (bf16[32,2048]{1,0:T(8,128)(2,1)S(1)}, bf16[32,2048]{1,0:T(8,128)(2,1)}, u32[]{:S(2)}) copy-start(bf16[32,2048]{1,0:T(8,128)(2,1)} %param.25) | copy-start | bytes 393220
  60.8 3.1 %collective-permute-start = (bf16[1,4,512]{2,1,0:T(4,128)(2,1)S(1)}, bf16[1,4,512]{2,1,0:T(4,128)(2,1)S(1)}, u32[]{:S(2)}, u32[]{:S(2)}) collective-permute-start(bf16[1,4,512]{2,1,0:T(4,128)(2,1)S(1)} %fusion.9), channel_id=1, source_target_pairs={{0,8},{8,0},{16,24},{24,16},{32,40},{40,32},{48,56},{56,48},{64,72... | collective-permute-start | bytes 12296 | tf_op jit(solution)/shard_map/ppermute | solution.py:22
  63.9 6.0 %collective-permute-start.1 = (bf16[2,4,512]{2,1,0:T(4,128)(2,1)S(1)}, bf16[2,4,512]{2,1,0:T(4,128)(2,1)S(1)}, u32[]{:S(2)}, u32[]{:S(2)}) collective-permute-start(bf16[2,4,512]{2,1,0:T(4,128)(2,1)S(1)} %pad_maximum_fusion.2), channel_id=1, source_target_pairs={{0,16},{8,24},{16,0},{24,8},{32,48},{40,56},{48,32},{56,40},{64,80... | collective-permute-start | bytes 24584 | tf_op jit(solution)/shard_map/ppermute | solution.py:22
  70.0 0.8 copy-start.10
  72.4 6.7 %copy-start.3 = (bf16[4,4,2048]{2,1,0:T(4,128)(2,1)S(1)}, bf16[4,4,2048]{2,1,0:T(4,128)(2,1)}, u32[]{:S(2)}) copy-start(bf16[4,4,2048]{2,1,0:T(4,128)(2,1)} %param.16) | copy-start | bytes 196612
  72.4 23.8 %all-to-all-start.1 = ((f32[64,1,512]{2,1,0:T(1,128)}), f32[64,1,512]{2,1,0:T(1,128)S(1)}, u32[]{:S(2)}, u32[]{:S(2)}) async-start(f32[64,1,512]{2,1,0:T(1,128)} %reshape.404), calls=%async_computation.1 | async-start | bytes 262144 | tf_op jit(solution)/shard_map/all_to_all | solution.py:65
  79.1 0.7 copy-start.7
  98.8 21.6 %all-to-all-start.2 = ((f32[64,1,512]{2,1,0:T(1,128)}), f32[64,1,512]{2,1,0:T(1,128)S(1)}, u32[]{:S(2)}, u32[]{:S(2)}) async-start(f32[64,1,512]{2,1,0:T(1,128)} %reshape.406), calls=%async_computation.2 | async-start | bytes 262144 | tf_op jit(solution)/shard_map/all_to_all | solution.py:67
  103.9 0.7 copy-start.9
  122.6 1.0 copy-start.4
  123.6 13.9 %copy-start.1 = (bf16[1,2048,176]{1,2,0:T(8,128)(2,1)S(1)}, bf16[1,2048,176]{1,2,0:T(8,128)(2,1)}, u32[]{:S(2)}) copy-start(bf16[1,2048,176]{1,2,0:T(8,128)(2,1)} %param.29) | copy-start | bytes 2162692
  137.5 1.8 copy-start.2
  176.6 21.7 %all-to-all-start.6 = ((f32[64,1,512]{2,1,0:T(1,128)}), f32[64,1,512]{2,1,0:T(1,128)S(1)}, u32[]{:S(2)}, u32[]{:S(2)}) async-start(f32[64,1,512]{2,1,0:T(1,128)} %reshape.410), calls=%async_computation.6 | async-start | bytes 262144 | tf_op jit(solution)/shard_map/all_to_all | solution.py:67

commit v5 on v4

--- a/solution.py
+++ b/solution.py
@@ -61,8 +61,8 @@
 def a2a_sum(x, axis):
     count = lax.axis_size(axis)
     rows, cols = x.shape
-    parts = x.reshape(rows, count, cols // count).transpose(1, 0, 2)
-    mine = lax.all_to_all(parts, axis, 0, 0, tiled=True).sum(axis=0)
+    parts = x.reshape(rows, count, cols // count).transpose(1, 0, 2).astype(jnp.bfloat16)
+    mine = lax.all_to_all(parts, axis, 0, 0, tiled=True).astype(jnp.float32).sum(axis=0)
     spread = jnp.broadcast_to(mine[None], (count,) + mine.shape)
     back = lax.all_to_all(spread, axis, 0, 0, tiled=True)
     return back.transpose(1, 0, 2).reshape(rows, cols)
@@ -75,7 +75,8 @@
 
 
 def a2a_scatter_sum(x, axis):
-    return lax.all_to_all(x, axis, 0, 0, tiled=True).sum(axis=0)
+    got = lax.all_to_all(x.astype(jnp.bfloat16), axis, 0, 0, tiled=True)
+    return got.astype(jnp.float32).sum(axis=0)
 
 
 def block_partial(query, query_rope, keys_lat, keys_rope, valid):
@@ -138,18 +139,19 @@
     peak_val, weight_sum, summed = block_partial(query, query_rope, cache_lat, cache_rope, cache_valid)
     head_bits = head_count.bit_length() - 1
     low_bits = blk_bits - head_bits
-    packed = jnp.concatenate([summed, peak_val[..., None], weight_sum[..., None]], axis=-1)
-    packed = packed.reshape(requests, new_steps, head_count, latent_dim + 2).transpose(2, 0, 1, 3)
-    packed = packed.reshape(head_count * requests, new_steps, latent_dim + 2)
-    got = lax.all_to_all(packed, "blk", 0, 0, tiled=True)
-    peaks = got[..., latent_dim]
-    totals = got[..., latent_dim + 1]
+    stats = jnp.stack([peak_val, weight_sum], axis=-1)
+    stats = stats.reshape(requests, new_steps, head_count, 2).transpose(2, 0, 1, 3)
+    stats = lax.all_to_all(stats.reshape(head_count * requests, new_steps, 2), "blk", 0, 0, tiled=True)
+    sums = summed.astype(jnp.bfloat16).reshape(requests, new_steps, head_count, latent_dim).transpose(2, 0, 1, 3)
+    sums = lax.all_to_all(sums.reshape(head_count * requests, new_steps, latent_dim), "blk", 0, 0, tiled=True)
+    peaks = stats[..., 0]
+    totals = stats[..., 1]
     peak_all = jnp.max(peaks, axis=0)
     factors = jnp.exp(peaks - peak_all[None])
     state = (
         peak_all[None],
         jnp.sum(factors * totals, axis=0)[None],
-        jnp.sum(factors[..., None] * got[..., :latent_dim], axis=0)[None],
+        jnp.sum(factors[..., None] * sums.astype(jnp.float32), axis=0)[None],
     )
     head_pick = me >> low_bits
     request_pick = me & ((1 << low_bits) - 1)

time: 201 us -> 194 us (0.965)
  other arithmetic: 8.01 us -> 4.96 us
  blocking collectives: 46.5 us -> 43.6 us
  waiting for transfers between devices: 85.5 us -> 82.7 us
    all_to_all x2 -> x3, waiting for transfers between devices: 50.6 us -> 47.1 us  [the longest x1 20.9 us: local(): lax.all_to_all(sums.reshape(head_count * requests, new_steps, latent_dim)...]
    all_to_all x2 -> x3, starting transfers between devices: 24.9 us -> 28.1 us  [the longest x1 18.2 us: local(): lax.all_to_all(stats.reshape(head_count * requests, new_steps, 2), 'blk',...]
    all_to_all x2, blocking collectives: 33.4 us -> 30.5 us  [the longest x1 21.2 us: a2a_sum(): lax.all_to_all(parts, axis, 0, 0, tiled=True).astype(jnp.float32)]
    ppermute x2, starting transfers between devices: 6.91 us -> 4.66 us  [exchange(): lax.ppermute(part, axis, xor_pairs(count, mask))]
  transfers between devices with their start and end apart: 6 -> 7, of which waited for: 6 -> 7; matrix products, arithmetic and copies ran while one was open for 1% -> 2% of each run, Pallas kernels for 0% -> 0%
where the time goes in v5:
time: 194 us
  waiting for transfers between devices  82.7 us (43%)
  blocking collectives  43.6 us (22%)
  starting transfers between devices  41.6 us (21%)
  local copies, waits for them, and re-layouts  14.1 us (7%)
  matrix products  6.14 us (3%)
  other arithmetic  4.96 us (3%)
    all_to_all x2, waiting for transfers between devices, a2a_sum(): back = lax.all_to_all(spread, axis, 0, 0, tiled=True)  32.8 us
    all_to_all x1, blocking collectives, a2a_sum(): lax.all_to_all(parts, axis, 0, 0, tiled=True).astype(jnp.float32)  21.2 us
    all_to_all x1, waiting for transfers between devices, local(): lax.all_to_all(sums.reshape(head_count * requests, new_steps, latent_dim)...  20.9 us
    all_to_all x1, starting transfers between devices, local(): lax.all_to_all(stats.reshape(head_count * requests, new_steps, 2), 'blk',...  18.2 us
    all_to_all x1, waiting for transfers between devices, a2a_sum(): lax.all_to_all(parts, axis, 0, 0, tiled=True).astype(jnp.float32)  13.9 us
    all_to_all x1, blocking collectives, a2a_gather(): return lax.all_to_all(spread, axis, 0, 0, tiled=True)  13.1 us
    all_to_all x1, waiting for transfers between devices, local(): lax.all_to_all(stats.reshape(head_count * requests, new_steps, 2), 'blk',...  12.4 us
    all_to_all x1, blocking collectives, a2a_scatter_sum(): got = lax.all_to_all(x.astype(jnp.bfloat16), axis, 0, 0, tiled=True)  9.33 us
  transfers between devices with their start and end apart: 7, of which 7 were waited for; matrix products, arithmetic and copies ran while one was open for 2% of the time, Pallas kernels for 0%

profile of v5, /device:TPU:1, one launch (start us, length us, event | category | flops | bytes accessed | tf_op | source)
XLA Modules:
  0.0 193.6 jit_solution(14760975209018817501)
XLA Ops:
  0.0 0.7 copy-done.11
  0.8 0.4 copy-done
  1.2 1.4 fusion.62
  2.7 0.3 fusion.60
  3.0 0.2 fusion.19
  3.3 0.8 copy.95
  4.1 18.2 %all-to-all-start = ((f32[64,4,2]{1,2,0:T(2,128)}), f32[64,4,2]{1,2,0:T(2,128)S(1)}, u32[]{:S(2)}, u32[]{:S(2)}) async-start(f32[64,4,2]{1,2,0:T(2,128)} %bitcast.4), calls=%async_computation | async-start | bytes 131072 | tf_op jit(solution)/shard_map/all_to_all | solution.py:144
  22.2 0.3 convolution_convert_fusion.3
  22.6 0.8 constant_dynamic-slice_fusion.1
  23.5 0.9 copy.80
  24.4 12.4 %all-to-all-done = f32[64,4,2]{1,2,0:T(2,128)S(1)} async-done(((f32[64,4,2]{1,2,0:T(2,128)}), f32[64,4,2]{1,2,0:T(2,128)S(1)}, u32[]{:S(2)}, u32[]{:S(2)}) %all-to-all-start) | async-done | bytes 2080 | tf_op jit(solution)/shard_map/all_to_all | solution.py:144
  36.8 4.4 %all-to-all-start.1 = ((bf16[64,4,512]{2,1,0:T(4,128)(2,1)}), bf16[64,4,512]{2,1,0:T(4,128)(2,1)S(1)}, u32[]{:S(2)}, u32[]{:S(2)}) async-start(bf16[64,4,512]{2,1,0:T(4,128)(2,1)} %bitcast.10), calls=%async_computation.1 | async-start | bytes 524288 | tf_op jit(solution)/shard_map/all_to_all | solution.py:146
  41.3 0.8 fusion.61
  42.5 0.2 fusion.37
  42.7 20.9 %all-to-all-done.1 = bf16[64,4,512]{2,1,0:T(4,128)(2,1)S(1)} async-done(((bf16[64,4,512]{2,1,0:T(4,128)(2,1)}), bf16[64,4,512]{2,1,0:T(4,128)(2,1)S(1)}, u32[]{:S(2)}, u32[]{:S(2)}) %all-to-all-start.1) | async-done | bytes 262176 | tf_op jit(solution)/shard_map/all_to_all | solution.py:146
  63.6 0.2 multiply_reduce_fusion.1
  63.8 0.2 fusion.11
  64.0 1.9 %collective-permute-start = (bf16[1,4,512]{2,1,0:T(4,128)(2,1)S(1)}, bf16[1,4,512]{2,1,0:T(4,128)(2,1)S(1)}, u32[]{:S(2)}, u32[]{:S(2)}) collective-permute-start(bf16[1,4,512]{2,1,0:T(4,128)(2,1)S(1)} %fusion.11), channel_id=1, source_target_pairs={{0,8},{8,0},{16,24},{24,16},{32,40},{40,32},{48,56},{56,48},{64,72... | collective-permute-start | bytes 12296 | tf_op jit(solution)/shard_map/ppermute | solution.py:22
  65.9 1.1 collective-permute-done
  67.1 2.7 %collective-permute-start.1 = (bf16[2,4,512]{2,1,0:T(4,128)(2,1)S(1)}, bf16[2,4,512]{2,1,0:T(4,128)(2,1)S(1)}, u32[]{:S(2)}, u32[]{:S(2)}) collective-permute-start(bf16[2,4,512]{2,1,0:T(4,128)(2,1)S(1)} %pad_maximum_fusion.1), channel_id=1, source_target_pairs={{0,16},{8,24},{16,0},{24,8},{32,48},{40,56},{48,32},{56,40},{64,80... | collective-permute-start | bytes 24584 | tf_op jit(solution)/shard_map/ppermute | solution.py:22
  69.8 1.7 collective-permute-done.1
  71.6 0.7 copy-done.10
  72.3 0.3 convolution_convert_fusion.1
  72.6 0.2 convert_element_type.144
  72.8 0.2 copy.82
  72.9 0.8 reshape.405
  73.8 5.5 %all-to-all-start.2 = ((bf16[64,2,256]{2,1,0:T(2,128)(2,1)}), bf16[64,2,256]{2,1,0:T(2,128)(2,1)S(1)}, u32[]{:S(2)}, u32[]{:S(2)}) async-start(bf16[64,2,256]{2,1,0:T(2,128)(2,1)} %reshape.405), calls=%async_computation.2 | async-start | bytes 131072 | tf_op jit(solution)/shard_map/all_to_all | solution.py:65
  79.5 0.6 copy-done.7
  80.1 13.9 %all-to-all-done.2 = bf16[64,2,256]{2,1,0:T(2,128)(2,1)S(1)} async-done(((bf16[64,2,256]{2,1,0:T(2,128)(2,1)}), bf16[64,2,256]{2,1,0:T(2,128)(2,1)S(1)}, u32[]{:S(2)}, u32[]{:S(2)}) %all-to-all-start.2) | async-done | bytes 65568 | tf_op jit(solution)/shard_map/all_to_all | solution.py:65
  94.0 0.2 reshape.406
  94.3 0.9 reshape.407
  95.2 4.4 %all-to-all-start.3 = ((f32[64,1,512]{2,1,0:T(1,128)}), f32[64,1,512]{2,1,0:T(1,128)S(1)}, u32[]{:S(2)}, u32[]{:S(2)}) async-start(f32[64,1,512]{2,1,0:T(1,128)} %reshape.407), calls=%async_computation.3 | async-start | bytes 262144 | tf_op jit(solution)/shard_map/all_to_all | solution.py:67
  99.8 0.3 reduce_window_sum.11
  100.3 0.6 copy-done.9
  101.0 15.8 %all-to-all-done.3 = f32[64,1,512]{2,1,0:T(1,128)S(1)} async-done(((f32[64,1,512]{2,1,0:T(1,128)}), f32[64,1,512]{2,1,0:T(1,128)S(1)}, u32[]{:S(2)}, u32[]{:S(2)}) %all-to-all-start.3) | async-done | bytes 131104 | tf_op jit(solution)/shard_map/all_to_all | solution.py:67
  116.8 0.5 broadcast.211
  117.3 0.9 reduce.14
  118.5 0.2 copy.121
  118.6 0.3 multiply_reduce_fusion
  118.9 0.2 multiply_convert_fusion
  119.2 0.3 convert_element_type.158
  119.5 0.2 reshape.387
  119.7 0.7 copy-done.4
  120.4 0.2 fusion.9
  120.6 0.2 select_reduce_fusion
  121.1 13.1 %all_to_all.40 = bf16[8,1,3,2048]{3,2,1,0:T(4,128)(2,1)S(1)} all-to-all(bf16[8,1,3,2048]{3,2,1,0:T(4,128)(2,1)S(1)} %broadcast_in_dim.42), channel_id=1, replica_groups=mesh['blk'=64,'exp'=8] {'exp'}, dimensions={0} | all-to-all | bytes 196608 | tf_op jit(solution)/shard_map/all_to_all | solution.py:74
  134.3 0.3 fusion.16
  134.6 1.4 fusion.4
  136.1 0.2 fusion
  136.4 9.3 %all_to_all.41 = bf16[8,1,3,2048]{3,2,1,0:T(4,128)(2,1)S(1)} all-to-all(bf16[8,1,3,2048]{3,2,1,0:T(4,128)(2,1)S(1)} %copy.88), channel_id=1, replica_groups=mesh['blk'=64,'exp'=8] {'exp'}, dimensions={0} | all-to-all | bytes 196608 | tf_op jit(solution)/shard_map/all_to_all | solution.py:78
  146.0 0.5 fusion.3
  146.4 0.3 copy.90
  146.7 0.2 reshape.409
  146.9 21.2 %all_to_all.42 = bf16[64,2,256]{2,1,0:T(2,128)(2,1)S(1)} all-to-all(bf16[64,2,256]{2,1,0:T(2,128)(2,1)S(1)} %reshape.409), channel_id=1, replica_groups=mesh['blk'=64,'exp'=8] {'blk'}, dimensions={0} | all-to-all | bytes 131072 | tf_op jit(solution)/shard_map/all_to_all | solution.py:65
  168.1 0.2 reshape.410
  168.3 0.3 copy.91
  168.8 0.9 reshape.411
  169.7 4.4 %all-to-all-start.7 = ((f32[64,1,512]{2,1,0:T(1,128)}), f32[64,1,512]{2,1,0:T(1,128)S(1)}, u32[]{:S(2)}, u32[]{:S(2)}) async-start(f32[64,1,512]{2,1,0:T(1,128)} %reshape.411), calls=%async_computation.7 | async-start | bytes 262144 | tf_op jit(solution)/shard_map/all_to_all | solution.py:67
  174.1 0.3 reshape.386
  174.4 16.9 %all-to-all-done.7 = f32[64,1,512]{2,1,0:T(1,128)S(1)} async-done(((f32[64,1,512]{2,1,0:T(1,128)}), f32[64,1,512]{2,1,0:T(1,128)S(1)}, u32[]{:S(2)}, u32[]{:S(2)}) %all-to-all-start.7) | async-done | bytes 131104 | tf_op jit(solution)/shard_map/all_to_all | solution.py:67
  191.3 1.0 reduce.15
  192.4 0.2 copy.94
  192.6 0.3 reshape.392
  192.9 0.7 add_convert_fusion
  (67 shorter events, 2.9 us)
Async XLA Ops:
  0.0 1.2 copy-start
  0.0 0.7 copy-start.11
  1.2 1.4 copy-start.6
  1.2 1.4 copy-start.8
  4.1 32.7 %all-to-all-start = ((f32[64,4,2]{1,2,0:T(2,128)}), f32[64,4,2]{1,2,0:T(2,128)S(1)}, u32[]{:S(2)}, u32[]{:S(2)}) async-start(f32[64,4,2]{1,2,0:T(2,128)} %bitcast.4), calls=%async_computation | async-start | bytes 131072 | tf_op jit(solution)/shard_map/all_to_all | solution.py:144
  22.6 0.8 copy-start.12
  36.8 26.8 %all-to-all-start.1 = ((bf16[64,4,512]{2,1,0:T(4,128)(2,1)}), bf16[64,4,512]{2,1,0:T(4,128)(2,1)S(1)}, u32[]{:S(2)}, u32[]{:S(2)}) async-start(bf16[64,4,512]{2,1,0:T(4,128)(2,1)} %bitcast.10), calls=%async_computation.1 | async-start | bytes 524288 | tf_op jit(solution)/shard_map/all_to_all | solution.py:146
  63.8 7.8 %copy-start.5 = (bf16[32,2048]{1,0:T(8,128)(2,1)S(1)}, bf16[32,2048]{1,0:T(8,128)(2,1)}, u32[]{:S(2)}) copy-start(bf16[32,2048]{1,0:T(8,128)(2,1)} %param.25) | copy-start | bytes 393220
  64.0 3.1 %collective-permute-start = (bf16[1,4,512]{2,1,0:T(4,128)(2,1)S(1)}, bf16[1,4,512]{2,1,0:T(4,128)(2,1)S(1)}, u32[]{:S(2)}, u32[]{:S(2)}) collective-permute-start(bf16[1,4,512]{2,1,0:T(4,128)(2,1)S(1)} %fusion.11), channel_id=1, source_target_pairs={{0,8},{8,0},{16,24},{24,16},{32,40},{40,32},{48,56},{56,48},{64,72... | collective-permute-start | bytes 12296 | tf_op jit(solution)/shard_map/ppermute | solution.py:22
  67.1 4.4 %collective-permute-start.1 = (bf16[2,4,512]{2,1,0:T(4,128)(2,1)S(1)}, bf16[2,4,512]{2,1,0:T(4,128)(2,1)S(1)}, u32[]{:S(2)}, u32[]{:S(2)}) collective-permute-start(bf16[2,4,512]{2,1,0:T(4,128)(2,1)S(1)} %pad_maximum_fusion.1), channel_id=1, source_target_pairs={{0,16},{8,24},{16,0},{24,8},{32,48},{40,56},{48,32},{56,40},{64,80... | collective-permute-start | bytes 24584 | tf_op jit(solution)/shard_map/ppermute | solution.py:22
  71.5 0.8 copy-start.10
  73.8 5.5 %copy-start.3 = (bf16[4,4,2048]{2,1,0:T(4,128)(2,1)S(1)}, bf16[4,4,2048]{2,1,0:T(4,128)(2,1)}, u32[]{:S(2)}) copy-start(bf16[4,4,2048]{2,1,0:T(4,128)(2,1)} %param.16) | copy-start | bytes 196612
  73.8 20.2 %all-to-all-start.2 = ((bf16[64,2,256]{2,1,0:T(2,128)(2,1)}), bf16[64,2,256]{2,1,0:T(2,128)(2,1)S(1)}, u32[]{:S(2)}, u32[]{:S(2)}) async-start(bf16[64,2,256]{2,1,0:T(2,128)(2,1)} %reshape.405), calls=%async_computation.2 | async-start | bytes 131072 | tf_op jit(solution)/shard_map/all_to_all | solution.py:65
  79.3 0.7 copy-start.7
  95.2 21.6 %all-to-all-start.3 = ((f32[64,1,512]{2,1,0:T(1,128)}), f32[64,1,512]{2,1,0:T(1,128)S(1)}, u32[]{:S(2)}, u32[]{:S(2)}) async-start(f32[64,1,512]{2,1,0:T(1,128)} %reshape.407), calls=%async_computation.3 | async-start | bytes 262144 | tf_op jit(solution)/shard_map/all_to_all | solution.py:67
  100.2 0.7 copy-start.9
  119.5 1.0 copy-start.4
  120.4 13.9 %copy-start.1 = (bf16[1,2048,176]{1,2,0:T(8,128)(2,1)S(1)}, bf16[1,2048,176]{1,2,0:T(8,128)(2,1)}, u32[]{:S(2)}) copy-start(bf16[1,2048,176]{1,2,0:T(8,128)(2,1)} %param.29) | copy-start | bytes 2162692
  134.3 1.8 copy-start.2
  169.7 21.6 %all-to-all-start.7 = ((f32[64,1,512]{2,1,0:T(1,128)}), f32[64,1,512]{2,1,0:T(1,128)S(1)}, u32[]{:S(2)}, u32[]{:S(2)}) async-start(f32[64,1,512]{2,1,0:T(1,128)} %reshape.411), calls=%async_computation.7 | async-start | bytes 262144 | tf_op jit(solution)/shard_map/all_to_all | solution.py:67

commit v6 on v4

--- a/solution.py
+++ b/solution.py
@@ -61,8 +61,8 @@
 def a2a_sum(x, axis):
     count = lax.axis_size(axis)
     rows, cols = x.shape
-    parts = x.reshape(rows, count, cols // count).transpose(1, 0, 2)
-    mine = lax.all_to_all(parts, axis, 0, 0, tiled=True).sum(axis=0)
+    parts = x.reshape(rows, count, cols // count).transpose(1, 0, 2).astype(jnp.bfloat16)
+    mine = lax.all_to_all(parts, axis, 0, 0, tiled=True).astype(jnp.float32).sum(axis=0)
     spread = jnp.broadcast_to(mine[None], (count,) + mine.shape)
     back = lax.all_to_all(spread, axis, 0, 0, tiled=True)
     return back.transpose(1, 0, 2).reshape(rows, cols)
@@ -75,7 +75,8 @@
 
 
 def a2a_scatter_sum(x, axis):
-    return lax.all_to_all(x, axis, 0, 0, tiled=True).sum(axis=0)
+    got = lax.all_to_all(x.astype(jnp.bfloat16), axis, 0, 0, tiled=True)
+    return got.astype(jnp.float32).sum(axis=0)
 
 
 def block_partial(query, query_rope, keys_lat, keys_rope, valid):

time: 201 us -> 194 us (0.965)
  blocking collectives: 46.5 us -> 43.4 us
  waiting for transfers between devices: 85.5 us -> 83 us
    all_to_all x2, blocking collectives: 33.4 us -> 30.4 us  [the longest x1 21 us: a2a_sum(): lax.all_to_all(parts, axis, 0, 0, tiled=True).astype(jnp.float32)]
    all_to_all x1, waiting for transfers between devices: 16.3 us -> 13.8 us  [a2a_sum(): lax.all_to_all(parts, axis, 0, 0, tiled=True).astype(jnp.float32)]
  transfers between devices with their start and end apart: 6 -> 6, of which waited for: 6 -> 6; matrix products, arithmetic and copies ran while one was open for 1% -> 2% of each run, Pallas kernels for 0% -> 0%
where the time goes in v6:
time: 194 us; the launch traced here: 193 us
  waiting for transfers between devices  83 us (43%)
  blocking collectives  43.4 us (22%)
  starting transfers between devices  40.7 us (21%)
  local copies, waits for them, and re-layouts  13.2 us (7%)
  matrix products  6.14 us (3%)
  other arithmetic  6.07 us (3%)
    all_to_all x1, waiting for transfers between devices, local(): got = lax.all_to_all(packed, 'blk', 0, 0, tiled=True)  34.3 us
    all_to_all x2, waiting for transfers between devices, a2a_sum(): back = lax.all_to_all(spread, axis, 0, 0, tiled=True)  32.8 us
    all_to_all x1, blocking collectives, a2a_sum(): lax.all_to_all(parts, axis, 0, 0, tiled=True).astype(jnp.float32)  21 us
    all_to_all x1, starting transfers between devices, local(): got = lax.all_to_all(packed, 'blk', 0, 0, tiled=True)  18.1 us
    all_to_all x1, waiting for transfers between devices, a2a_sum(): lax.all_to_all(parts, axis, 0, 0, tiled=True).astype(jnp.float32)  13.8 us
    all_to_all x1, blocking collectives, a2a_gather(): return lax.all_to_all(spread, axis, 0, 0, tiled=True)  13.1 us
    all_to_all x1, blocking collectives, a2a_scatter_sum(): got = lax.all_to_all(x.astype(jnp.bfloat16), axis, 0, 0, tiled=True)  9.33 us
    all_to_all x2, starting transfers between devices, a2a_sum(): back = lax.all_to_all(spread, axis, 0, 0, tiled=True)  8.89 us
  transfers between devices with their start and end apart: 6, of which 6 were waited for; matrix products, arithmetic and copies ran while one was open for 2% of the time, Pallas kernels for 0%

profile of v6, /device:TPU:1, one launch (start us, length us, event | category | flops | bytes accessed | tf_op | source)
XLA Modules:
  0.0 192.9 jit_solution(9271414680182264881)
XLA Ops:
  0.0 0.7 copy-done.11
  0.8 0.4 copy-done
  1.2 1.4 fusion.64
  2.7 0.3 fusion.62
  3.0 0.2 fusion.19
  3.2 0.3 fusion.21
  3.7 0.2 copy.104
  3.8 0.2 copy.105
  4.0 0.3 copy.103
  4.4 1.0 pad_maximum_fusion
  5.4 18.1 %all-to-all-start = ((f32[64,4,514]{2,1,0:T(4,128)}), f32[64,4,514]{2,1,0:T(4,128)S(1)}, u32[]{:S(2)}, u32[]{:S(2)}) async-start(f32[64,4,514]{2,1,0:T(4,128)} %bitcast.4), calls=%async_computation | async-start | bytes 1310720 | tf_op jit(solution)/shard_map/all_to_all | solution.py:145
  23.6 0.8 constant_dynamic-slice_fusion.1
  24.5 0.8 fusion.63
  25.4 34.3 %all-to-all-done = f32[64,4,514]{2,1,0:T(4,128)S(1)} async-done(((f32[64,4,514]{2,1,0:T(4,128)}), f32[64,4,514]{2,1,0:T(4,128)S(1)}, u32[]{:S(2)}, u32[]{:S(2)}) %all-to-all-start) | async-done | bytes 526368 | tf_op jit(solution)/shard_map/all_to_all | solution.py:145
  59.6 0.2 fusion.61
  60.1 0.2 fusion.39
  60.5 0.2 fusion.18
  60.6 0.2 fusion.11
  60.8 1.9 %collective-permute-start = (bf16[1,4,512]{2,1,0:T(4,128)(2,1)S(1)}, bf16[1,4,512]{2,1,0:T(4,128)(2,1)S(1)}, u32[]{:S(2)}, u32[]{:S(2)}) collective-permute-start(bf16[1,4,512]{2,1,0:T(4,128)(2,1)S(1)} %fusion.11), channel_id=1, source_target_pairs={{0,8},{8,0},{16,24},{24,16},{32,40},{40,32},{48,56},{56,48},{64,72... | collective-permute-start | bytes 12296 | tf_op jit(solution)/shard_map/ppermute | solution.py:22
  62.8 1.1 collective-permute-done
  63.9 5.0 %collective-permute-start.1 = (bf16[2,4,512]{2,1,0:T(4,128)(2,1)S(1)}, bf16[2,4,512]{2,1,0:T(4,128)(2,1)S(1)}, u32[]{:S(2)}, u32[]{:S(2)}) collective-permute-start(bf16[2,4,512]{2,1,0:T(4,128)(2,1)S(1)} %pad_maximum_fusion.2), channel_id=1, source_target_pairs={{0,16},{8,24},{16,0},{24,8},{32,48},{40,56},{48,32},{56,40},{64,80... | collective-permute-start | bytes 24584 | tf_op jit(solution)/shard_map/ppermute | solution.py:22
  68.9 1.0 collective-permute-done.1
  70.0 0.7 copy-done.10
  70.7 0.3 convolution_convert_fusion.1
  71.0 0.2 convert_element_type.136
  71.2 0.2 copy.111
  71.4 0.8 reshape.398
  72.2 6.7 %all-to-all-start.1 = ((bf16[64,2,256]{2,1,0:T(2,128)(2,1)}), bf16[64,2,256]{2,1,0:T(2,128)(2,1)S(1)}, u32[]{:S(2)}, u32[]{:S(2)}) async-start(bf16[64,2,256]{2,1,0:T(2,128)(2,1)} %reshape.398), calls=%async_computation.1 | async-start | bytes 131072 | tf_op jit(solution)/shard_map/all_to_all | solution.py:65
  79.1 0.6 copy-done.7
  79.7 13.8 %all-to-all-done.1 = bf16[64,2,256]{2,1,0:T(2,128)(2,1)S(1)} async-done(((bf16[64,2,256]{2,1,0:T(2,128)(2,1)}), bf16[64,2,256]{2,1,0:T(2,128)(2,1)S(1)}, u32[]{:S(2)}, u32[]{:S(2)}) %all-to-all-start.1) | async-done | bytes 65568 | tf_op jit(solution)/shard_map/all_to_all | solution.py:65
  93.5 0.2 reshape.399
  93.8 0.9 reshape.400
  94.7 4.4 %all-to-all-start.2 = ((f32[64,1,512]{2,1,0:T(1,128)}), f32[64,1,512]{2,1,0:T(1,128)S(1)}, u32[]{:S(2)}, u32[]{:S(2)}) async-start(f32[64,1,512]{2,1,0:T(1,128)} %reshape.400), calls=%async_computation.2 | async-start | bytes 262144 | tf_op jit(solution)/shard_map/all_to_all | solution.py:67
  99.3 0.3 reduce_window_sum.11
  99.8 0.6 copy-done.9
  100.5 15.8 %all-to-all-done.2 = f32[64,1,512]{2,1,0:T(1,128)S(1)} async-done(((f32[64,1,512]{2,1,0:T(1,128)}), f32[64,1,512]{2,1,0:T(1,128)S(1)}, u32[]{:S(2)}, u32[]{:S(2)}) %all-to-all-start.2) | async-done | bytes 131104 | tf_op jit(solution)/shard_map/all_to_all | solution.py:67
  116.3 0.5 broadcast.211
  116.9 0.9 reduce.14
  118.0 0.2 copy.149
  118.2 0.3 multiply_reduce_fusion
  118.5 0.2 multiply_convert_fusion
  118.7 0.3 convert_element_type.150
  119.0 0.2 reshape.380
  119.2 0.7 copy-done.4
  119.9 0.2 fusion.9
  120.2 0.2 select_reduce_fusion
  120.6 13.1 %all_to_all.35 = bf16[8,1,3,2048]{3,2,1,0:T(4,128)(2,1)S(1)} all-to-all(bf16[8,1,3,2048]{3,2,1,0:T(4,128)(2,1)S(1)} %broadcast_in_dim.42), channel_id=1, replica_groups=mesh['blk'=64,'exp'=8] {'exp'}, dimensions={0} | all-to-all | bytes 196608 | tf_op jit(solution)/shard_map/all_to_all | solution.py:74
  133.8 0.3 fusion.16
  134.1 1.4 fusion.4
  135.6 0.2 fusion
  135.9 9.3 %all_to_all.36 = bf16[8,1,3,2048]{3,2,1,0:T(4,128)(2,1)S(1)} all-to-all(bf16[8,1,3,2048]{3,2,1,0:T(4,128)(2,1)S(1)} %copy.117), channel_id=1, replica_groups=mesh['blk'=64,'exp'=8] {'exp'}, dimensions={0} | all-to-all | bytes 196608 | tf_op jit(solution)/shard_map/all_to_all | solution.py:78
  145.5 0.5 fusion.3
  146.0 0.3 copy.119
  146.4 21.0 %all_to_all.37 = bf16[64,2,256]{2,1,0:T(2,128)(2,1)S(1)} all-to-all(bf16[64,2,256]{2,1,0:T(2,128)(2,1)S(1)} %reshape.402), channel_id=1, replica_groups=mesh['blk'=64,'exp'=8] {'blk'}, dimensions={0} | all-to-all | bytes 131072 | tf_op jit(solution)/shard_map/all_to_all | solution.py:65
  167.5 0.2 reshape.403
  167.7 0.3 copy.120
  168.1 0.9 reshape.404
  169.0 4.4 %all-to-all-start.6 = ((f32[64,1,512]{2,1,0:T(1,128)}), f32[64,1,512]{2,1,0:T(1,128)S(1)}, u32[]{:S(2)}, u32[]{:S(2)}) async-start(f32[64,1,512]{2,1,0:T(1,128)} %reshape.404), calls=%async_computation.6 | async-start | bytes 262144 | tf_op jit(solution)/shard_map/all_to_all | solution.py:67
  173.5 0.3 reshape.379
  173.7 16.9 %all-to-all-done.6 = f32[64,1,512]{2,1,0:T(1,128)S(1)} async-done(((f32[64,1,512]{2,1,0:T(1,128)}), f32[64,1,512]{2,1,0:T(1,128)S(1)}, u32[]{:S(2)}, u32[]{:S(2)}) %all-to-all-start.6) | async-done | bytes 131104 | tf_op jit(solution)/shard_map/all_to_all | solution.py:67
  190.7 1.0 reduce.15
  191.8 0.2 copy.123
  192.0 0.3 reshape.385
  192.2 0.7 add_convert_fusion
  (66 shorter events, 3.1 us)
Async XLA Ops:
  0.0 1.2 copy-start
  0.0 0.7 copy-start.11
  1.2 1.4 copy-start.6
  1.2 1.4 copy-start.8
  5.4 54.2 %all-to-all-start = ((f32[64,4,514]{2,1,0:T(4,128)}), f32[64,4,514]{2,1,0:T(4,128)S(1)}, u32[]{:S(2)}, u32[]{:S(2)}) async-start(f32[64,4,514]{2,1,0:T(4,128)} %bitcast.4), calls=%async_computation | async-start | bytes 1310720 | tf_op jit(solution)/shard_map/all_to_all | solution.py:145
  23.6 0.8 copy-start.12
  60.6 9.4 %copy-start.5 = (bf16[32,2048]{1,0:T(8,128)(2,1)S(1)}, bf16[32,2048]{1,0:T(8,128)(2,1)}, u32[]{:S(2)}) copy-start(bf16[32,2048]{1,0:T(8,128)(2,1)} %param.25) | copy-start | bytes 393220
  60.8 3.1 %collective-permute-start = (bf16[1,4,512]{2,1,0:T(4,128)(2,1)S(1)}, bf16[1,4,512]{2,1,0:T(4,128)(2,1)S(1)}, u32[]{:S(2)}, u32[]{:S(2)}) collective-permute-start(bf16[1,4,512]{2,1,0:T(4,128)(2,1)S(1)} %fusion.11), channel_id=1, source_target_pairs={{0,8},{8,0},{16,24},{24,16},{32,40},{40,32},{48,56},{56,48},{64,72... | collective-permute-start | bytes 12296 | tf_op jit(solution)/shard_map/ppermute | solution.py:22
  63.9 6.0 %collective-permute-start.1 = (bf16[2,4,512]{2,1,0:T(4,128)(2,1)S(1)}, bf16[2,4,512]{2,1,0:T(4,128)(2,1)S(1)}, u32[]{:S(2)}, u32[]{:S(2)}) collective-permute-start(bf16[2,4,512]{2,1,0:T(4,128)(2,1)S(1)} %pad_maximum_fusion.2), channel_id=1, source_target_pairs={{0,16},{8,24},{16,0},{24,8},{32,48},{40,56},{48,32},{56,40},{64,80... | collective-permute-start | bytes 24584 | tf_op jit(solution)/shard_map/ppermute | solution.py:22
  70.0 0.8 copy-start.10
  72.2 6.7 %copy-start.3 = (bf16[4,4,2048]{2,1,0:T(4,128)(2,1)S(1)}, bf16[4,4,2048]{2,1,0:T(4,128)(2,1)}, u32[]{:S(2)}) copy-start(bf16[4,4,2048]{2,1,0:T(4,128)(2,1)} %param.16) | copy-start | bytes 196612
  72.2 21.3 %all-to-all-start.1 = ((bf16[64,2,256]{2,1,0:T(2,128)(2,1)}), bf16[64,2,256]{2,1,0:T(2,128)(2,1)S(1)}, u32[]{:S(2)}, u32[]{:S(2)}) async-start(bf16[64,2,256]{2,1,0:T(2,128)(2,1)} %reshape.398), calls=%async_computation.1 | async-start | bytes 131072 | tf_op jit(solution)/shard_map/all_to_all | solution.py:65
  79.0 0.7 copy-start.7
  94.7 21.6 %all-to-all-start.2 = ((f32[64,1,512]{2,1,0:T(1,128)}), f32[64,1,512]{2,1,0:T(1,128)S(1)}, u32[]{:S(2)}, u32[]{:S(2)}) async-start(f32[64,1,512]{2,1,0:T(1,128)} %reshape.400), calls=%async_computation.2 | async-start | bytes 262144 | tf_op jit(solution)/shard_map/all_to_all | solution.py:67
  99.7 0.7 copy-start.9
  119.0 1.0 copy-start.4
  119.9 13.9 %copy-start.1 = (bf16[1,2048,176]{1,2,0:T(8,128)(2,1)S(1)}, bf16[1,2048,176]{1,2,0:T(8,128)(2,1)}, u32[]{:S(2)}) copy-start(bf16[1,2048,176]{1,2,0:T(8,128)(2,1)} %param.29) | copy-start | bytes 2162692
  133.8 1.8 copy-start.2
  169.0 21.6 %all-to-all-start.6 = ((f32[64,1,512]{2,1,0:T(1,128)}), f32[64,1,512]{2,1,0:T(1,128)S(1)}, u32[]{:S(2)}, u32[]{:S(2)}) async-start(f32[64,1,512]{2,1,0:T(1,128)} %reshape.404), calls=%async_computation.6 | async-start | bytes 262144 | tf_op jit(solution)/shard_map/all_to_all | solution.py:67

commit v7 on v6

--- a/solution.py
+++ b/solution.py
@@ -142,7 +142,8 @@
     packed = jnp.concatenate([summed, peak_val[..., None], weight_sum[..., None]], axis=-1)
     packed = packed.reshape(requests, new_steps, head_count, latent_dim + 2).transpose(2, 0, 1, 3)
     packed = packed.reshape(head_count * requests, new_steps, latent_dim + 2)
-    got = lax.all_to_all(packed, "blk", 0, 0, tiled=True)
+    flat = packed.reshape(head_count * requests, new_steps * (latent_dim + 2))
+    got = lax.all_to_all(flat, "blk", 0, 0, tiled=True).reshape(packed.shape)
     peaks = got[..., latent_dim]
     totals = got[..., latent_dim + 1]
     peak_all = jnp.max(peaks, axis=0)
@@ -207,8 +208,13 @@
     groups_out = partial_out.reshape(local_count, groups, CAP, width).transpose(1, 0, 2, 3)
     expert_out = a2a_scatter_sum(groups_out, "exp")
     moe_part = jnp.einsum("esr,esd->rd", combine_map, expert_out, precision=lax.Precision.HIGHEST)
-    moe_all = a2a_sum(moe_part, "blk")
-    result = (mixed + moe_all).astype(jnp.bfloat16)
+    count = lax.axis_size("blk")
+    cols = width // count
+    parts = moe_part.reshape(token_rows, count, cols).transpose(1, 0, 2).astype(jnp.bfloat16)
+    moe_block = lax.all_to_all(parts, "blk", 0, 0, tiled=True).astype(jnp.float32).sum(axis=0)
+    mixed_block = lax.dynamic_slice_in_dim(mixed, me * cols, cols, axis=1)
+    result_block = (mixed_block + moe_block).astype(jnp.bfloat16)
+    result = a2a_gather(result_block, "blk").transpose(1, 0, 2).reshape(token_rows, width)
     return result.reshape(requests, new_steps, width)
 
 

time: 194 us -> 188 us (0.969)
  waiting for transfers between devices: 83 us -> 77.6 us
  local copies, waits for them, and re-layouts: 13.2 us -> 16 us
  blocking collectives: 43.4 us -> 40.9 us
    all_to_all x1 -> x0, blocking collectives: 21 us -> none  [a2a_sum(): lax.all_to_all(parts, axis, 0, 0, tiled=True).astype(jnp.float32)]
    all_to_all x1 -> x2, blocking collectives: 13.1 us -> 31.5 us  [a2a_gather(): return lax.all_to_all(spread, axis, 0, 0, tiled=True)]
    all_to_all x2 -> x1, waiting for transfers between devices: 32.8 us -> 15.8 us  [a2a_sum(): back = lax.all_to_all(spread, axis, 0, 0, tiled=True)]
    all_to_all x1 -> x2, waiting for transfers between devices: 34.3 us -> 45.8 us  [the longest x1 31.2 us: local(): got = lax.all_to_all(flat, 'blk', 0, 0, tiled=True).reshape(packed.shape)]
    all_to_all x1 -> x2, starting transfers between devices: 18.1 us -> 25.3 us  [the longest x1 18.2 us: local(): got = lax.all_to_all(flat, 'blk', 0, 0, tiled=True).reshape(packed.shape)]
    all_to_all x2 -> x1, starting transfers between devices: 8.89 us -> 4.44 us  [a2a_sum(): back = lax.all_to_all(spread, axis, 0, 0, tiled=True)]
    unnamed x35 -> x37, local copies, waits for them, and re-layouts: 7.37 us -> 7.69 us
  transfers between devices with their start and end apart: 6 -> 6, of which waited for: 6 -> 6; matrix products, arithmetic and copies ran while one was open for 2% -> 1% of each run, Pallas kernels for 0% -> 0%
where the time goes in v7:
time: 188 us; the launch traced here: 187 us
  waiting for transfers between devices  77.6 us (41%)
  starting transfers between devices  42.3 us (22%)
  blocking collectives  40.9 us (22%)
  local copies, waits for them, and re-layouts  16 us (9%)
  matrix products  5.03 us (3%)
  other arithmetic  5.02 us (3%)
    all_to_all x2, blocking collectives, a2a_gather(): return lax.all_to_all(spread, axis, 0, 0, tiled=True)  31.5 us
    all_to_all x1, waiting for transfers between devices, local(): got = lax.all_to_all(flat, 'blk', 0, 0, tiled=True).reshape(packed.shape)  31.2 us
    all_to_all x1, starting transfers between devices, local(): got = lax.all_to_all(flat, 'blk', 0, 0, tiled=True).reshape(packed.shape)  18.2 us
    all_to_all x1, waiting for transfers between devices, a2a_sum(): back = lax.all_to_all(spread, axis, 0, 0, tiled=True)  15.8 us
    all_to_all x1, waiting for transfers between devices, local(): lax.all_to_all(parts, 'blk', 0, 0, tiled=True).astype(jnp.float32)  14.7 us
    all_to_all x1, waiting for transfers between devices, a2a_sum(): lax.all_to_all(parts, axis, 0, 0, tiled=True).astype(jnp.float32)  13.8 us
    all_to_all x1, blocking collectives, a2a_scatter_sum(): got = lax.all_to_all(x.astype(jnp.bfloat16), axis, 0, 0, tiled=True)  9.33 us
    unnamed x37, local copies, waits for them, and re-layouts  7.69 us
  transfers between devices with their start and end apart: 6, of which 6 were waited for; matrix products, arithmetic and copies ran while one was open for 1% of the time, Pallas kernels for 0%

profile of v7, /device:TPU:1, one launch (start us, length us, event | category | flops | bytes accessed | tf_op | source)
XLA Modules:
  0.0 187.2 jit_solution(7871111192520448969)
XLA Ops:
  0.0 0.7 copy-done.12
  0.8 0.4 copy-done
  1.2 1.4 fusion.63
  2.7 0.3 fusion.61
  2.9 0.4 fusion.21
  3.3 0.2 fusion.19
  3.6 0.3 copy.127
  4.0 0.2 copy.129
  4.2 0.2 copy.128
  4.4 0.2 maximum_bitcast_fusion
  4.6 1.7 all_to_all.32
  6.3 18.2 %all-to-all-start = ((f32[64,1,2056]{2,1,0:T(1,128)}), f32[64,1,2056]{2,1,0:T(1,128)S(1)}, u32[]{:S(2)}, u32[]{:S(2)}) async-start(f32[64,1,2056]{2,1,0:T(1,128)} %all_to_all.32), calls=%async_computation | async-start | bytes 1114112 | tf_op jit(solution)/shard_map/all_to_all | solution.py:146
  24.5 0.8 constant_dynamic-slice_fusion.2
  25.4 0.8 fusion.62
  26.3 31.2 %all-to-all-done = f32[64,1,2056]{2,1,0:T(1,128)S(1)} async-done(((f32[64,1,2056]{2,1,0:T(1,128)}), f32[64,1,2056]{2,1,0:T(1,128)S(1)}, u32[]{:S(2)}, u32[]{:S(2)}) %all-to-all-start) | async-done | bytes 526368 | tf_op jit(solution)/shard_map/all_to_all | solution.py:146
  57.4 1.3 reduce.10
  58.8 0.4 reshape.369
  59.2 0.2 fusion.60
  59.7 0.2 fusion.39
  60.0 0.2 fusion.18
  60.2 0.2 fusion.11
  60.4 1.9 %collective-permute-start = (bf16[1,4,512]{2,1,0:T(4,128)(2,1)S(1)}, bf16[1,4,512]{2,1,0:T(4,128)(2,1)S(1)}, u32[]{:S(2)}, u32[]{:S(2)}) collective-permute-start(bf16[1,4,512]{2,1,0:T(4,128)(2,1)S(1)} %fusion.11), channel_id=1, source_target_pairs={{0,8},{8,0},{16,24},{24,16},{32,40},{40,32},{48,56},{56,48},{64,72... | collective-permute-start | bytes 12296 | tf_op jit(solution)/shard_map/ppermute | solution.py:22
  62.3 1.1 collective-permute-done
  63.5 4.0 %collective-permute-start.1 = (bf16[2,4,512]{2,1,0:T(4,128)(2,1)S(1)}, bf16[2,4,512]{2,1,0:T(4,128)(2,1)S(1)}, u32[]{:S(2)}, u32[]{:S(2)}) collective-permute-start(bf16[2,4,512]{2,1,0:T(4,128)(2,1)S(1)} %pad_maximum_fusion.1), channel_id=1, source_target_pairs={{0,16},{8,24},{16,0},{24,8},{32,48},{40,56},{48,32},{56,40},{64,80... | collective-permute-start | bytes 24584 | tf_op jit(solution)/shard_map/ppermute | solution.py:22
  67.5 1.0 collective-permute-done.1
  68.6 0.7 copy-done.10
  69.3 0.3 convolution_convert_fusion.1
  69.5 0.2 convert_element_type.133
  69.8 0.2 copy.134
  69.9 0.8 reshape.393
  70.8 6.6 %all-to-all-start.1 = ((bf16[64,2,256]{2,1,0:T(2,128)(2,1)}), bf16[64,2,256]{2,1,0:T(2,128)(2,1)S(1)}, u32[]{:S(2)}, u32[]{:S(2)}) async-start(bf16[64,2,256]{2,1,0:T(2,128)(2,1)} %reshape.393), calls=%async_computation.1 | async-start | bytes 131072 | tf_op jit(solution)/shard_map/all_to_all | solution.py:65
  77.6 0.6 copy-done.8
  78.2 13.8 %all-to-all-done.1 = bf16[64,2,256]{2,1,0:T(2,128)(2,1)S(1)} async-done(((bf16[64,2,256]{2,1,0:T(2,128)(2,1)}), bf16[64,2,256]{2,1,0:T(2,128)(2,1)S(1)}, u32[]{:S(2)}, u32[]{:S(2)}) %all-to-all-start.1) | async-done | bytes 65568 | tf_op jit(solution)/shard_map/all_to_all | solution.py:65
  92.0 0.2 reshape.394
  92.3 0.9 reshape.395
  93.2 4.4 %all-to-all-start.2 = ((f32[64,1,512]{2,1,0:T(1,128)}), f32[64,1,512]{2,1,0:T(1,128)S(1)}, u32[]{:S(2)}, u32[]{:S(2)}) async-start(f32[64,1,512]{2,1,0:T(1,128)} %reshape.395), calls=%async_computation.2 | async-start | bytes 262144 | tf_op jit(solution)/shard_map/all_to_all | solution.py:67
  97.8 0.3 reduce_window_sum.11
  98.3 0.6 copy-done.11
  99.0 15.8 %all-to-all-done.2 = f32[64,1,512]{2,1,0:T(1,128)S(1)} async-done(((f32[64,1,512]{2,1,0:T(1,128)}), f32[64,1,512]{2,1,0:T(1,128)S(1)}, u32[]{:S(2)}, u32[]{:S(2)}) %all-to-all-start.2) | async-done | bytes 131104 | tf_op jit(solution)/shard_map/all_to_all | solution.py:67
  114.8 0.5 broadcast.212
  115.3 0.9 reduce.15
  116.6 0.2 reshape.375
  116.9 0.3 multiply_reduce_fusion
  117.2 0.2 multiply_convert_fusion
  117.4 0.3 convert_element_type.145
  117.8 0.6 copy-done.5
  118.4 0.2 fusion.9
  118.6 0.2 select_reduce_fusion
  119.1 13.2 %all_to_all.40 = bf16[8,1,3,2048]{3,2,1,0:T(4,128)(2,1)S(1)} all-to-all(bf16[8,1,3,2048]{3,2,1,0:T(4,128)(2,1)S(1)} %broadcast_in_dim.42), channel_id=1, replica_groups=mesh['blk'=64,'exp'=8] {'exp'}, dimensions={0} | all-to-all | bytes 196608 | tf_op jit(solution)/shard_map/all_to_all | solution.py:74
  132.4 0.3 fusion.16
  132.7 0.3 fusion.4
  133.1 0.4 copy-done.2
  133.5 0.2 fusion
  133.8 9.3 %all_to_all.41 = bf16[8,1,3,2048]{3,2,1,0:T(4,128)(2,1)S(1)} all-to-all(bf16[8,1,3,2048]{3,2,1,0:T(4,128)(2,1)S(1)} %copy.140), channel_id=1, replica_groups=mesh['blk'=64,'exp'=8] {'exp'}, dimensions={0} | all-to-all | bytes 196608 | tf_op jit(solution)/shard_map/all_to_all | solution.py:78
  143.4 0.5 fusion.3
  143.9 0.3 copy.142
  144.2 0.8 reshape.397
  145.0 7.2 %all-to-all-start.5 = ((bf16[64,2,256]{2,1,0:T(2,128)(2,1)}), bf16[64,2,256]{2,1,0:T(2,128)(2,1)S(1)}, u32[]{:S(2)}, u32[]{:S(2)}) async-start(bf16[64,2,256]{2,1,0:T(2,128)(2,1)} %reshape.397), calls=%async_computation.5 | async-start | bytes 131072 | tf_op jit(solution)/shard_map/all_to_all | solution.py:214
  152.2 14.7 %all-to-all-done.5 = bf16[64,2,256]{2,1,0:T(2,128)(2,1)S(1)} async-done(((bf16[64,2,256]{2,1,0:T(2,128)(2,1)}), bf16[64,2,256]{2,1,0:T(2,128)(2,1)S(1)}, u32[]{:S(2)}, u32[]{:S(2)}) %all-to-all-start.5) | async-done | bytes 65568 | tf_op jit(solution)/shard_map/all_to_all | solution.py:214
  166.8 0.2 reshape.398
  167.0 0.3 copy.143
  167.8 18.3 %all_to_all.42 = bf16[64,2,256]{2,1,0:T(2,128)(2,1)S(1)} all-to-all(bf16[64,2,256]{2,1,0:T(2,128)(2,1)S(1)} %reshape.399), channel_id=1, replica_groups=mesh['blk'=64,'exp'=8] {'blk'}, dimensions={0} | all-to-all | bytes 131072 | tf_op jit(solution)/shard_map/all_to_all | solution.py:74
  186.1 0.2 reshape.400
  186.3 0.9 reshape_reshape.4
  (70 shorter events, 3.2 us)
Async XLA Ops:
  0.0 1.2 copy-start
  0.0 0.7 copy-start.12
  1.2 1.4 copy-start.7
  1.2 1.4 copy-start.9
  6.3 51.1 %all-to-all-start = ((f32[64,1,2056]{2,1,0:T(1,128)}), f32[64,1,2056]{2,1,0:T(1,128)S(1)}, u32[]{:S(2)}, u32[]{:S(2)}) async-start(f32[64,1,2056]{2,1,0:T(1,128)} %all_to_all.32), calls=%async_computation | async-start | bytes 1114112 | tf_op jit(solution)/shard_map/all_to_all | solution.py:146
  24.5 0.8 copy-start.13
  60.2 8.4 %copy-start.6 = (bf16[32,2048]{1,0:T(8,128)(2,1)S(1)}, bf16[32,2048]{1,0:T(8,128)(2,1)}, u32[]{:S(2)}) copy-start(bf16[32,2048]{1,0:T(8,128)(2,1)} %param.25) | copy-start | bytes 393220
  60.4 3.1 %collective-permute-start = (bf16[1,4,512]{2,1,0:T(4,128)(2,1)S(1)}, bf16[1,4,512]{2,1,0:T(4,128)(2,1)S(1)}, u32[]{:S(2)}, u32[]{:S(2)}) collective-permute-start(bf16[1,4,512]{2,1,0:T(4,128)(2,1)S(1)} %fusion.11), channel_id=1, source_target_pairs={{0,8},{8,0},{16,24},{24,16},{32,40},{40,32},{48,56},{56,48},{64,72... | collective-permute-start | bytes 12296 | tf_op jit(solution)/shard_map/ppermute | solution.py:22
  63.5 5.0 %collective-permute-start.1 = (bf16[2,4,512]{2,1,0:T(4,128)(2,1)S(1)}, bf16[2,4,512]{2,1,0:T(4,128)(2,1)S(1)}, u32[]{:S(2)}, u32[]{:S(2)}) collective-permute-start(bf16[2,4,512]{2,1,0:T(4,128)(2,1)S(1)} %pad_maximum_fusion.1), channel_id=1, source_target_pairs={{0,16},{8,24},{16,0},{24,8},{32,48},{40,56},{48,32},{56,40},{64,80... | collective-permute-start | bytes 24584 | tf_op jit(solution)/shard_map/ppermute | solution.py:22
  68.5 0.8 copy-start.10
  70.8 6.6 %copy-start.4 = (bf16[4,4,2048]{2,1,0:T(4,128)(2,1)S(1)}, bf16[4,4,2048]{2,1,0:T(4,128)(2,1)}, u32[]{:S(2)}) copy-start(bf16[4,4,2048]{2,1,0:T(4,128)(2,1)} %param.16) | copy-start | bytes 196612
  70.8 21.2 %all-to-all-start.1 = ((bf16[64,2,256]{2,1,0:T(2,128)(2,1)}), bf16[64,2,256]{2,1,0:T(2,128)(2,1)S(1)}, u32[]{:S(2)}, u32[]{:S(2)}) async-start(bf16[64,2,256]{2,1,0:T(2,128)(2,1)} %reshape.393), calls=%async_computation.1 | async-start | bytes 131072 | tf_op jit(solution)/shard_map/all_to_all | solution.py:65
  77.4 0.7 copy-start.8
  93.2 21.6 %all-to-all-start.2 = ((f32[64,1,512]{2,1,0:T(1,128)}), f32[64,1,512]{2,1,0:T(1,128)S(1)}, u32[]{:S(2)}, u32[]{:S(2)}) async-start(f32[64,1,512]{2,1,0:T(1,128)} %reshape.395), calls=%async_computation.2 | async-start | bytes 262144 | tf_op jit(solution)/shard_map/all_to_all | solution.py:67
  98.2 0.7 copy-start.11
  117.4 1.0 copy-start.5
  117.7 14.7 %copy-start.1 = (bf16[1,2048,176]{1,2,0:T(8,128)(2,1)S(1)}, bf16[1,2048,176]{1,2,0:T(8,128)(2,1)}, u32[]{:S(2)}) copy-start(bf16[1,2048,176]{1,2,0:T(8,128)(2,1)} %param.29) | copy-start | bytes 2162692
  119.0 13.7 %copy-start.3 = (bf16[1,2048,176]{1,2,0:T(8,128)(2,1)S(1)}, bf16[1,2048,176]{1,2,0:T(8,128)(2,1)}, u32[]{:S(2)}) copy-start(bf16[1,2048,176]{1,2,0:T(8,128)(2,1)} %param.30) | copy-start | bytes 2162692
  132.4 1.1 copy-start.2
  145.0 21.8 %all-to-all-start.5 = ((bf16[64,2,256]{2,1,0:T(2,128)(2,1)}), bf16[64,2,256]{2,1,0:T(2,128)(2,1)S(1)}, u32[]{:S(2)}, u32[]{:S(2)}) async-start(bf16[64,2,256]{2,1,0:T(2,128)(2,1)} %reshape.397), calls=%async_computation.5 | async-start | bytes 131072 | tf_op jit(solution)/shard_map/all_to_all | solution.py:214

commit v8 on v7

--- a/solution.py
+++ b/solution.py
@@ -104,6 +104,14 @@
     weight_sum = factor_left * total_left + factor_right * total_right
     summed = factor_left[..., None] * sum_left + factor_right[..., None] * sum_right
     return (peak_val, weight_sum, summed)
+
+
+def merge_packed(left, right, width):
+    peak_val, weight_sum, summed = merge_pair(
+        (left[..., width], left[..., width + 1], left[..., :width]),
+        (right[..., width], right[..., width + 1], right[..., :width]),
+    )
+    return jnp.concatenate([summed, peak_val[..., None], weight_sum[..., None]], axis=-1)
 
 
 def local(
@@ -140,10 +148,19 @@
     head_bits = head_count.bit_length() - 1
     low_bits = blk_bits - head_bits
     packed = jnp.concatenate([summed, peak_val[..., None], weight_sum[..., None]], axis=-1)
-    packed = packed.reshape(requests, new_steps, head_count, latent_dim + 2).transpose(2, 0, 1, 3)
-    packed = packed.reshape(head_count * requests, new_steps, latent_dim + 2)
-    flat = packed.reshape(head_count * requests, new_steps * (latent_dim + 2))
-    got = lax.all_to_all(flat, "blk", 0, 0, tiled=True).reshape(packed.shape)
+    packed = packed.reshape((2,) * low_bits + (query_rows, latent_dim + 2))
+    for bit in range(low_bits):
+        axis_pos = low_bits - 1 - bit
+        side = (me >> bit) & 1
+        keep = lax.dynamic_index_in_dim(packed, side, axis_pos, keepdims=False)
+        send = lax.dynamic_index_in_dim(packed, 1 - side, axis_pos, keepdims=False)
+        packed = merge_packed(keep, exchange(send, "blk", 1 << bit), latent_dim)
+    packed = packed.reshape(new_steps, head_count, latent_dim + 2).transpose(1, 0, 2)
+    flat = packed.reshape(head_count, new_steps * (latent_dim + 2))
+    quad = 1 << low_bits
+    owners = [[slot + quad * h for h in range(head_count)] for slot in range(quad)]
+    got = lax.all_to_all(flat, "blk", 0, 0, tiled=True, axis_index_groups=owners)
+    got = got.reshape(head_count, new_steps, latent_dim + 2)
     peaks = got[..., latent_dim]
     totals = got[..., latent_dim + 1]
     peak_all = jnp.max(peaks, axis=0)

time: 188 us -> 178 us (0.947)
  waiting for transfers between devices: 77.6 us -> 63.5 us
  starting transfers between devices: 42.3 us -> 48.5 us
    all_to_all x1, waiting for transfers between devices: 31.2 us -> 11.3 us  [local(): lax.all_to_all(flat, 'blk', 0, 0, tiled=True, axis_index_groups=owners)]
    ppermute x2 -> x4, starting transfers between devices: 5.9 us -> 18.9 us  [exchange(): lax.ppermute(part, axis, xor_pairs(count, mask))]
    all_to_all x1, starting transfers between devices: 18.2 us -> 10.7 us  [local(): lax.all_to_all(flat, 'blk', 0, 0, tiled=True, axis_index_groups=owners)]
    ppermute x2 -> x4, waiting for transfers between devices: 2.15 us -> 7.92 us  [exchange(): lax.ppermute(part, axis, xor_pairs(count, mask))]
  transfers between devices with their start and end apart: 6 -> 8, of which waited for: 6 -> 8; matrix products, arithmetic and copies ran while one was open for 1% -> 2% of each run, Pallas kernels for 0% -> 0%
where the time goes in v8:
time: 178 us; the launch traced here: 177 us
  waiting for transfers between devices  63.5 us (36%)
  starting transfers between devices  48.5 us (27%)
  blocking collectives  40.9 us (23%)
  local copies, waits for them, and re-layouts  14.3 us (8%)
  matrix products  5.03 us (3%)
  other arithmetic  4.59 us (3%)
    all_to_all x2, blocking collectives, a2a_gather(): return lax.all_to_all(spread, axis, 0, 0, tiled=True)  31.5 us
    ppermute x4, starting transfers between devices, exchange(): lax.ppermute(part, axis, xor_pairs(count, mask))  18.9 us
    all_to_all x1, waiting for transfers between devices, a2a_sum(): back = lax.all_to_all(spread, axis, 0, 0, tiled=True)  15.8 us
    all_to_all x1, waiting for transfers between devices, local(): lax.all_to_all(parts, 'blk', 0, 0, tiled=True).astype(jnp.float32)  14.7 us
    all_to_all x1, waiting for transfers between devices, a2a_sum(): lax.all_to_all(parts, axis, 0, 0, tiled=True).astype(jnp.float32)  13.8 us
    all_to_all x1, waiting for transfers between devices, local(): lax.all_to_all(flat, 'blk', 0, 0, tiled=True, axis_index_groups=owners)  11.3 us
    all_to_all x1, starting transfers between devices, local(): lax.all_to_all(flat, 'blk', 0, 0, tiled=True, axis_index_groups=owners)  10.7 us
    all_to_all x1, blocking collectives, a2a_scatter_sum(): got = lax.all_to_all(x.astype(jnp.bfloat16), axis, 0, 0, tiled=True)  9.33 us
  transfers between devices with their start and end apart: 8, of which 8 were waited for; matrix products, arithmetic and copies ran while one was open for 2% of the time, Pallas kernels for 0%

profile of v8, /device:TPU:1, one launch (start us, length us, event | category | flops | bytes accessed | tf_op | source)
XLA Modules:
  0.0 177.4 jit_solution(14363000990395590243)
XLA Ops:
  0.0 0.7 copy-done.12
  0.8 0.4 copy-done
  1.2 1.4 fusion.71
  2.7 0.3 fusion.69
  2.9 0.4 fusion.21
  3.3 0.2 fusion.19
  3.9 8.7 %collective-permute-start = (f32[2,64,514]{2,1,0:T(8,128)S(1)}, f32[2,64,514]{2,1,0:T(8,128)S(1)}, u32[]{:S(2)}, u32[]{:S(2)}) collective-permute-start(f32[2,64,514]{2,1,0:T(8,128)S(1)} %get-tuple-element.19), channel_id=1, source_target_pairs={{0,8},{8,0},{16,24},{24,16},{32,40},{40,32},{48,56},{56,48},{64,72... | collective-permute-start | bytes 789512 | tf_op jit(solution)/shard_map/ppermute | solution.py:22
  12.7 1.2 collective-permute-done
  14.4 1.9 %collective-permute-start.1 = (f32[64,514]{1,0:T(8,128)S(1)}, f32[64,514]{1,0:T(8,128)S(1)}, u32[]{:S(2)}, u32[]{:S(2)}) collective-permute-start(f32[64,514]{1,0:T(8,128)S(1)} %get-tuple-element.21), channel_id=1, source_target_pairs={{0,16},{8,24},{16,0},{24,8},{32,48},{40,56},{48,32},{56,40},{64,80... | collective-permute-start | bytes 394760 | tf_op jit(solution)/shard_map/ppermute | solution.py:22
  16.3 0.8 constant_dynamic-slice_fusion.2
  17.1 4.6 %collective-permute-done.1 = f32[64,514]{1,0:T(8,128)S(1)} collective-permute-done((f32[64,514]{1,0:T(8,128)S(1)}, f32[64,514]{1,0:T(8,128)S(1)}, u32[]{:S(2)}, u32[]{:S(2)}) %collective-permute-start.1) | collective-permute-done | bytes 131616 | tf_op jit(solution)/shard_map/ppermute | solution.py:22
  22.1 0.9 all_to_all.32
  23.0 10.7 %all-to-all-start = ((f32[16,1,2056]{2,1,0:T(1,128)}), f32[16,1,2056]{2,1,0:T(1,128)S(1)}, u32[]{:S(2)}, u32[]{:S(2)}) async-start(f32[16,1,2056]{2,1,0:T(1,128)} %all_to_all.32), calls=%async_computation | async-start | bytes 278528 | tf_op jit(solution)/shard_map/all_to_all | solution.py:162
  33.9 0.8 fusion.70
  34.7 11.3 %all-to-all-done = f32[16,1,2056]{2,1,0:T(1,128)S(1)} async-done(((f32[16,1,2056]{2,1,0:T(1,128)}), f32[16,1,2056]{2,1,0:T(1,128)S(1)}, u32[]{:S(2)}, u32[]{:S(2)}) %all-to-all-start) | async-done | bytes 131616 | tf_op jit(solution)/shard_map/all_to_all | solution.py:162
  46.0 0.3 reduce.14
  46.9 0.2 fusion.49
  47.3 0.2 fusion.11
  47.5 5.1 %collective-permute-start.2 = (bf16[1,4,512]{2,1,0:T(4,128)(2,1)S(1)}, bf16[1,4,512]{2,1,0:T(4,128)(2,1)S(1)}, u32[]{:S(2)}, u32[]{:S(2)}) collective-permute-start(bf16[1,4,512]{2,1,0:T(4,128)(2,1)S(1)} %fusion.11), channel_id=1, source_target_pairs={{0,8},{8,0},{16,24},{24,16},{32,40},{40,32},{48,56},{56,48},{64,72... | collective-permute-start | bytes 12296 | tf_op jit(solution)/shard_map/ppermute | solution.py:22
  52.7 0.8 collective-permute-done.2
  53.5 3.1 %collective-permute-start.3 = (bf16[2,4,512]{2,1,0:T(4,128)(2,1)S(1)}, bf16[2,4,512]{2,1,0:T(4,128)(2,1)S(1)}, u32[]{:S(2)}, u32[]{:S(2)}) collective-permute-start(bf16[2,4,512]{2,1,0:T(4,128)(2,1)S(1)} %pad_maximum_fusion.3), channel_id=1, source_target_pairs={{0,16},{8,24},{16,0},{24,8},{32,48},{40,56},{48,32},{56,40},{64,80... | collective-permute-start | bytes 24584 | tf_op jit(solution)/shard_map/ppermute | solution.py:22
  56.5 1.3 collective-permute-done.3
  58.0 0.7 copy-done.10
  58.7 0.3 convolution_convert_fusion.1
  58.9 0.2 convert_element_type.133
  59.1 0.2 copy.139
  59.3 0.8 reshape.402
  60.2 7.3 %all-to-all-start.1 = ((bf16[64,2,256]{2,1,0:T(2,128)(2,1)}), bf16[64,2,256]{2,1,0:T(2,128)(2,1)S(1)}, u32[]{:S(2)}, u32[]{:S(2)}) async-start(bf16[64,2,256]{2,1,0:T(2,128)(2,1)} %reshape.402), calls=%async_computation.1 | async-start | bytes 131072 | tf_op jit(solution)/shard_map/all_to_all | solution.py:65
  67.7 0.6 copy-done.8
  68.3 13.8 %all-to-all-done.1 = bf16[64,2,256]{2,1,0:T(2,128)(2,1)S(1)} async-done(((bf16[64,2,256]{2,1,0:T(2,128)(2,1)}), bf16[64,2,256]{2,1,0:T(2,128)(2,1)S(1)}, u32[]{:S(2)}, u32[]{:S(2)}) %all-to-all-start.1) | async-done | bytes 65568 | tf_op jit(solution)/shard_map/all_to_all | solution.py:65
  82.1 0.2 reshape.403
  82.4 0.9 reshape.404
  83.3 4.4 %all-to-all-start.2 = ((f32[64,1,512]{2,1,0:T(1,128)}), f32[64,1,512]{2,1,0:T(1,128)S(1)}, u32[]{:S(2)}, u32[]{:S(2)}) async-start(f32[64,1,512]{2,1,0:T(1,128)} %reshape.404), calls=%async_computation.2 | async-start | bytes 262144 | tf_op jit(solution)/shard_map/all_to_all | solution.py:67
  87.9 0.3 reduce_window_sum.11
  88.4 0.6 copy-done.11
  89.1 15.8 %all-to-all-done.2 = f32[64,1,512]{2,1,0:T(1,128)S(1)} async-done(((f32[64,1,512]{2,1,0:T(1,128)}), f32[64,1,512]{2,1,0:T(1,128)S(1)}, u32[]{:S(2)}, u32[]{:S(2)}) %all-to-all-start.2) | async-done | bytes 131104 | tf_op jit(solution)/shard_map/all_to_all | solution.py:67
  104.9 0.5 broadcast.216
  105.4 0.9 reduce.23
  106.4 0.2 reshape.405
  106.6 0.2 copy.176
  106.8 0.2 reshape.380
  107.0 0.3 multiply_reduce_fusion
  107.3 0.2 multiply_convert_fusion
  107.6 0.3 convert_element_type.145
  107.9 0.6 copy-done.5
  108.5 0.2 fusion.9
  108.7 0.2 select_reduce_fusion
  109.2 13.2 %all_to_all.40 = bf16[8,1,3,2048]{3,2,1,0:T(4,128)(2,1)S(1)} all-to-all(bf16[8,1,3,2048]{3,2,1,0:T(4,128)(2,1)S(1)} %broadcast_in_dim.38), channel_id=1, replica_groups=mesh['blk'=64,'exp'=8] {'exp'}, dimensions={0} | all-to-all | bytes 196608 | tf_op jit(solution)/shard_map/all_to_all | solution.py:74
  122.5 0.3 fusion.16
  122.9 0.3 fusion.4
  123.2 0.4 copy-done.2
  123.6 0.2 fusion
  123.9 9.3 %all_to_all.41 = bf16[8,1,3,2048]{3,2,1,0:T(4,128)(2,1)S(1)} all-to-all(bf16[8,1,3,2048]{3,2,1,0:T(4,128)(2,1)S(1)} %copy.145), channel_id=1, replica_groups=mesh['blk'=64,'exp'=8] {'exp'}, dimensions={0} | all-to-all | bytes 196608 | tf_op jit(solution)/shard_map/all_to_all | solution.py:78
  133.5 0.5 fusion.3
  134.0 0.3 copy.147
  134.3 0.8 reshape.406
  135.1 7.2 %all-to-all-start.5 = ((bf16[64,2,256]{2,1,0:T(2,128)(2,1)}), bf16[64,2,256]{2,1,0:T(2,128)(2,1)S(1)}, u32[]{:S(2)}, u32[]{:S(2)}) async-start(bf16[64,2,256]{2,1,0:T(2,128)(2,1)} %reshape.406), calls=%async_computation.5 | async-start | bytes 131072 | tf_op jit(solution)/shard_map/all_to_all | solution.py:231
  142.3 14.7 %all-to-all-done.5 = bf16[64,2,256]{2,1,0:T(2,128)(2,1)S(1)} async-done(((bf16[64,2,256]{2,1,0:T(2,128)(2,1)}), bf16[64,2,256]{2,1,0:T(2,128)(2,1)S(1)}, u32[]{:S(2)}, u32[]{:S(2)}) %all-to-all-start.5) | async-done | bytes 65568 | tf_op jit(solution)/shard_map/all_to_all | solution.py:231
  157.0 0.2 reshape.407
  157.2 0.3 copy.148
  157.7 0.2 reshape.408
  157.9 18.3 %all_to_all.42 = bf16[64,2,256]{2,1,0:T(2,128)(2,1)S(1)} all-to-all(bf16[64,2,256]{2,1,0:T(2,128)(2,1)S(1)} %reshape.408), channel_id=1, replica_groups=mesh['blk'=64,'exp'=8] {'blk'}, dimensions={0} | all-to-all | bytes 131072 | tf_op jit(solution)/shard_map/all_to_all | solution.py:74
  176.2 0.2 reshape.409
  176.4 0.9 reshape_reshape.3
  (82 shorter events, 4.2 us)
Async XLA Ops:
  0.0 1.2 copy-start
  0.0 0.7 copy-start.12
  1.2 1.4 copy-start.7
  1.2 1.4 copy-start.9
  3.9 10.0 %collective-permute-start = (f32[2,64,514]{2,1,0:T(8,128)S(1)}, f32[2,64,514]{2,1,0:T(8,128)S(1)}, u32[]{:S(2)}, u32[]{:S(2)}) collective-permute-start(f32[2,64,514]{2,1,0:T(8,128)S(1)} %get-tuple-element.19), channel_id=1, source_target_pairs={{0,8},{8,0},{16,24},{24,16},{32,40},{40,32},{48,56},{56,48},{64,72... | collective-permute-start | bytes 789512 | tf_op jit(solution)/shard_map/ppermute | solution.py:22
  14.4 7.3 %collective-permute-start.1 = (f32[64,514]{1,0:T(8,128)S(1)}, f32[64,514]{1,0:T(8,128)S(1)}, u32[]{:S(2)}, u32[]{:S(2)}) collective-permute-start(f32[64,514]{1,0:T(8,128)S(1)} %get-tuple-element.21), channel_id=1, source_target_pairs={{0,16},{8,24},{16,0},{24,8},{32,48},{40,56},{48,32},{56,40},{64,80... | collective-permute-start | bytes 394760 | tf_op jit(solution)/shard_map/ppermute | solution.py:22
  23.0 10.7 %copy-start.13 = (bf16[4,4,512]{2,1,0:T(4,128)(2,1)S(1)}, bf16[4,4,512]{2,1,0:T(4,128)(2,1)}, u32[]{:S(2)}) copy-start(bf16[4,4,512]{2,1,0:T(4,128)(2,1)} %param.19) | copy-start | bytes 49156
  23.0 23.0 %all-to-all-start = ((f32[16,1,2056]{2,1,0:T(1,128)}), f32[16,1,2056]{2,1,0:T(1,128)S(1)}, u32[]{:S(2)}, u32[]{:S(2)}) async-start(f32[16,1,2056]{2,1,0:T(1,128)} %all_to_all.32), calls=%async_computation | async-start | bytes 278528 | tf_op jit(solution)/shard_map/all_to_all | solution.py:162
  47.3 10.6 %copy-start.6 = (bf16[32,2048]{1,0:T(8,128)(2,1)S(1)}, bf16[32,2048]{1,0:T(8,128)(2,1)}, u32[]{:S(2)}) copy-start(bf16[32,2048]{1,0:T(8,128)(2,1)} %param.25) | copy-start | bytes 393220
  47.5 5.9 %collective-permute-start.2 = (bf16[1,4,512]{2,1,0:T(4,128)(2,1)S(1)}, bf16[1,4,512]{2,1,0:T(4,128)(2,1)S(1)}, u32[]{:S(2)}, u32[]{:S(2)}) collective-permute-start(bf16[1,4,512]{2,1,0:T(4,128)(2,1)S(1)} %fusion.11), channel_id=1, source_target_pairs={{0,8},{8,0},{16,24},{24,16},{32,40},{40,32},{48,56},{56,48},{64,72... | collective-permute-start | bytes 12296 | tf_op jit(solution)/shard_map/ppermute | solution.py:22
  53.5 4.4 %collective-permute-start.3 = (bf16[2,4,512]{2,1,0:T(4,128)(2,1)S(1)}, bf16[2,4,512]{2,1,0:T(4,128)(2,1)S(1)}, u32[]{:S(2)}, u32[]{:S(2)}) collective-permute-start(bf16[2,4,512]{2,1,0:T(4,128)(2,1)S(1)} %pad_maximum_fusion.3), channel_id=1, source_target_pairs={{0,16},{8,24},{16,0},{24,8},{32,48},{40,56},{48,32},{56,40},{64,80... | collective-permute-start | bytes 24584 | tf_op jit(solution)/shard_map/ppermute | solution.py:22
  57.9 0.8 copy-start.10
  60.1 7.4 %copy-start.4 = (bf16[4,4,2048]{2,1,0:T(4,128)(2,1)S(1)}, bf16[4,4,2048]{2,1,0:T(4,128)(2,1)}, u32[]{:S(2)}) copy-start(bf16[4,4,2048]{2,1,0:T(4,128)(2,1)} %param.16) | copy-start | bytes 196612
  60.2 21.9 %all-to-all-start.1 = ((bf16[64,2,256]{2,1,0:T(2,128)(2,1)}), bf16[64,2,256]{2,1,0:T(2,128)(2,1)S(1)}, u32[]{:S(2)}, u32[]{:S(2)}) async-start(bf16[64,2,256]{2,1,0:T(2,128)(2,1)} %reshape.402), calls=%async_computation.1 | async-start | bytes 131072 | tf_op jit(solution)/shard_map/all_to_all | solution.py:65
  67.5 0.7 copy-start.8
  83.3 21.6 %all-to-all-start.2 = ((f32[64,1,512]{2,1,0:T(1,128)}), f32[64,1,512]{2,1,0:T(1,128)S(1)}, u32[]{:S(2)}, u32[]{:S(2)}) async-start(f32[64,1,512]{2,1,0:T(1,128)} %reshape.404), calls=%async_computation.2 | async-start | bytes 262144 | tf_op jit(solution)/shard_map/all_to_all | solution.py:67
  88.3 0.7 copy-start.11
  107.5 1.0 copy-start.5
  107.8 14.7 %copy-start.1 = (bf16[1,2048,176]{1,2,0:T(8,128)(2,1)S(1)}, bf16[1,2048,176]{1,2,0:T(8,128)(2,1)}, u32[]{:S(2)}) copy-start(bf16[1,2048,176]{1,2,0:T(8,128)(2,1)} %param.29) | copy-start | bytes 2162692
  109.1 13.7 %copy-start.3 = (bf16[1,2048,176]{1,2,0:T(8,128)(2,1)S(1)}, bf16[1,2048,176]{1,2,0:T(8,128)(2,1)}, u32[]{:S(2)}) copy-start(bf16[1,2048,176]{1,2,0:T(8,128)(2,1)} %param.30) | copy-start | bytes 2162692
  122.5 1.1 copy-start.2
  135.1 21.8 %all-to-all-start.5 = ((bf16[64,2,256]{2,1,0:T(2,128)(2,1)}), bf16[64,2,256]{2,1,0:T(2,128)(2,1)S(1)}, u32[]{:S(2)}, u32[]{:S(2)}) async-start(bf16[64,2,256]{2,1,0:T(2,128)(2,1)} %reshape.406), calls=%async_computation.5 | async-start | bytes 131072 | tf_op jit(solution)/shard_map/all_to_all | solution.py:231

commit v9 on v8

--- a/solution.py
+++ b/solution.py
@@ -63,8 +63,8 @@
     rows, cols = x.shape
     parts = x.reshape(rows, count, cols // count).transpose(1, 0, 2).astype(jnp.bfloat16)
     mine = lax.all_to_all(parts, axis, 0, 0, tiled=True).astype(jnp.float32).sum(axis=0)
-    spread = jnp.broadcast_to(mine[None], (count,) + mine.shape)
-    back = lax.all_to_all(spread, axis, 0, 0, tiled=True)
+    spread = jnp.broadcast_to(mine.astype(jnp.bfloat16)[None], (count,) + mine.shape)
+    back = lax.all_to_all(spread, axis, 0, 0, tiled=True).astype(jnp.float32)
     return back.transpose(1, 0, 2).reshape(rows, cols)
 
 

time: 178 us -> 175 us (0.983)
  waiting for transfers between devices: 63.5 us -> 60.7 us
    all_to_all x1, waiting for transfers between devices: 15.8 us -> 13.3 us  [a2a_sum(): back = lax.all_to_all(spread, axis, 0, 0, tiled=True).astype(jnp.float32)]
where the time goes in v9:
time: 175 us; the launch traced here: 174 us
  waiting for transfers between devices  60.7 us (35%)
  starting transfers between devices  48.5 us (28%)
  blocking collectives  40.9 us (23%)
  local copies, waits for them, and re-layouts  14.5 us (8%)
  matrix products  5.03 us (3%)
  other arithmetic  3.44 us (2%)
    all_to_all x2, blocking collectives, a2a_gather(): return lax.all_to_all(spread, axis, 0, 0, tiled=True)  31.5 us
    ppermute x4, starting transfers between devices, exchange(): lax.ppermute(part, axis, xor_pairs(count, mask))  18.9 us
    all_to_all x1, waiting for transfers between devices, local(): lax.all_to_all(parts, 'blk', 0, 0, tiled=True).astype(jnp.float32)  14.7 us
    all_to_all x1, waiting for transfers between devices, a2a_sum(): lax.all_to_all(parts, axis, 0, 0, tiled=True).astype(jnp.float32)  13.5 us
    all_to_all x1, waiting for transfers between devices, a2a_sum(): back = lax.all_to_all(spread, axis, 0, 0, tiled=True).astype(jnp.float32)  13.3 us
    all_to_all x1, waiting for transfers between devices, local(): lax.all_to_all(flat, 'blk', 0, 0, tiled=True, axis_index_groups=owners)  11.3 us
    all_to_all x1, starting transfers between devices, local(): lax.all_to_all(flat, 'blk', 0, 0, tiled=True, axis_index_groups=owners)  10.7 us
    all_to_all x1, blocking collectives, a2a_scatter_sum(): got = lax.all_to_all(x.astype(jnp.bfloat16), axis, 0, 0, tiled=True)  9.33 us
  transfers between devices with their start and end apart: 8, of which 8 were waited for; matrix products, arithmetic and copies ran while one was open for 2% of the time, Pallas kernels for 0%

profile of v9, /device:TPU:1, one launch (start us, length us, event | category | flops | bytes accessed | tf_op | source)
XLA Modules:
  0.0 173.6 jit_solution(4088901048530730377)
XLA Ops:
  0.0 0.7 copy-done.12
  0.8 0.4 copy-done
  1.2 1.4 fusion.71
  2.7 0.3 fusion.69
  2.9 0.4 fusion.21
  3.3 0.2 fusion.19
  3.9 8.7 %collective-permute-start = (f32[2,64,514]{2,1,0:T(8,128)S(1)}, f32[2,64,514]{2,1,0:T(8,128)S(1)}, u32[]{:S(2)}, u32[]{:S(2)}) collective-permute-start(f32[2,64,514]{2,1,0:T(8,128)S(1)} %get-tuple-element.19), channel_id=1, source_target_pairs={{0,8},{8,0},{16,24},{24,16},{32,40},{40,32},{48,56},{56,48},{64,72... | collective-permute-start | bytes 789512 | tf_op jit(solution)/shard_map/ppermute | solution.py:22
  12.7 1.2 collective-permute-done
  14.4 1.9 %collective-permute-start.1 = (f32[64,514]{1,0:T(8,128)S(1)}, f32[64,514]{1,0:T(8,128)S(1)}, u32[]{:S(2)}, u32[]{:S(2)}) collective-permute-start(f32[64,514]{1,0:T(8,128)S(1)} %get-tuple-element.21), channel_id=1, source_target_pairs={{0,16},{8,24},{16,0},{24,8},{32,48},{40,56},{48,32},{56,40},{64,80... | collective-permute-start | bytes 394760 | tf_op jit(solution)/shard_map/ppermute | solution.py:22
  16.3 0.8 constant_dynamic-slice_fusion.2
  17.1 4.6 %collective-permute-done.1 = f32[64,514]{1,0:T(8,128)S(1)} collective-permute-done((f32[64,514]{1,0:T(8,128)S(1)}, f32[64,514]{1,0:T(8,128)S(1)}, u32[]{:S(2)}, u32[]{:S(2)}) %collective-permute-start.1) | collective-permute-done | bytes 131616 | tf_op jit(solution)/shard_map/ppermute | solution.py:22
  22.1 0.9 all_to_all.32
  23.0 10.7 %all-to-all-start = ((f32[16,1,2056]{2,1,0:T(1,128)}), f32[16,1,2056]{2,1,0:T(1,128)S(1)}, u32[]{:S(2)}, u32[]{:S(2)}) async-start(f32[16,1,2056]{2,1,0:T(1,128)} %all_to_all.32), calls=%async_computation | async-start | bytes 278528 | tf_op jit(solution)/shard_map/all_to_all | solution.py:162
  33.9 0.8 fusion.70
  34.7 11.3 %all-to-all-done = f32[16,1,2056]{2,1,0:T(1,128)S(1)} async-done(((f32[16,1,2056]{2,1,0:T(1,128)}), f32[16,1,2056]{2,1,0:T(1,128)S(1)}, u32[]{:S(2)}, u32[]{:S(2)}) %all-to-all-start) | async-done | bytes 131616 | tf_op jit(solution)/shard_map/all_to_all | solution.py:162
  46.0 0.3 reduce.15
  46.9 0.2 fusion.50
  47.3 0.2 fusion.11
  47.5 5.1 %collective-permute-start.2 = (bf16[1,4,512]{2,1,0:T(4,128)(2,1)S(1)}, bf16[1,4,512]{2,1,0:T(4,128)(2,1)S(1)}, u32[]{:S(2)}, u32[]{:S(2)}) collective-permute-start(bf16[1,4,512]{2,1,0:T(4,128)(2,1)S(1)} %fusion.11), channel_id=1, source_target_pairs={{0,8},{8,0},{16,24},{24,16},{32,40},{40,32},{48,56},{56,48},{64,72... | collective-permute-start | bytes 12296 | tf_op jit(solution)/shard_map/ppermute | solution.py:22
  52.7 0.8 collective-permute-done.2
  53.5 3.1 %collective-permute-start.3 = (bf16[2,4,512]{2,1,0:T(4,128)(2,1)S(1)}, bf16[2,4,512]{2,1,0:T(4,128)(2,1)S(1)}, u32[]{:S(2)}, u32[]{:S(2)}) collective-permute-start(bf16[2,4,512]{2,1,0:T(4,128)(2,1)S(1)} %pad_maximum_fusion.3), channel_id=1, source_target_pairs={{0,16},{8,24},{16,0},{24,8},{32,48},{40,56},{48,32},{56,40},{64,80... | collective-permute-start | bytes 24584 | tf_op jit(solution)/shard_map/ppermute | solution.py:22
  56.5 1.3 collective-permute-done.3
  58.0 0.7 copy-done.10
  58.7 0.3 convolution_convert_fusion.1
  58.9 0.2 convert_element_type.133
  59.1 0.2 copy.139
  59.3 0.8 reshape.402
  60.2 7.3 %all-to-all-start.1 = ((bf16[64,2,256]{2,1,0:T(2,128)(2,1)}), bf16[64,2,256]{2,1,0:T(2,128)(2,1)S(1)}, u32[]{:S(2)}, u32[]{:S(2)}) async-start(bf16[64,2,256]{2,1,0:T(2,128)(2,1)} %reshape.402), calls=%async_computation.1 | async-start | bytes 131072 | tf_op jit(solution)/shard_map/all_to_all | solution.py:65
  67.7 0.2 copy.145
  67.9 0.5 copy-done.8
  68.5 13.5 %all-to-all-done.1 = bf16[64,2,256]{2,1,0:T(2,128)(2,1)S(1)} async-done(((bf16[64,2,256]{2,1,0:T(2,128)(2,1)}), bf16[64,2,256]{2,1,0:T(2,128)(2,1)S(1)}, u32[]{:S(2)}, u32[]{:S(2)}) %all-to-all-start.1) | async-done | bytes 65568 | tf_op jit(solution)/shard_map/all_to_all | solution.py:65
  82.1 0.2 reshape.403
  82.4 0.8 reshape.404
  83.2 4.4 %all-to-all-start.2 = ((bf16[64,2,256]{2,1,0:T(2,128)(2,1)}), bf16[64,2,256]{2,1,0:T(2,128)(2,1)S(1)}, u32[]{:S(2)}, u32[]{:S(2)}) async-start(bf16[64,2,256]{2,1,0:T(2,128)(2,1)} %reshape.404), calls=%async_computation.2 | async-start | bytes 131072 | tf_op jit(solution)/shard_map/all_to_all | solution.py:67
  87.8 0.3 reduce_window_sum.11
  88.3 0.6 copy-done.11
  89.0 13.3 %all-to-all-done.2 = bf16[64,2,256]{2,1,0:T(2,128)(2,1)S(1)} async-done(((bf16[64,2,256]{2,1,0:T(2,128)(2,1)}), bf16[64,2,256]{2,1,0:T(2,128)(2,1)S(1)}, u32[]{:S(2)}, u32[]{:S(2)}) %all-to-all-start.2) | async-done | bytes 65568 | tf_op jit(solution)/shard_map/all_to_all | solution.py:67
  102.3 0.2 reshape.405
  102.5 0.3 copy.140
  102.8 0.2 copy.141
  103.1 0.2 reshape.380
  103.3 0.2 multiply_reduce_fusion
  103.6 0.2 copy.147
  103.8 0.3 convert_element_type.144
  104.1 0.6 copy-done.5
  104.8 0.2 fusion.9
  105.0 0.2 select_reduce_fusion
  105.5 13.2 %all_to_all.40 = bf16[8,1,3,2048]{3,2,1,0:T(4,128)(2,1)S(1)} all-to-all(bf16[8,1,3,2048]{3,2,1,0:T(4,128)(2,1)S(1)} %broadcast_in_dim.38), channel_id=1, replica_groups=mesh['blk'=64,'exp'=8] {'exp'}, dimensions={0} | all-to-all | bytes 196608 | tf_op jit(solution)/shard_map/all_to_all | solution.py:74
  118.8 0.3 fusion.16
  119.1 0.3 fusion.4
  119.5 0.4 copy-done.2
  119.9 0.2 fusion
  120.2 9.3 %all_to_all.41 = bf16[8,1,3,2048]{3,2,1,0:T(4,128)(2,1)S(1)} all-to-all(bf16[8,1,3,2048]{3,2,1,0:T(4,128)(2,1)S(1)} %copy.149), channel_id=1, replica_groups=mesh['blk'=64,'exp'=8] {'exp'}, dimensions={0} | all-to-all | bytes 196608 | tf_op jit(solution)/shard_map/all_to_all | solution.py:78
  129.8 0.5 fusion.3
  130.3 0.3 copy.151
  130.6 0.8 reshape.406
  131.4 7.2 %all-to-all-start.5 = ((bf16[64,2,256]{2,1,0:T(2,128)(2,1)}), bf16[64,2,256]{2,1,0:T(2,128)(2,1)S(1)}, u32[]{:S(2)}, u32[]{:S(2)}) async-start(bf16[64,2,256]{2,1,0:T(2,128)(2,1)} %reshape.406), calls=%async_computation.5 | async-start | bytes 131072 | tf_op jit(solution)/shard_map/all_to_all | solution.py:231
  138.6 14.7 %all-to-all-done.5 = bf16[64,2,256]{2,1,0:T(2,128)(2,1)S(1)} async-done(((bf16[64,2,256]{2,1,0:T(2,128)(2,1)}), bf16[64,2,256]{2,1,0:T(2,128)(2,1)S(1)}, u32[]{:S(2)}, u32[]{:S(2)}) %all-to-all-start.5) | async-done | bytes 65568 | tf_op jit(solution)/shard_map/all_to_all | solution.py:231
  153.2 0.2 reshape.407
  153.4 0.3 copy.152
  154.0 0.2 reshape.408
  154.1 18.3 %all_to_all.42 = bf16[64,2,256]{2,1,0:T(2,128)(2,1)S(1)} all-to-all(bf16[64,2,256]{2,1,0:T(2,128)(2,1)S(1)} %reshape.408), channel_id=1, replica_groups=mesh['blk'=64,'exp'=8] {'blk'}, dimensions={0} | all-to-all | bytes 131072 | tf_op jit(solution)/shard_map/all_to_all | solution.py:74
  172.4 0.2 reshape.409
  172.7 0.9 reshape_reshape.3
  (85 shorter events, 4.4 us)
Async XLA Ops:
  0.0 1.2 copy-start
  0.0 0.7 copy-start.12
  1.2 1.4 copy-start.7
  1.2 1.4 copy-start.9
  3.9 10.0 %collective-permute-start = (f32[2,64,514]{2,1,0:T(8,128)S(1)}, f32[2,64,514]{2,1,0:T(8,128)S(1)}, u32[]{:S(2)}, u32[]{:S(2)}) collective-permute-start(f32[2,64,514]{2,1,0:T(8,128)S(1)} %get-tuple-element.19), channel_id=1, source_target_pairs={{0,8},{8,0},{16,24},{24,16},{32,40},{40,32},{48,56},{56,48},{64,72... | collective-permute-start | bytes 789512 | tf_op jit(solution)/shard_map/ppermute | solution.py:22
  14.4 7.3 %collective-permute-start.1 = (f32[64,514]{1,0:T(8,128)S(1)}, f32[64,514]{1,0:T(8,128)S(1)}, u32[]{:S(2)}, u32[]{:S(2)}) collective-permute-start(f32[64,514]{1,0:T(8,128)S(1)} %get-tuple-element.21), channel_id=1, source_target_pairs={{0,16},{8,24},{16,0},{24,8},{32,48},{40,56},{48,32},{56,40},{64,80... | collective-permute-start | bytes 394760 | tf_op jit(solution)/shard_map/ppermute | solution.py:22
  23.0 10.7 %copy-start.13 = (bf16[4,4,512]{2,1,0:T(4,128)(2,1)S(1)}, bf16[4,4,512]{2,1,0:T(4,128)(2,1)}, u32[]{:S(2)}) copy-start(bf16[4,4,512]{2,1,0:T(4,128)(2,1)} %param.19) | copy-start | bytes 49156
  23.0 23.0 %all-to-all-start = ((f32[16,1,2056]{2,1,0:T(1,128)}), f32[16,1,2056]{2,1,0:T(1,128)S(1)}, u32[]{:S(2)}, u32[]{:S(2)}) async-start(f32[16,1,2056]{2,1,0:T(1,128)} %all_to_all.32), calls=%async_computation | async-start | bytes 278528 | tf_op jit(solution)/shard_map/all_to_all | solution.py:162
  47.3 10.6 %copy-start.6 = (bf16[32,2048]{1,0:T(8,128)(2,1)S(1)}, bf16[32,2048]{1,0:T(8,128)(2,1)}, u32[]{:S(2)}) copy-start(bf16[32,2048]{1,0:T(8,128)(2,1)} %param.25) | copy-start | bytes 393220
  47.5 5.9 %collective-permute-start.2 = (bf16[1,4,512]{2,1,0:T(4,128)(2,1)S(1)}, bf16[1,4,512]{2,1,0:T(4,128)(2,1)S(1)}, u32[]{:S(2)}, u32[]{:S(2)}) collective-permute-start(bf16[1,4,512]{2,1,0:T(4,128)(2,1)S(1)} %fusion.11), channel_id=1, source_target_pairs={{0,8},{8,0},{16,24},{24,16},{32,40},{40,32},{48,56},{56,48},{64,72... | collective-permute-start | bytes 12296 | tf_op jit(solution)/shard_map/ppermute | solution.py:22
  53.5 4.4 %collective-permute-start.3 = (bf16[2,4,512]{2,1,0:T(4,128)(2,1)S(1)}, bf16[2,4,512]{2,1,0:T(4,128)(2,1)S(1)}, u32[]{:S(2)}, u32[]{:S(2)}) collective-permute-start(bf16[2,4,512]{2,1,0:T(4,128)(2,1)S(1)} %pad_maximum_fusion.3), channel_id=1, source_target_pairs={{0,16},{8,24},{16,0},{24,8},{32,48},{40,56},{48,32},{56,40},{64,80... | collective-permute-start | bytes 24584 | tf_op jit(solution)/shard_map/ppermute | solution.py:22
  57.9 0.8 copy-start.10
  60.1 7.4 %copy-start.4 = (bf16[4,4,2048]{2,1,0:T(4,128)(2,1)S(1)}, bf16[4,4,2048]{2,1,0:T(4,128)(2,1)}, u32[]{:S(2)}) copy-start(bf16[4,4,2048]{2,1,0:T(4,128)(2,1)} %param.16) | copy-start | bytes 196612
  60.2 21.9 %all-to-all-start.1 = ((bf16[64,2,256]{2,1,0:T(2,128)(2,1)}), bf16[64,2,256]{2,1,0:T(2,128)(2,1)S(1)}, u32[]{:S(2)}, u32[]{:S(2)}) async-start(bf16[64,2,256]{2,1,0:T(2,128)(2,1)} %reshape.402), calls=%async_computation.1 | async-start | bytes 131072 | tf_op jit(solution)/shard_map/all_to_all | solution.py:65
  67.7 0.7 copy-start.8
  83.2 19.1 %all-to-all-start.2 = ((bf16[64,2,256]{2,1,0:T(2,128)(2,1)}), bf16[64,2,256]{2,1,0:T(2,128)(2,1)S(1)}, u32[]{:S(2)}, u32[]{:S(2)}) async-start(bf16[64,2,256]{2,1,0:T(2,128)(2,1)} %reshape.404), calls=%async_computation.2 | async-start | bytes 131072 | tf_op jit(solution)/shard_map/all_to_all | solution.py:67
  88.2 0.7 copy-start.11
  103.8 1.0 copy-start.5
  104.1 14.7 %copy-start.1 = (bf16[1,2048,176]{1,2,0:T(8,128)(2,1)S(1)}, bf16[1,2048,176]{1,2,0:T(8,128)(2,1)}, u32[]{:S(2)}) copy-start(bf16[1,2048,176]{1,2,0:T(8,128)(2,1)} %param.29) | copy-start | bytes 2162692
  105.4 13.7 %copy-start.3 = (bf16[1,2048,176]{1,2,0:T(8,128)(2,1)S(1)}, bf16[1,2048,176]{1,2,0:T(8,128)(2,1)}, u32[]{:S(2)}) copy-start(bf16[1,2048,176]{1,2,0:T(8,128)(2,1)} %param.30) | copy-start | bytes 2162692
  118.8 1.1 copy-start.2
  131.4 21.8 %all-to-all-start.5 = ((bf16[64,2,256]{2,1,0:T(2,128)(2,1)}), bf16[64,2,256]{2,1,0:T(2,128)(2,1)S(1)}, u32[]{:S(2)}, u32[]{:S(2)}) async-start(bf16[64,2,256]{2,1,0:T(2,128)(2,1)} %reshape.406), calls=%async_computation.5 | async-start | bytes 131072 | tf_op jit(solution)/shard_map/all_to_all | solution.py:231

commit v10 on v9

--- a/solution.py
+++ b/solution.py
@@ -156,11 +156,18 @@
         send = lax.dynamic_index_in_dim(packed, 1 - side, axis_pos, keepdims=False)
         packed = merge_packed(keep, exchange(send, "blk", 1 << bit), latent_dim)
     packed = packed.reshape(new_steps, head_count, latent_dim + 2).transpose(1, 0, 2)
-    flat = packed.reshape(head_count, new_steps * (latent_dim + 2))
+    top = blk_bits - 1
+    half = head_count // 2
+    packed = packed.reshape(2, half, new_steps, latent_dim + 2)
+    side = (me >> top) & 1
+    keep = lax.dynamic_index_in_dim(packed, side, 0, keepdims=False)
+    send = lax.dynamic_index_in_dim(packed, 1 - side, 0, keepdims=False)
+    packed = merge_packed(keep, exchange(send, "blk", 1 << top), latent_dim)
+    flat = packed.reshape(half, new_steps * (latent_dim + 2))
     quad = 1 << low_bits
-    owners = [[slot + quad * h for h in range(head_count)] for slot in range(quad)]
+    owners = [[slot + quad * (upper * half + h) for h in range(half)] for upper in range(2) for slot in range(quad)]
     got = lax.all_to_all(flat, "blk", 0, 0, tiled=True, axis_index_groups=owners)
-    got = got.reshape(head_count, new_steps, latent_dim + 2)
+    got = got.reshape(half, new_steps, latent_dim + 2)
     peaks = got[..., latent_dim]
     totals = got[..., latent_dim + 1]
     peak_all = jnp.max(peaks, axis=0)

time: 175 us -> 178 us (1.017)
  waiting for transfers between devices: 60.7 us -> 64.1 us
    ppermute x4 -> x5, waiting for transfers between devices: 7.92 us -> 11.1 us  [exchange(): lax.ppermute(part, axis, xor_pairs(count, mask))]
    ppermute x4 -> x5, starting transfers between devices: 18.9 us -> 21.1 us  [exchange(): lax.ppermute(part, axis, xor_pairs(count, mask))]
  transfers between devices with their start and end apart: 8 -> 9, of which waited for: 8 -> 9; matrix products, arithmetic and copies ran while one was open for 2% -> 2% of each run, Pallas kernels for 0% -> 0%
where the time goes in v10:
time: 178 us; the launch traced here: 177 us
  waiting for transfers between devices  64.1 us (36%)
  starting transfers between devices  48.1 us (27%)
  blocking collectives  41.1 us (23%)
  local copies, waits for them, and re-layouts  14.3 us (8%)
  matrix products  5.03 us (3%)
  other arithmetic  3.59 us (2%)
    all_to_all x2, blocking collectives, a2a_gather(): return lax.all_to_all(spread, axis, 0, 0, tiled=True)  31.8 us
    ppermute x5, starting transfers between devices, exchange(): lax.ppermute(part, axis, xor_pairs(count, mask))  21.1 us
    all_to_all x1, waiting for transfers between devices, local(): lax.all_to_all(parts, 'blk', 0, 0, tiled=True).astype(jnp.float32)  14.7 us
    all_to_all x1, waiting for transfers between devices, a2a_sum(): lax.all_to_all(parts, axis, 0, 0, tiled=True).astype(jnp.float32)  13.5 us
    all_to_all x1, waiting for transfers between devices, a2a_sum(): back = lax.all_to_all(spread, axis, 0, 0, tiled=True).astype(jnp.float32)  13.3 us
    all_to_all x1, waiting for transfers between devices, local(): lax.all_to_all(flat, 'blk', 0, 0, tiled=True, axis_index_groups=owners)  11.5 us
    ppermute x5, waiting for transfers between devices, exchange(): lax.ppermute(part, axis, xor_pairs(count, mask))  11.1 us
    all_to_all x1, starting transfers between devices, local(): lax.all_to_all(flat, 'blk', 0, 0, tiled=True, axis_index_groups=owners)  9.47 us
  transfers between devices with their start and end apart: 9, of which 9 were waited for; matrix products, arithmetic and copies ran while one was open for 2% of the time, Pallas kernels for 0%

profile of v10, /device:TPU:1, one launch (start us, length us, event | category | flops | bytes accessed | tf_op | source)
XLA Modules:
  0.0 176.7 jit_solution(3407637060307846132)
XLA Ops:
  0.0 0.7 copy-done.12
  0.8 0.4 copy-done
  1.2 1.4 fusion.75
  2.7 0.3 fusion.73
  2.9 0.4 fusion.21
  3.3 0.2 fusion.19
  3.9 8.7 %collective-permute-start = (f32[2,64,514]{2,1,0:T(8,128)S(1)}, f32[2,64,514]{2,1,0:T(8,128)S(1)}, u32[]{:S(2)}, u32[]{:S(2)}) collective-permute-start(f32[2,64,514]{2,1,0:T(8,128)S(1)} %get-tuple-element.22), channel_id=1, source_target_pairs={{0,8},{8,0},{16,24},{24,16},{32,40},{40,32},{48,56},{56,48},{64,72... | collective-permute-start | bytes 789512 | tf_op jit(solution)/shard_map/ppermute | solution.py:22
  12.7 0.8 constant_dynamic-slice_fusion.2
  13.5 0.4 collective-permute-done
  14.4 1.9 %collective-permute-start.1 = (f32[64,514]{1,0:T(8,128)S(1)}, f32[64,514]{1,0:T(8,128)S(1)}, u32[]{:S(2)}, u32[]{:S(2)}) collective-permute-start(f32[64,514]{1,0:T(8,128)S(1)} %get-tuple-element.24), channel_id=1, source_target_pairs={{0,16},{8,24},{16,0},{24,8},{32,48},{40,56},{48,32},{56,40},{64,80... | collective-permute-start | bytes 394760 | tf_op jit(solution)/shard_map/ppermute | solution.py:22
  16.5 5.2 %collective-permute-done.1 = f32[64,514]{1,0:T(8,128)S(1)} collective-permute-done((f32[64,514]{1,0:T(8,128)S(1)}, f32[64,514]{1,0:T(8,128)S(1)}, u32[]{:S(2)}, u32[]{:S(2)}) %collective-permute-start.1) | collective-permute-done | bytes 131616 | tf_op jit(solution)/shard_map/ppermute | solution.py:22
  22.1 1.9 %collective-permute-start.2 = (f32[8,4,514]{2,0,1:T(8,128)S(1)}, f32[8,4,514]{2,0,1:T(8,128)S(1)}, u32[]{:S(2)}, u32[]{:S(2)}) collective-permute-start(f32[8,4,514]{2,0,1:T(8,128)S(1)} %get-tuple-element.26), channel_id=1, source_target_pairs={{0,256},{8,264},{16,272},{24,280},{32,288},{40,296},{48,304},{56,3... | collective-permute-start | bytes 197384 | tf_op jit(solution)/shard_map/ppermute | solution.py:22
  24.0 3.2 %collective-permute-done.2 = f32[8,4,514]{2,0,1:T(8,128)S(1)} collective-permute-done((f32[8,4,514]{2,0,1:T(8,128)S(1)}, f32[8,4,514]{2,0,1:T(8,128)S(1)}, u32[]{:S(2)}, u32[]{:S(2)}) %collective-permute-start.2) | collective-permute-done | bytes 65824 | tf_op jit(solution)/shard_map/ppermute | solution.py:22
  27.6 0.8 all_to_all.32
  28.4 9.5 %all-to-all-start = ((f32[8,1,2056]{2,1,0:T(1,128)}), f32[8,1,2056]{2,1,0:T(1,128)S(1)}, u32[]{:S(2)}, u32[]{:S(2)}) async-start(f32[8,1,2056]{2,1,0:T(1,128)} %all_to_all.32), calls=%async_computation | async-start | bytes 139264 | tf_op jit(solution)/shard_map/all_to_all | solution.py:169
  37.9 0.8 fusion.74
  38.7 11.5 %all-to-all-done = f32[8,1,2056]{2,1,0:T(1,128)S(1)} async-done(((f32[8,1,2056]{2,1,0:T(1,128)}), f32[8,1,2056]{2,1,0:T(1,128)S(1)}, u32[]{:S(2)}, u32[]{:S(2)}) %all-to-all-start) | async-done | bytes 65824 | tf_op jit(solution)/shard_map/all_to_all | solution.py:169
  50.9 0.2 fusion.54
  51.3 0.2 fusion.11
  51.5 5.5 %collective-permute-start.3 = (bf16[1,4,512]{2,1,0:T(4,128)(2,1)S(1)}, bf16[1,4,512]{2,1,0:T(4,128)(2,1)S(1)}, u32[]{:S(2)}, u32[]{:S(2)}) collective-permute-start(bf16[1,4,512]{2,1,0:T(4,128)(2,1)S(1)} %fusion.11), channel_id=1, source_target_pairs={{0,8},{8,0},{16,24},{24,16},{32,40},{40,32},{48,56},{56,48},{64,72... | collective-permute-start | bytes 12296 | tf_op jit(solution)/shard_map/ppermute | solution.py:22
  57.0 0.8 collective-permute-done.3
  57.8 3.0 %collective-permute-start.4 = (bf16[2,4,512]{2,1,0:T(4,128)(2,1)S(1)}, bf16[2,4,512]{2,1,0:T(4,128)(2,1)S(1)}, u32[]{:S(2)}, u32[]{:S(2)}) collective-permute-start(bf16[2,4,512]{2,1,0:T(4,128)(2,1)S(1)} %pad_maximum_fusion.4), channel_id=1, source_target_pairs={{0,16},{8,24},{16,0},{24,8},{32,48},{40,56},{48,32},{56,40},{64,80... | collective-permute-start | bytes 24584 | tf_op jit(solution)/shard_map/ppermute | solution.py:22
  60.9 1.4 collective-permute-done.4
  62.3 0.7 copy-done.10
  63.0 0.3 convolution_convert_fusion.1
  63.3 0.2 convert_element_type.133
  63.5 0.2 copy.153
  63.7 0.8 reshape.408
  64.5 5.8 %all-to-all-start.1 = ((bf16[64,2,256]{2,1,0:T(2,128)(2,1)}), bf16[64,2,256]{2,1,0:T(2,128)(2,1)S(1)}, u32[]{:S(2)}, u32[]{:S(2)}) async-start(bf16[64,2,256]{2,1,0:T(2,128)(2,1)} %reshape.408), calls=%async_computation.1 | async-start | bytes 131072 | tf_op jit(solution)/shard_map/all_to_all | solution.py:65
  70.5 0.2 copy.159
  70.7 0.5 copy-done.8
  71.4 13.5 %all-to-all-done.1 = bf16[64,2,256]{2,1,0:T(2,128)(2,1)S(1)} async-done(((bf16[64,2,256]{2,1,0:T(2,128)(2,1)}), bf16[64,2,256]{2,1,0:T(2,128)(2,1)S(1)}, u32[]{:S(2)}, u32[]{:S(2)}) %all-to-all-start.1) | async-done | bytes 65568 | tf_op jit(solution)/shard_map/all_to_all | solution.py:65
  84.9 0.2 reshape.409
  85.2 0.8 reshape.410
  86.1 4.4 %all-to-all-start.2 = ((bf16[64,2,256]{2,1,0:T(2,128)(2,1)}), bf16[64,2,256]{2,1,0:T(2,128)(2,1)S(1)}, u32[]{:S(2)}, u32[]{:S(2)}) async-start(bf16[64,2,256]{2,1,0:T(2,128)(2,1)} %reshape.410), calls=%async_computation.2 | async-start | bytes 131072 | tf_op jit(solution)/shard_map/all_to_all | solution.py:67
  90.6 0.3 reduce_window_sum.11
  91.1 0.6 copy-done.11
  91.9 13.3 %all-to-all-done.2 = bf16[64,2,256]{2,1,0:T(2,128)(2,1)S(1)} async-done(((bf16[64,2,256]{2,1,0:T(2,128)(2,1)}), bf16[64,2,256]{2,1,0:T(2,128)(2,1)S(1)}, u32[]{:S(2)}, u32[]{:S(2)}) %all-to-all-start.2) | async-done | bytes 65568 | tf_op jit(solution)/shard_map/all_to_all | solution.py:67
  105.2 0.2 reshape.411
  105.4 0.3 copy.154
  105.7 0.2 copy.155
  105.9 0.2 reshape.384
  106.2 0.2 multiply_reduce_fusion
  106.5 0.2 copy.161
  106.7 0.3 convert_element_type.144
  107.0 0.6 copy-done.5
  107.6 0.2 fusion.9
  107.8 0.2 select_reduce_fusion
  108.3 13.5 %all_to_all.40 = bf16[8,1,3,2048]{3,2,1,0:T(4,128)(2,1)S(1)} all-to-all(bf16[8,1,3,2048]{3,2,1,0:T(4,128)(2,1)S(1)} %broadcast_in_dim.38), channel_id=1, replica_groups=mesh['blk'=64,'exp'=8] {'exp'}, dimensions={0} | all-to-all | bytes 196608 | tf_op jit(solution)/shard_map/all_to_all | solution.py:74
  121.9 0.3 fusion.16
  122.2 0.3 fusion.4
  122.5 0.4 copy-done.2
  123.0 0.2 fusion
  123.3 9.3 %all_to_all.41 = bf16[8,1,3,2048]{3,2,1,0:T(4,128)(2,1)S(1)} all-to-all(bf16[8,1,3,2048]{3,2,1,0:T(4,128)(2,1)S(1)} %copy.163), channel_id=1, replica_groups=mesh['blk'=64,'exp'=8] {'exp'}, dimensions={0} | all-to-all | bytes 196608 | tf_op jit(solution)/shard_map/all_to_all | solution.py:78
  132.9 0.5 fusion.3
  133.4 0.3 copy.165
  133.6 0.8 reshape.412
  134.5 7.2 %all-to-all-start.5 = ((bf16[64,2,256]{2,1,0:T(2,128)(2,1)}), bf16[64,2,256]{2,1,0:T(2,128)(2,1)S(1)}, u32[]{:S(2)}, u32[]{:S(2)}) async-start(bf16[64,2,256]{2,1,0:T(2,128)(2,1)} %reshape.412), calls=%async_computation.5 | async-start | bytes 131072 | tf_op jit(solution)/shard_map/all_to_all | solution.py:238
  141.6 14.7 %all-to-all-done.5 = bf16[64,2,256]{2,1,0:T(2,128)(2,1)S(1)} async-done(((bf16[64,2,256]{2,1,0:T(2,128)(2,1)}), bf16[64,2,256]{2,1,0:T(2,128)(2,1)S(1)}, u32[]{:S(2)}, u32[]{:S(2)}) %all-to-all-start.5) | async-done | bytes 65568 | tf_op jit(solution)/shard_map/all_to_all | solution.py:238
  156.3 0.2 reshape.413
  156.5 0.3 copy.166
  157.2 18.3 %all_to_all.42 = bf16[64,2,256]{2,1,0:T(2,128)(2,1)S(1)} all-to-all(bf16[64,2,256]{2,1,0:T(2,128)(2,1)S(1)} %reshape.414), channel_id=1, replica_groups=mesh['blk'=64,'exp'=8] {'blk'}, dimensions={0} | all-to-all | bytes 131072 | tf_op jit(solution)/shard_map/all_to_all | solution.py:74
  175.5 0.2 reshape.415
  175.8 0.9 reshape_reshape.3
  (92 shorter events, 5.0 us)
Async XLA Ops:
  0.0 1.2 copy-start
  0.0 0.7 copy-start.12
  1.2 1.4 copy-start.7
  1.2 1.4 copy-start.9
  3.9 10.0 %collective-permute-start = (f32[2,64,514]{2,1,0:T(8,128)S(1)}, f32[2,64,514]{2,1,0:T(8,128)S(1)}, u32[]{:S(2)}, u32[]{:S(2)}) collective-permute-start(f32[2,64,514]{2,1,0:T(8,128)S(1)} %get-tuple-element.22), channel_id=1, source_target_pairs={{0,8},{8,0},{16,24},{24,16},{32,40},{40,32},{48,56},{56,48},{64,72... | collective-permute-start | bytes 789512 | tf_op jit(solution)/shard_map/ppermute | solution.py:22
  14.3 2.0 %copy-start.13 = (bf16[4,4,512]{2,1,0:T(4,128)(2,1)S(1)}, bf16[4,4,512]{2,1,0:T(4,128)(2,1)}, u32[]{:S(2)}) copy-start(bf16[4,4,512]{2,1,0:T(4,128)(2,1)} %param.19) | copy-start | bytes 49156
  14.4 7.3 %collective-permute-start.1 = (f32[64,514]{1,0:T(8,128)S(1)}, f32[64,514]{1,0:T(8,128)S(1)}, u32[]{:S(2)}, u32[]{:S(2)}) collective-permute-start(f32[64,514]{1,0:T(8,128)S(1)} %get-tuple-element.24), channel_id=1, source_target_pairs={{0,16},{8,24},{16,0},{24,8},{32,48},{40,56},{48,32},{56,40},{64,80... | collective-permute-start | bytes 394760 | tf_op jit(solution)/shard_map/ppermute | solution.py:22
  22.1 5.2 %collective-permute-start.2 = (f32[8,4,514]{2,0,1:T(8,128)S(1)}, f32[8,4,514]{2,0,1:T(8,128)S(1)}, u32[]{:S(2)}, u32[]{:S(2)}) collective-permute-start(f32[8,4,514]{2,0,1:T(8,128)S(1)} %get-tuple-element.26), channel_id=1, source_target_pairs={{0,256},{8,264},{16,272},{24,280},{32,288},{40,296},{48,304},{56,3... | collective-permute-start | bytes 197384 | tf_op jit(solution)/shard_map/ppermute | solution.py:22
  28.4 21.8 %all-to-all-start = ((f32[8,1,2056]{2,1,0:T(1,128)}), f32[8,1,2056]{2,1,0:T(1,128)S(1)}, u32[]{:S(2)}, u32[]{:S(2)}) async-start(f32[8,1,2056]{2,1,0:T(1,128)} %all_to_all.32), calls=%async_computation | async-start | bytes 139264 | tf_op jit(solution)/shard_map/all_to_all | solution.py:169
  51.3 11.0 %copy-start.6 = (bf16[32,2048]{1,0:T(8,128)(2,1)S(1)}, bf16[32,2048]{1,0:T(8,128)(2,1)}, u32[]{:S(2)}) copy-start(bf16[32,2048]{1,0:T(8,128)(2,1)} %param.25) | copy-start | bytes 393220
  51.5 6.3 %collective-permute-start.3 = (bf16[1,4,512]{2,1,0:T(4,128)(2,1)S(1)}, bf16[1,4,512]{2,1,0:T(4,128)(2,1)S(1)}, u32[]{:S(2)}, u32[]{:S(2)}) collective-permute-start(bf16[1,4,512]{2,1,0:T(4,128)(2,1)S(1)} %fusion.11), channel_id=1, source_target_pairs={{0,8},{8,0},{16,24},{24,16},{32,40},{40,32},{48,56},{56,48},{64,72... | collective-permute-start | bytes 12296 | tf_op jit(solution)/shard_map/ppermute | solution.py:22
  57.8 4.4 %collective-permute-start.4 = (bf16[2,4,512]{2,1,0:T(4,128)(2,1)S(1)}, bf16[2,4,512]{2,1,0:T(4,128)(2,1)S(1)}, u32[]{:S(2)}, u32[]{:S(2)}) collective-permute-start(bf16[2,4,512]{2,1,0:T(4,128)(2,1)S(1)} %pad_maximum_fusion.4), channel_id=1, source_target_pairs={{0,16},{8,24},{16,0},{24,8},{32,48},{40,56},{48,32},{56,40},{64,80... | collective-permute-start | bytes 24584 | tf_op jit(solution)/shard_map/ppermute | solution.py:22
  62.3 0.8 copy-start.10
  64.5 5.9 %copy-start.4 = (bf16[4,4,2048]{2,1,0:T(4,128)(2,1)S(1)}, bf16[4,4,2048]{2,1,0:T(4,128)(2,1)}, u32[]{:S(2)}) copy-start(bf16[4,4,2048]{2,1,0:T(4,128)(2,1)} %param.16) | copy-start | bytes 196612
  64.5 20.4 %all-to-all-start.1 = ((bf16[64,2,256]{2,1,0:T(2,128)(2,1)}), bf16[64,2,256]{2,1,0:T(2,128)(2,1)S(1)}, u32[]{:S(2)}, u32[]{:S(2)}) async-start(bf16[64,2,256]{2,1,0:T(2,128)(2,1)} %reshape.408), calls=%async_computation.1 | async-start | bytes 131072 | tf_op jit(solution)/shard_map/all_to_all | solution.py:65
  70.5 0.7 copy-start.8
  86.1 19.1 %all-to-all-start.2 = ((bf16[64,2,256]{2,1,0:T(2,128)(2,1)}), bf16[64,2,256]{2,1,0:T(2,128)(2,1)S(1)}, u32[]{:S(2)}, u32[]{:S(2)}) async-start(bf16[64,2,256]{2,1,0:T(2,128)(2,1)} %reshape.410), calls=%async_computation.2 | async-start | bytes 131072 | tf_op jit(solution)/shard_map/all_to_all | solution.py:67
  91.0 0.7 copy-start.11
  106.7 1.0 copy-start.5
  107.0 14.9 %copy-start.1 = (bf16[1,2048,176]{1,2,0:T(8,128)(2,1)S(1)}, bf16[1,2048,176]{1,2,0:T(8,128)(2,1)}, u32[]{:S(2)}) copy-start(bf16[1,2048,176]{1,2,0:T(8,128)(2,1)} %param.29) | copy-start | bytes 2162692
  108.3 13.9 %copy-start.3 = (bf16[1,2048,176]{1,2,0:T(8,128)(2,1)S(1)}, bf16[1,2048,176]{1,2,0:T(8,128)(2,1)}, u32[]{:S(2)}) copy-start(bf16[1,2048,176]{1,2,0:T(8,128)(2,1)} %param.30) | copy-start | bytes 2162692
  121.9 1.1 copy-start.2
  134.5 21.8 %all-to-all-start.5 = ((bf16[64,2,256]{2,1,0:T(2,128)(2,1)}), bf16[64,2,256]{2,1,0:T(2,128)(2,1)S(1)}, u32[]{:S(2)}, u32[]{:S(2)}) async-start(bf16[64,2,256]{2,1,0:T(2,128)(2,1)} %reshape.412), calls=%async_computation.5 | async-start | bytes 131072 | tf_op jit(solution)/shard_map/all_to_all | solution.py:238
